TPU v7x, 256 devices: a whole 4x4x8 slice. The times are simulated.
256 devices in a mesh: tm: 32 (over x, y, core), row: 8 (over z).
Axes of the slice: x: 4, y: 4, z: 8, core: 2. Of those that a mesh axis runs over, the one named last changes fastest.
Arguments:
- right_side: float32 [32, 512, 1024], P('tm', 'row'), may hold values from -6 to 6
- kappa: float32 [512, 1024], P('row'), may hold values from 0.5 to 8
Outputs:
- solution: float32 [32, 512, 1024], P('tm', 'row')
All inputs are finite; a program needn't handle non-finite values.
Results may differ from a plain program's by a relative error of at most 0.0003.
Values sent between devices are 32-bit elements; how exact they have to be, the bound alone decides.
No kernel may reach another device: no remote copies, remote signals or barrier semaphores. Data moves between devices by JAX's collectives and lax.ppermute only.
A program may use at most 64 MiB of HBM per device.

v0:
```python
import math

import jax
import jax.numpy as jnp
from jax import lax
from jax.sharding import PartitionSpec as P

SWEEPS = 2
DEGREE = 4


circulant_alpha = 0.05
courant_rows = 0.5
courant_cols = 0.25
cheb_centre = 1.0
cheb_half = 0.7


def from_partner(value, axis, bit):
    mask = 2**bit
    pairs = [(source, source ^ mask) for source in range(lax.axis_size(axis))]
    return lax.ppermute(value, axis, pairs)


def padded_2(block, sides, width):
    for axis, dim in sides:
        count = lax.axis_size(axis)
        forward = [(i, i + 1) for i in range(count - 1)]
        backward = [(target, source) for source, target in forward]
        low = lax.ppermute(
            lax.slice_in_dim(block, block.shape[dim] - width, None, axis=dim), axis, forward
        )
        high = lax.ppermute(lax.slice_in_dim(block, 0, width, axis=dim), axis, backward)
        block = jnp.concatenate([low, block, high], axis=dim)
    return block


def step_weights(count):
    return [
        1.0 / (cheb_centre + cheb_half * math.cos(math.pi * (2 * number + 1) / (2 * count)))
        for number in range(count)
    ]


def face_terms(kappa_rows):
    padded = jnp.pad(kappa_rows, ((0, 0), (1, 1)))
    centre = padded[1:-1, 1:-1]
    north = 0.5 * (centre + padded[2:, 1:-1])
    south = 0.5 * (centre + padded[:-2, 1:-1])
    east = 0.5 * (centre + padded[1:-1, 2:])
    west = 0.5 * (centre + padded[1:-1, :-2])
    diagonal = north + south + east + west + (courant_rows + courant_cols)
    return (north, south, east, west, diagonal)


def spatial(extended, faces):
    north, south, east, west, diagonal = faces
    padded = jnp.pad(extended, ((0, 0), (0, 0), (0, 0), (1, 1)))
    centre = padded[:, :, 1:-1, 1:-1]
    above = padded[:, :, 2:, 1:-1]
    below = padded[:, :, :-2, 1:-1]
    after = padded[:, :, 1:-1, 2:]
    before = padded[:, :, 1:-1, :-2]
    coupled = north * above + south * below + east * after + west * before
    return diagonal * centre - coupled - courant_rows * below - courant_cols * before


def rotate(pair, cosine, sine):
    return jnp.stack([pair[0] * cosine - pair[1] * sine, pair[0] * sine + pair[1] * cosine])


def short_transform(pair, sign):
    count = pair.shape[1]
    index = jnp.arange(count, dtype=jnp.int32)
    angles = 2.0 * math.pi / count * (index[:, None] * index[None, :] % count).astype(jnp.float32)
    cosine = jnp.cos(angles)
    sine = sign * jnp.sin(angles)
    highest = lax.Precision.HIGHEST
    real = jnp.einsum("kj,jrc->krc", cosine, pair[0], precision=highest) - jnp.einsum(
        "kj,jrc->krc", sine, pair[1], precision=highest
    )
    imag = jnp.einsum("kj,jrc->krc", cosine, pair[1], precision=highest) + jnp.einsum(
        "kj,jrc->krc", sine, pair[0], precision=highest
    )
    return jnp.stack([real, imag])


def bit_reversed(device, levels):
    total = jnp.zeros((), jnp.int32)
    for place in range(levels):
        total = total + device // 2**place % 2 * 2 ** (levels - 1 - place)
    return total


def forward_pairs(scaled, device, levels, tm_size, total_steps):
    place = levels - 1
    half = 2**place
    lower = device // half % 2 == 1
    angle = -math.pi / half * (device % half).astype(jnp.float32)
    partner = from_partner(scaled, "tm", place)
    summed = scaled + partner
    differ = partner - scaled
    real = jnp.where(lower, differ * jnp.cos(angle), summed)
    imag = jnp.where(lower, differ * jnp.sin(angle), jnp.zeros_like(summed))
    state = jnp.stack([real, imag])
    for place in range(levels - 2, -1, -1):
        half = 2**place
        lower = device // half % 2 == 1
        angle = -math.pi / half * (device % half).astype(jnp.float32)
        partner = from_partner(state, "tm", place)
        summed = state + partner
        rotated = rotate(partner - state, jnp.cos(angle), jnp.sin(angle))
        state = jnp.where(lower, rotated, summed)
    first_index = bit_reversed(device, levels)
    steps_dev = scaled.shape[0]
    local_steps = jnp.arange(steps_dev, dtype=jnp.int32)
    twist = (
        -2.0 * math.pi / total_steps * (local_steps * first_index % total_steps).astype(jnp.float32)
    )
    state = rotate(state, jnp.cos(twist)[:, None, None], jnp.sin(twist)[:, None, None])
    spectrum = short_transform(state, -1.0)
    frequencies = first_index + tm_size * local_steps
    return (spectrum, frequencies)


def backward_pairs(solved, device, levels, total_steps):
    steps_dev = solved.shape[1]
    first_index = bit_reversed(device, levels)
    state = short_transform(solved, 1.0) * (1.0 / steps_dev)
    local_steps = jnp.arange(steps_dev, dtype=jnp.int32)
    twist = (
        2.0 * math.pi / total_steps * (local_steps * first_index % total_steps).astype(jnp.float32)
    )
    state = rotate(state, jnp.cos(twist)[:, None, None], jnp.sin(twist)[:, None, None])
    for place in range(0, levels - 1):
        half = 2**place
        lower = device // half % 2 == 1
        angle = math.pi / half * (device % half).astype(jnp.float32)
        cosine = jnp.cos(angle)
        sine = jnp.sin(angle)
        partner = from_partner(state, "tm", place)
        upper_value = (state + rotate(partner, cosine, sine)) * 0.5
        lower_value = (partner - rotate(state, cosine, sine)) * 0.5
        state = jnp.where(lower, lower_value, upper_value)
    place = levels - 1
    half = 2**place
    lower = device // half % 2 == 1
    angle = math.pi / half * (device % half).astype(jnp.float32)
    own_turned = state[0] * jnp.cos(angle) - state[1] * jnp.sin(angle)
    outgoing = jnp.where(lower, own_turned, state[0])
    received = from_partner(outgoing, "tm", place)
    return jnp.where(lower, (received - own_turned) * 0.5, (state[0] + received) * 0.5)


def shift_terms(frequencies, faces, total_steps):
    decay = circulant_alpha ** (1.0 / total_steps)
    theta = 2.0 * math.pi / total_steps * frequencies.astype(jnp.float32)
    shift_real = (1.0 - decay * jnp.cos(theta))[:, None, None]
    shift_imag = (decay * jnp.sin(theta))[:, None, None]
    diag_real = shift_real + faces[4]
    magnitude = diag_real * diag_real + shift_imag * shift_imag
    return (shift_real, shift_imag, diag_real / magnitude, -shift_imag / magnitude)


def solve_each(spectrum, frequencies, kappa):
    total_steps = spectrum.shape[1] * lax.axis_size("tm")
    kappa_rows = padded_2(kappa, (("row", 0),), 1)
    faces = face_terms(kappa_rows)
    shift_real, shift_imag, inv_real, inv_imag = shift_terms(frequencies, faces, total_steps)
    state = jnp.zeros_like(spectrum)
    first = True
    for sweep in range(SWEEPS):
        for weight in step_weights(DEGREE):
            if first:
                residual = spectrum
                first = False
            else:
                extended = padded_2(state, (("row", 2),), 1)
                image = spatial(extended, faces)
                image_real = shift_real * state[0] - shift_imag * state[1] + image[0]
                image_imag = shift_real * state[1] + shift_imag * state[0] + image[1]
                residual = spectrum - jnp.stack([image_real, image_imag])
            corr_real = inv_real * residual[0] - inv_imag * residual[1]
            corr_imag = inv_real * residual[1] + inv_imag * residual[0]
            state = state + weight * jnp.stack([corr_real, corr_imag])
    return state


def solve_block(spectrum, frequencies, kappa):
    return solve_each(spectrum, frequencies, kappa)


def body(right_side, kappa):
    steps_dev = right_side.shape[0]
    tm_size = lax.axis_size("tm")
    total_steps = steps_dev * tm_size
    device = lax.axis_index("tm")
    local_steps = jnp.arange(steps_dev, dtype=jnp.int32)
    global_steps = device * steps_dev + local_steps
    log_alpha = math.log(circulant_alpha)
    step_float = global_steps.astype(jnp.float32)
    scaled = right_side * jnp.exp(log_alpha * step_float / total_steps)[:, None, None]
    levels = tm_size.bit_length() - 1
    spectrum, frequencies = forward_pairs(scaled, device, levels, tm_size, total_steps)
    solved = solve_block(spectrum, frequencies, kappa)
    signal = backward_pairs(solved, device, levels, total_steps)
    return signal * jnp.exp(-log_alpha * step_float / total_steps)[:, None, None]


def solution(mesh):
    placed = (P("tm", "row", None), P("row", None))
    return jax.shard_map(
        body, mesh=mesh, in_specs=placed, out_specs=P("tm", "row", None), check_vma=False
    )
```

profile of v0, /device:TPU:134, one launch (start us, length us, event | category | flops | bytes accessed | tf_op | source)
XLA Modules:
  0.0 186.4 jit_solution(15976000156440027366)
XLA Ops:
  0.1 1.0 broadcast_multiply_fusion
  1.1 1.5 collective-permute-start.2
  2.8 8.0 %collective-permute-done.2 = f32[1,64,1024]{2,1,0:T(8,128)S(1)} collective-permute-done((f32[1,64,1024]{2,1,0:T(8,128)S(1)}, f32[1,64,1024]{2,1,0:T(8,128)S(1)}, u32[]{:S(2)}, u32[]{:S(2)}) %collective-permute-start.2) | collective-permute-done | bytes 262176 | tf_op jit(solution)/shard_map/ppermute | solution.py:22
  10.9 0.9 collective-permute-start.3
  12.0 11.8 %collective-permute-done.3 = f32[2,1,64,1024]{3,2,1,0:T(8,128)S(1)} collective-permute-done((f32[2,1,64,1024]{3,2,1,0:T(8,128)S(1)}, f32[2,1,64,1024]{3,2,1,0:T(8,128)S(1)}, u32[]{:S(2)}, u32[]{:S(2)}) %collective-permute-start.3) | collective-permute-done | bytes 524320 | tf_op jit(solution)/shard_map/ppermute | solution.py:22
  24.0 3.3 %collective-permute-start.4 = (f32[2,1,64,1024]{3,2,1,0:T(8,128)S(1)}, f32[2,1,64,1024]{3,2,1,0:T(8,128)S(1)}, u32[]{:S(2)}, u32[]{:S(2)}) collective-permute-start(f32[2,1,64,1024]{3,2,1,0:T(8,128)S(1)} %maximum_select_fusion), channel_id=1, source_target_pairs={{0,32},{8,40},{16,48},{24,56},{32,0},{40,8},{48,16},{56,24},{64,96... | collective-permute-start | bytes 1572872 | tf_op jit(solution)/shard_map/ppermute | solution.py:22
  27.5 10.0 %collective-permute-done.4 = f32[2,1,64,1024]{3,2,1,0:T(8,128)S(1)} collective-permute-done((f32[2,1,64,1024]{3,2,1,0:T(8,128)S(1)}, f32[2,1,64,1024]{3,2,1,0:T(8,128)S(1)}, u32[]{:S(2)}, u32[]{:S(2)}) %collective-permute-start.4) | collective-permute-done | bytes 524320 | tf_op jit(solution)/shard_map/ppermute | solution.py:22
  37.9 1.7 collective-permute-start.5
  39.8 9.2 %collective-permute-done.5 = f32[2,1,64,1024]{3,2,1,0:T(8,128)S(1)} collective-permute-done((f32[2,1,64,1024]{3,2,1,0:T(8,128)S(1)}, f32[2,1,64,1024]{3,2,1,0:T(8,128)S(1)}, u32[]{:S(2)}, u32[]{:S(2)}) %collective-permute-start.5) | collective-permute-done | bytes 524320 | tf_op jit(solution)/shard_map/ppermute | solution.py:22
  49.4 0.7 copy-done
  50.1 2.0 %collective-permute-start = (f32[1,1024]{1,0:T(1,128)S(1)}, f32[1,1024]{1,0:T(1,128)S(1)}, u32[]{:S(2)}, u32[]{:S(2)}) collective-permute-start(f32[1,1024]{1,0:T(1,128)S(1)} %get-tuple-element.89), channel_id=1, source_target_pairs={{1,0},{2,1},{3,2},{4,3},{5,4},{6,5},{7,6},{9,8},{10,9},{11,10},{12... | collective-permute-start | bytes 12296 | tf_op jit(solution)/shard_map/ppermute | solution.py:33
  52.2 3.8 %collective-permute-start.1 = (f32[1,1024]{1,0:T(1,128)S(1)}, f32[1,1024]{1,0:T(1,128)S(1)}, u32[]{:S(2)}, u32[]{:S(2)}) collective-permute-start(f32[1,1024]{1,0:T(1,128)S(1)} %get-tuple-element.88), channel_id=1, source_target_pairs={{0,1},{1,2},{2,3},{3,4},{4,5},{5,6},{6,7},{8,9},{9,10},{10,11},{11... | collective-permute-start | bytes 12296 | tf_op jit(solution)/shard_map/ppermute | solution.py:30
  56.2 2.7 %collective-permute-done.1 = f32[1,1024]{1,0:T(1,128)S(1)} collective-permute-done((f32[1,1024]{1,0:T(1,128)S(1)}, f32[1,1024]{1,0:T(1,128)S(1)}, u32[]{:S(2)}, u32[]{:S(2)}) %collective-permute-start.1) | collective-permute-done | bytes 4128 | tf_op jit(solution)/shard_map/ppermute | solution.py:30
  59.0 0.2 add_add_fusion
  59.9 1.9 %collective-permute-start.7 = (f32[2,1,1,1024]{3,2,1,0:T(1,128)S(1)}, f32[2,1,1,1024]{3,2,1,0:T(1,128)S(1)}, u32[]{:S(2)}, u32[]{:S(2)}) collective-permute-start(f32[2,1,1,1024]{3,2,1,0:T(1,128)S(1)} %get-tuple-element.77), channel_id=1, source_target_pairs={{1,0},{2,1},{3,2},{4,3},{5,4},{6,5},{7,6},{9,8},{10,9},{11,10},{12... | collective-permute-start | bytes 24584 | tf_op jit(solution)/shard_map/ppermute | solution.py:33
  61.9 3.9 %collective-permute-start.8 = (f32[2,1,1,1024]{3,2,1,0:T(1,128)S(1)}, f32[2,1,1,1024]{3,2,1,0:T(1,128)S(1)}, u32[]{:S(2)}, u32[]{:S(2)}) collective-permute-start(f32[2,1,1,1024]{3,2,1,0:T(1,128)S(1)} %get-tuple-element.76), channel_id=1, source_target_pairs={{0,1},{1,2},{2,3},{3,4},{4,5},{5,6},{6,7},{8,9},{9,10},{10,11},{11... | collective-permute-start | bytes 24584 | tf_op jit(solution)/shard_map/ppermute | solution.py:30
  65.8 2.8 %collective-permute-done.8 = f32[2,1,1,1024]{3,2,1,0:T(1,128)S(1)} collective-permute-done((f32[2,1,1,1024]{3,2,1,0:T(1,128)S(1)}, f32[2,1,1,1024]{3,2,1,0:T(1,128)S(1)}, u32[]{:S(2)}, u32[]{:S(2)}) %collective-permute-start.8) | collective-permute-done | bytes 8224 | tf_op jit(solution)/shard_map/ppermute | solution.py:30
  68.6 0.3 select_maximum_fusion.12
  68.9 0.4 fusion.47
  69.7 2.7 %collective-permute-start.10 = (f32[2,1,1,1024]{3,2,1,0:T(1,128)S(1)}, f32[2,1,1,1024]{3,2,1,0:T(1,128)S(1)}, u32[]{:S(2)}, u32[]{:S(2)}) collective-permute-start(f32[2,1,1,1024]{3,2,1,0:T(1,128)S(1)} %get-tuple-element.70), channel_id=1, source_target_pairs={{0,1},{1,2},{2,3},{3,4},{4,5},{5,6},{6,7},{8,9},{9,10},{10,11},{11... | collective-permute-start | bytes 24584 | tf_op jit(solution)/shard_map/ppermute | solution.py:30
  72.4 4.3 %collective-permute-start.9 = (f32[2,1,1,1024]{3,2,1,0:T(1,128)S(1)}, f32[2,1,1,1024]{3,2,1,0:T(1,128)S(1)}, u32[]{:S(2)}, u32[]{:S(2)}) collective-permute-start(f32[2,1,1,1024]{3,2,1,0:T(1,128)S(1)} %get-tuple-element.71), channel_id=1, source_target_pairs={{1,0},{2,1},{3,2},{4,3},{5,4},{6,5},{7,6},{9,8},{10,9},{11,10},{12... | collective-permute-start | bytes 24584 | tf_op jit(solution)/shard_map/ppermute | solution.py:33
  76.8 1.3 collective-permute-done.9
  78.1 0.3 select_maximum_fusion.10
  78.4 0.4 fusion.40
  79.3 5.4 %collective-permute-start.11 = (f32[2,1,1,1024]{3,2,1,0:T(1,128)S(1)}, f32[2,1,1,1024]{3,2,1,0:T(1,128)S(1)}, u32[]{:S(2)}, u32[]{:S(2)}) collective-permute-start(f32[2,1,1,1024]{3,2,1,0:T(1,128)S(1)} %get-tuple-element.69), channel_id=1, source_target_pairs={{1,0},{2,1},{3,2},{4,3},{5,4},{6,5},{7,6},{9,8},{10,9},{11,10},{12... | collective-permute-start | bytes 24584 | tf_op jit(solution)/shard_map/ppermute | solution.py:33
  84.7 1.9 %collective-permute-start.12 = (f32[2,1,1,1024]{3,2,1,0:T(1,128)S(1)}, f32[2,1,1,1024]{3,2,1,0:T(1,128)S(1)}, u32[]{:S(2)}, u32[]{:S(2)}) collective-permute-start(f32[2,1,1,1024]{3,2,1,0:T(1,128)S(1)} %get-tuple-element.68), channel_id=1, source_target_pairs={{0,1},{1,2},{2,3},{3,4},{4,5},{5,6},{6,7},{8,9},{9,10},{10,11},{11... | collective-permute-start | bytes 24584 | tf_op jit(solution)/shard_map/ppermute | solution.py:30
  86.6 4.8 %collective-permute-done.12 = f32[2,1,1,1024]{3,2,1,0:T(1,128)S(1)} collective-permute-done((f32[2,1,1,1024]{3,2,1,0:T(1,128)S(1)}, f32[2,1,1,1024]{3,2,1,0:T(1,128)S(1)}, u32[]{:S(2)}, u32[]{:S(2)}) %collective-permute-start.12) | collective-permute-done | bytes 8224 | tf_op jit(solution)/shard_map/ppermute | solution.py:30
  91.4 0.3 select_maximum_fusion.8
  91.7 0.4 fusion.33
  92.6 1.9 %collective-permute-start.13 = (f32[2,1,1,1024]{3,2,1,0:T(1,128)S(1)}, f32[2,1,1,1024]{3,2,1,0:T(1,128)S(1)}, u32[]{:S(2)}, u32[]{:S(2)}) collective-permute-start(f32[2,1,1,1024]{3,2,1,0:T(1,128)S(1)} %get-tuple-element.67), channel_id=1, source_target_pairs={{1,0},{2,1},{3,2},{4,3},{5,4},{6,5},{7,6},{9,8},{10,9},{11,10},{12... | collective-permute-start | bytes 24584 | tf_op jit(solution)/shard_map/ppermute | solution.py:33
  94.6 3.9 %collective-permute-start.14 = (f32[2,1,1,1024]{3,2,1,0:T(1,128)S(1)}, f32[2,1,1,1024]{3,2,1,0:T(1,128)S(1)}, u32[]{:S(2)}, u32[]{:S(2)}) collective-permute-start(f32[2,1,1,1024]{3,2,1,0:T(1,128)S(1)} %get-tuple-element.66), channel_id=1, source_target_pairs={{0,1},{1,2},{2,3},{3,4},{4,5},{5,6},{6,7},{8,9},{9,10},{10,11},{11... | collective-permute-start | bytes 24584 | tf_op jit(solution)/shard_map/ppermute | solution.py:30
  98.5 2.8 %collective-permute-done.14 = f32[2,1,1,1024]{3,2,1,0:T(1,128)S(1)} collective-permute-done((f32[2,1,1,1024]{3,2,1,0:T(1,128)S(1)}, f32[2,1,1,1024]{3,2,1,0:T(1,128)S(1)}, u32[]{:S(2)}, u32[]{:S(2)}) %collective-permute-start.14) | collective-permute-done | bytes 8224 | tf_op jit(solution)/shard_map/ppermute | solution.py:30
  101.3 0.3 select_maximum_fusion.6
  101.6 0.4 fusion.26
  102.3 0.3 fusion.53
  102.6 1.9 %collective-permute-start.15 = (f32[2,1,1,1024]{3,2,1,0:T(1,128)S(1)}, f32[2,1,1,1024]{3,2,1,0:T(1,128)S(1)}, u32[]{:S(2)}, u32[]{:S(2)}) collective-permute-start(f32[2,1,1,1024]{3,2,1,0:T(1,128)S(1)} %get-tuple-element.65), channel_id=1, source_target_pairs={{1,0},{2,1},{3,2},{4,3},{5,4},{6,5},{7,6},{9,8},{10,9},{11,10},{12... | collective-permute-start | bytes 24584 | tf_op jit(solution)/shard_map/ppermute | solution.py:33
  104.5 3.9 %collective-permute-start.16 = (f32[2,1,1,1024]{3,2,1,0:T(1,128)S(1)}, f32[2,1,1,1024]{3,2,1,0:T(1,128)S(1)}, u32[]{:S(2)}, u32[]{:S(2)}) collective-permute-start(f32[2,1,1,1024]{3,2,1,0:T(1,128)S(1)} %get-tuple-element.64), channel_id=1, source_target_pairs={{0,1},{1,2},{2,3},{3,4},{4,5},{5,6},{6,7},{8,9},{9,10},{10,11},{11... | collective-permute-start | bytes 24584 | tf_op jit(solution)/shard_map/ppermute | solution.py:30
  108.4 2.8 %collective-permute-done.16 = f32[2,1,1,1024]{3,2,1,0:T(1,128)S(1)} collective-permute-done((f32[2,1,1,1024]{3,2,1,0:T(1,128)S(1)}, f32[2,1,1,1024]{3,2,1,0:T(1,128)S(1)}, u32[]{:S(2)}, u32[]{:S(2)}) %collective-permute-start.16) | collective-permute-done | bytes 8224 | tf_op jit(solution)/shard_map/ppermute | solution.py:30
  111.3 0.3 select_maximum_fusion.4
  111.5 0.4 fusion.19
  112.2 0.3 fusion.54
  112.6 2.1 %collective-permute-start.17 = (f32[2,1,1,1024]{3,2,1,0:T(1,128)S(1)}, f32[2,1,1,1024]{3,2,1,0:T(1,128)S(1)}, u32[]{:S(2)}, u32[]{:S(2)}) collective-permute-start(f32[2,1,1,1024]{3,2,1,0:T(1,128)S(1)} %get-tuple-element.63), channel_id=1, source_target_pairs={{1,0},{2,1},{3,2},{4,3},{5,4},{6,5},{7,6},{9,8},{10,9},{11,10},{12... | collective-permute-start | bytes 24584 | tf_op jit(solution)/shard_map/ppermute | solution.py:33
  114.7 3.9 %collective-permute-start.18 = (f32[2,1,1,1024]{3,2,1,0:T(1,128)S(1)}, f32[2,1,1,1024]{3,2,1,0:T(1,128)S(1)}, u32[]{:S(2)}, u32[]{:S(2)}) collective-permute-start(f32[2,1,1,1024]{3,2,1,0:T(1,128)S(1)} %get-tuple-element.62), channel_id=1, source_target_pairs={{0,1},{1,2},{2,3},{3,4},{4,5},{5,6},{6,7},{8,9},{9,10},{10,11},{11... | collective-permute-start | bytes 24584 | tf_op jit(solution)/shard_map/ppermute | solution.py:30
  118.6 2.8 %collective-permute-done.18 = f32[2,1,1,1024]{3,2,1,0:T(1,128)S(1)} collective-permute-done((f32[2,1,1,1024]{3,2,1,0:T(1,128)S(1)}, f32[2,1,1,1024]{3,2,1,0:T(1,128)S(1)}, u32[]{:S(2)}, u32[]{:S(2)}) %collective-permute-start.18) | collective-permute-done | bytes 8224 | tf_op jit(solution)/shard_map/ppermute | solution.py:30
  121.4 0.3 select_maximum_fusion.2
  121.7 0.4 fusion.12
  122.4 0.4 fusion.55
  122.8 1.9 %collective-permute-start.19 = (f32[2,1,1,1024]{3,2,1,0:T(1,128)S(1)}, f32[2,1,1,1024]{3,2,1,0:T(1,128)S(1)}, u32[]{:S(2)}, u32[]{:S(2)}) collective-permute-start(f32[2,1,1,1024]{3,2,1,0:T(1,128)S(1)} %get-tuple-element.61), channel_id=1, source_target_pairs={{1,0},{2,1},{3,2},{4,3},{5,4},{6,5},{7,6},{9,8},{10,9},{11,10},{12... | collective-permute-start | bytes 24584 | tf_op jit(solution)/shard_map/ppermute | solution.py:33
  124.7 3.9 %collective-permute-start.20 = (f32[2,1,1,1024]{3,2,1,0:T(1,128)S(1)}, f32[2,1,1,1024]{3,2,1,0:T(1,128)S(1)}, u32[]{:S(2)}, u32[]{:S(2)}) collective-permute-start(f32[2,1,1,1024]{3,2,1,0:T(1,128)S(1)} %get-tuple-element.60), channel_id=1, source_target_pairs={{0,1},{1,2},{2,3},{3,4},{4,5},{5,6},{6,7},{8,9},{9,10},{10,11},{11... | collective-permute-start | bytes 24584 | tf_op jit(solution)/shard_map/ppermute | solution.py:30
  128.7 2.8 %collective-permute-done.20 = f32[2,1,1,1024]{3,2,1,0:T(1,128)S(1)} collective-permute-done((f32[2,1,1,1024]{3,2,1,0:T(1,128)S(1)}, f32[2,1,1,1024]{3,2,1,0:T(1,128)S(1)}, u32[]{:S(2)}, u32[]{:S(2)}) %collective-permute-start.20) | collective-permute-done | bytes 8224 | tf_op jit(solution)/shard_map/ppermute | solution.py:30
  131.5 0.3 select_maximum_fusion
  131.8 0.4 fusion.5
  132.4 0.5 fusion.56
  133.2 1.9 %collective-permute-done.21 = f32[2,1,64,1024]{3,2,1,0:T(8,128)S(1)} collective-permute-done((f32[2,1,64,1024]{3,2,1,0:T(8,128)S(1)}, f32[2,1,64,1024]{3,2,1,0:T(8,128)S(1)}, u32[]{:S(2)}, u32[]{:S(2)}) %collective-permute-start.21) | collective-permute-done | bytes 524320 | tf_op jit(solution)/shard_map/ppermute | solution.py:22
  135.4 1.6 collective-permute-start.22
  137.2 12.2 %collective-permute-done.22 = f32[2,1,64,1024]{3,2,1,0:T(8,128)S(1)} collective-permute-done((f32[2,1,64,1024]{3,2,1,0:T(8,128)S(1)}, f32[2,1,64,1024]{3,2,1,0:T(8,128)S(1)}, u32[]{:S(2)}, u32[]{:S(2)}) %collective-permute-start.22) | collective-permute-done | bytes 524320 | tf_op jit(solution)/shard_map/ppermute | solution.py:22
  149.5 0.4 fusion.61
  149.9 3.2 %collective-permute-start.23 = (f32[2,1,64,1024]{3,2,1,0:T(8,128)S(1)}, f32[2,1,64,1024]{3,2,1,0:T(8,128)S(1)}, u32[]{:S(2)}, u32[]{:S(2)}) collective-permute-start(f32[2,1,64,1024]{3,2,1,0:T(8,128)S(1)} %fusion.61), channel_id=1, source_target_pairs={{0,32},{8,40},{16,48},{24,56},{32,0},{40,8},{48,16},{56,24},{64,96... | collective-permute-start | bytes 1572872 | tf_op jit(solution)/shard_map/ppermute | solution.py:22
  153.3 11.3 %collective-permute-done.23 = f32[2,1,64,1024]{3,2,1,0:T(8,128)S(1)} collective-permute-done((f32[2,1,64,1024]{3,2,1,0:T(8,128)S(1)}, f32[2,1,64,1024]{3,2,1,0:T(8,128)S(1)}, u32[]{:S(2)}, u32[]{:S(2)}) %collective-permute-start.23) | collective-permute-done | bytes 524320 | tf_op jit(solution)/shard_map/ppermute | solution.py:22
  164.9 0.9 collective-permute-start.24
  166.2 11.1 %collective-permute-done.24 = f32[2,1,64,1024]{3,2,1,0:T(8,128)S(1)} collective-permute-done((f32[2,1,64,1024]{3,2,1,0:T(8,128)S(1)}, f32[2,1,64,1024]{3,2,1,0:T(8,128)S(1)}, u32[]{:S(2)}, u32[]{:S(2)}) %collective-permute-start.24) | collective-permute-done | bytes 524320 | tf_op jit(solution)/shard_map/ppermute | solution.py:22
  177.7 1.3 collective-permute-start.25
  179.1 6.6 %collective-permute-done.25 = f32[1,64,1024]{2,1,0:T(8,128)S(1)} collective-permute-done((f32[1,64,1024]{2,1,0:T(8,128)S(1)}, f32[1,64,1024]{2,1,0:T(8,128)S(1)}, u32[]{:S(2)}, u32[]{:S(2)}) %collective-permute-start.25) | collective-permute-done | bytes 262176 | tf_op jit(solution)/shard_map/ppermute | solution.py:22
  185.6 0.8 select_multiply_fusion
  (77 shorter events, 5.4 us)
Async XLA Ops:
  0.0 10.7 %copy-start.1 = (f32[1,64,1024]{2,1,0:T(8,128)S(1)}, f32[1,64,1024]{2,1,0:T(8,128)}, u32[]{:S(2)}) copy-start(f32[1,64,1024]{2,1,0:T(8,128)} %param.2) | copy-start | bytes 786436
  1.1 9.6 %collective-permute-start.2 = (f32[1,64,1024]{2,1,0:T(8,128)S(1)}, f32[1,64,1024]{2,1,0:T(8,128)S(1)}, u32[]{:S(2)}, u32[]{:S(2)}) collective-permute-start(f32[1,64,1024]{2,1,0:T(8,128)S(1)} %broadcast_multiply_fusion), channel_id=1, source_target_pairs={{0,128},{8,136},{16,144},{24,152},{32,160},{40,168},{48,176},{56,1... | collective-permute-start | bytes 786440 | tf_op jit(solution)/shard_map/ppermute | solution.py:22
  10.9 12.9 %collective-permute-start.3 = (f32[2,1,64,1024]{3,2,1,0:T(8,128)S(1)}, f32[2,1,64,1024]{3,2,1,0:T(8,128)S(1)}, u32[]{:S(2)}, u32[]{:S(2)}) collective-permute-start(f32[2,1,64,1024]{3,2,1,0:T(8,128)S(1)} %pad_maximum_fusion.14), channel_id=1, source_target_pairs={{0,64},{8,72},{16,80},{24,88},{32,96},{40,104},{48,112},{56,120},{... | collective-permute-start | bytes 1572872 | tf_op jit(solution)/shard_map/ppermute | solution.py:22
  24.0 13.5 %collective-permute-start.4 = (f32[2,1,64,1024]{3,2,1,0:T(8,128)S(1)}, f32[2,1,64,1024]{3,2,1,0:T(8,128)S(1)}, u32[]{:S(2)}, u32[]{:S(2)}) collective-permute-start(f32[2,1,64,1024]{3,2,1,0:T(8,128)S(1)} %maximum_select_fusion), channel_id=1, source_target_pairs={{0,32},{8,40},{16,48},{24,56},{32,0},{40,8},{48,16},{56,24},{64,96... | collective-permute-start | bytes 1572872 | tf_op jit(solution)/shard_map/ppermute | solution.py:22
  37.9 11.1 %collective-permute-start.5 = (f32[2,1,64,1024]{3,2,1,0:T(8,128)S(1)}, f32[2,1,64,1024]{3,2,1,0:T(8,128)S(1)}, u32[]{:S(2)}, u32[]{:S(2)}) collective-permute-start(f32[2,1,64,1024]{3,2,1,0:T(8,128)S(1)} %maximum_select_fusion.1), channel_id=1, source_target_pairs={{0,16},{8,24},{16,0},{24,8},{32,48},{40,56},{48,32},{56,40},{64,80... | collective-permute-start | bytes 1572872 | tf_op jit(solution)/shard_map/ppermute | solution.py:22
  49.2 1.0 copy-start
  49.3 10.0 %collective-permute-start.6 = (f32[2,1,64,1024]{3,2,1,0:T(8,128)S(1)}, f32[2,1,64,1024]{3,2,1,0:T(8,128)S(1)}, u32[]{:S(2)}, u32[]{:S(2)}) collective-permute-start(f32[2,1,64,1024]{3,2,1,0:T(8,128)S(1)} %maximum_select_fusion.2), channel_id=1, source_target_pairs={{0,8},{8,0},{16,24},{24,16},{32,40},{40,32},{48,56},{56,48},{64,72... | collective-permute-start | bytes 1572872 | tf_op jit(solution)/shard_map/ppermute | solution.py:22
  50.1 6.0 %collective-permute-start = (f32[1,1024]{1,0:T(1,128)S(1)}, f32[1,1024]{1,0:T(1,128)S(1)}, u32[]{:S(2)}, u32[]{:S(2)}) collective-permute-start(f32[1,1024]{1,0:T(1,128)S(1)} %get-tuple-element.89), channel_id=1, source_target_pairs={{1,0},{2,1},{3,2},{4,3},{5,4},{6,5},{7,6},{9,8},{10,9},{11,10},{12... | collective-permute-start | bytes 12296 | tf_op jit(solution)/shard_map/ppermute | solution.py:33
  52.2 6.7 %collective-permute-start.1 = (f32[1,1024]{1,0:T(1,128)S(1)}, f32[1,1024]{1,0:T(1,128)S(1)}, u32[]{:S(2)}, u32[]{:S(2)}) collective-permute-start(f32[1,1024]{1,0:T(1,128)S(1)} %get-tuple-element.88), channel_id=1, source_target_pairs={{0,1},{1,2},{2,3},{3,4},{4,5},{5,6},{6,7},{8,9},{9,10},{10,11},{11... | collective-permute-start | bytes 12296 | tf_op jit(solution)/shard_map/ppermute | solution.py:30
  59.9 5.9 %collective-permute-start.7 = (f32[2,1,1,1024]{3,2,1,0:T(1,128)S(1)}, f32[2,1,1,1024]{3,2,1,0:T(1,128)S(1)}, u32[]{:S(2)}, u32[]{:S(2)}) collective-permute-start(f32[2,1,1,1024]{3,2,1,0:T(1,128)S(1)} %get-tuple-element.77), channel_id=1, source_target_pairs={{1,0},{2,1},{3,2},{4,3},{5,4},{6,5},{7,6},{9,8},{10,9},{11,10},{12... | collective-permute-start | bytes 24584 | tf_op jit(solution)/shard_map/ppermute | solution.py:33
  61.9 6.8 %collective-permute-start.8 = (f32[2,1,1,1024]{3,2,1,0:T(1,128)S(1)}, f32[2,1,1,1024]{3,2,1,0:T(1,128)S(1)}, u32[]{:S(2)}, u32[]{:S(2)}) collective-permute-start(f32[2,1,1,1024]{3,2,1,0:T(1,128)S(1)} %get-tuple-element.76), channel_id=1, source_target_pairs={{0,1},{1,2},{2,3},{3,4},{4,5},{5,6},{6,7},{8,9},{9,10},{10,11},{11... | collective-permute-start | bytes 24584 | tf_op jit(solution)/shard_map/ppermute | solution.py:30
  69.7 7.1 %collective-permute-start.10 = (f32[2,1,1,1024]{3,2,1,0:T(1,128)S(1)}, f32[2,1,1,1024]{3,2,1,0:T(1,128)S(1)}, u32[]{:S(2)}, u32[]{:S(2)}) collective-permute-start(f32[2,1,1,1024]{3,2,1,0:T(1,128)S(1)} %get-tuple-element.70), channel_id=1, source_target_pairs={{0,1},{1,2},{2,3},{3,4},{4,5},{5,6},{6,7},{8,9},{9,10},{10,11},{11... | collective-permute-start | bytes 24584 | tf_op jit(solution)/shard_map/ppermute | solution.py:30
  72.4 5.7 %collective-permute-start.9 = (f32[2,1,1,1024]{3,2,1,0:T(1,128)S(1)}, f32[2,1,1,1024]{3,2,1,0:T(1,128)S(1)}, u32[]{:S(2)}, u32[]{:S(2)}) collective-permute-start(f32[2,1,1,1024]{3,2,1,0:T(1,128)S(1)} %get-tuple-element.71), channel_id=1, source_target_pairs={{1,0},{2,1},{3,2},{4,3},{5,4},{6,5},{7,6},{9,8},{10,9},{11,10},{12... | collective-permute-start | bytes 24584 | tf_op jit(solution)/shard_map/ppermute | solution.py:33
  79.3 7.3 %collective-permute-start.11 = (f32[2,1,1,1024]{3,2,1,0:T(1,128)S(1)}, f32[2,1,1,1024]{3,2,1,0:T(1,128)S(1)}, u32[]{:S(2)}, u32[]{:S(2)}) collective-permute-start(f32[2,1,1,1024]{3,2,1,0:T(1,128)S(1)} %get-tuple-element.69), channel_id=1, source_target_pairs={{1,0},{2,1},{3,2},{4,3},{5,4},{6,5},{7,6},{9,8},{10,9},{11,10},{12... | collective-permute-start | bytes 24584 | tf_op jit(solution)/shard_map/ppermute | solution.py:33
  84.7 6.8 %collective-permute-start.12 = (f32[2,1,1,1024]{3,2,1,0:T(1,128)S(1)}, f32[2,1,1,1024]{3,2,1,0:T(1,128)S(1)}, u32[]{:S(2)}, u32[]{:S(2)}) collective-permute-start(f32[2,1,1,1024]{3,2,1,0:T(1,128)S(1)} %get-tuple-element.68), channel_id=1, source_target_pairs={{0,1},{1,2},{2,3},{3,4},{4,5},{5,6},{6,7},{8,9},{9,10},{10,11},{11... | collective-permute-start | bytes 24584 | tf_op jit(solution)/shard_map/ppermute | solution.py:30
  92.6 5.9 %collective-permute-start.13 = (f32[2,1,1,1024]{3,2,1,0:T(1,128)S(1)}, f32[2,1,1,1024]{3,2,1,0:T(1,128)S(1)}, u32[]{:S(2)}, u32[]{:S(2)}) collective-permute-start(f32[2,1,1,1024]{3,2,1,0:T(1,128)S(1)} %get-tuple-element.67), channel_id=1, source_target_pairs={{1,0},{2,1},{3,2},{4,3},{5,4},{6,5},{7,6},{9,8},{10,9},{11,10},{12... | collective-permute-start | bytes 24584 | tf_op jit(solution)/shard_map/ppermute | solution.py:33
  94.6 6.8 %collective-permute-start.14 = (f32[2,1,1,1024]{3,2,1,0:T(1,128)S(1)}, f32[2,1,1,1024]{3,2,1,0:T(1,128)S(1)}, u32[]{:S(2)}, u32[]{:S(2)}) collective-permute-start(f32[2,1,1,1024]{3,2,1,0:T(1,128)S(1)} %get-tuple-element.66), channel_id=1, source_target_pairs={{0,1},{1,2},{2,3},{3,4},{4,5},{5,6},{6,7},{8,9},{9,10},{10,11},{11... | collective-permute-start | bytes 24584 | tf_op jit(solution)/shard_map/ppermute | solution.py:30
  102.6 5.9 %collective-permute-start.15 = (f32[2,1,1,1024]{3,2,1,0:T(1,128)S(1)}, f32[2,1,1,1024]{3,2,1,0:T(1,128)S(1)}, u32[]{:S(2)}, u32[]{:S(2)}) collective-permute-start(f32[2,1,1,1024]{3,2,1,0:T(1,128)S(1)} %get-tuple-element.65), channel_id=1, source_target_pairs={{1,0},{2,1},{3,2},{4,3},{5,4},{6,5},{7,6},{9,8},{10,9},{11,10},{12... | collective-permute-start | bytes 24584 | tf_op jit(solution)/shard_map/ppermute | solution.py:33
  104.5 6.8 %collective-permute-start.16 = (f32[2,1,1,1024]{3,2,1,0:T(1,128)S(1)}, f32[2,1,1,1024]{3,2,1,0:T(1,128)S(1)}, u32[]{:S(2)}, u32[]{:S(2)}) collective-permute-start(f32[2,1,1,1024]{3,2,1,0:T(1,128)S(1)} %get-tuple-element.64), channel_id=1, source_target_pairs={{0,1},{1,2},{2,3},{3,4},{4,5},{5,6},{6,7},{8,9},{9,10},{10,11},{11... | collective-permute-start | bytes 24584 | tf_op jit(solution)/shard_map/ppermute | solution.py:30
  112.6 6.0 %collective-permute-start.17 = (f32[2,1,1,1024]{3,2,1,0:T(1,128)S(1)}, f32[2,1,1,1024]{3,2,1,0:T(1,128)S(1)}, u32[]{:S(2)}, u32[]{:S(2)}) collective-permute-start(f32[2,1,1,1024]{3,2,1,0:T(1,128)S(1)} %get-tuple-element.63), channel_id=1, source_target_pairs={{1,0},{2,1},{3,2},{4,3},{5,4},{6,5},{7,6},{9,8},{10,9},{11,10},{12... | collective-permute-start | bytes 24584 | tf_op jit(solution)/shard_map/ppermute | solution.py:33
  114.7 6.8 %collective-permute-start.18 = (f32[2,1,1,1024]{3,2,1,0:T(1,128)S(1)}, f32[2,1,1,1024]{3,2,1,0:T(1,128)S(1)}, u32[]{:S(2)}, u32[]{:S(2)}) collective-permute-start(f32[2,1,1,1024]{3,2,1,0:T(1,128)S(1)} %get-tuple-element.62), channel_id=1, source_target_pairs={{0,1},{1,2},{2,3},{3,4},{4,5},{5,6},{6,7},{8,9},{9,10},{10,11},{11... | collective-permute-start | bytes 24584 | tf_op jit(solution)/shard_map/ppermute | solution.py:30
  122.8 5.9 %collective-permute-start.19 = (f32[2,1,1,1024]{3,2,1,0:T(1,128)S(1)}, f32[2,1,1,1024]{3,2,1,0:T(1,128)S(1)}, u32[]{:S(2)}, u32[]{:S(2)}) collective-permute-start(f32[2,1,1,1024]{3,2,1,0:T(1,128)S(1)} %get-tuple-element.61), channel_id=1, source_target_pairs={{1,0},{2,1},{3,2},{4,3},{5,4},{6,5},{7,6},{9,8},{10,9},{11,10},{12... | collective-permute-start | bytes 24584 | tf_op jit(solution)/shard_map/ppermute | solution.py:33
  124.7 6.8 %collective-permute-start.20 = (f32[2,1,1,1024]{3,2,1,0:T(1,128)S(1)}, f32[2,1,1,1024]{3,2,1,0:T(1,128)S(1)}, u32[]{:S(2)}, u32[]{:S(2)}) collective-permute-start(f32[2,1,1,1024]{3,2,1,0:T(1,128)S(1)} %get-tuple-element.60), channel_id=1, source_target_pairs={{0,1},{1,2},{2,3},{3,4},{4,5},{5,6},{6,7},{8,9},{9,10},{10,11},{11... | collective-permute-start | bytes 24584 | tf_op jit(solution)/shard_map/ppermute | solution.py:30
  133.1 2.0 %collective-permute-start.21 = (f32[2,1,64,1024]{3,2,1,0:T(8,128)S(1)}, f32[2,1,64,1024]{3,2,1,0:T(8,128)S(1)}, u32[]{:S(2)}, u32[]{:S(2)}) collective-permute-start(f32[2,1,64,1024]{3,2,1,0:T(8,128)S(1)} %pad_maximum_fusion.17), channel_id=1, source_target_pairs={{0,8},{8,0},{16,24},{24,16},{32,40},{40,32},{48,56},{56,48},{64,72... | collective-permute-start | bytes 1572872 | tf_op jit(solution)/shard_map/ppermute | solution.py:22
  135.4 14.1 %collective-permute-start.22 = (f32[2,1,64,1024]{3,2,1,0:T(8,128)S(1)}, f32[2,1,64,1024]{3,2,1,0:T(8,128)S(1)}, u32[]{:S(2)}, u32[]{:S(2)}) collective-permute-start(f32[2,1,64,1024]{3,2,1,0:T(8,128)S(1)} %fusion.58), channel_id=1, source_target_pairs={{0,16},{8,24},{16,0},{24,8},{32,48},{40,56},{48,32},{56,40},{64,80... | collective-permute-start | bytes 1572872 | tf_op jit(solution)/shard_map/ppermute | solution.py:22
  149.9 14.7 %collective-permute-start.23 = (f32[2,1,64,1024]{3,2,1,0:T(8,128)S(1)}, f32[2,1,64,1024]{3,2,1,0:T(8,128)S(1)}, u32[]{:S(2)}, u32[]{:S(2)}) collective-permute-start(f32[2,1,64,1024]{3,2,1,0:T(8,128)S(1)} %fusion.61), channel_id=1, source_target_pairs={{0,32},{8,40},{16,48},{24,56},{32,0},{40,8},{48,16},{56,24},{64,96... | collective-permute-start | bytes 1572872 | tf_op jit(solution)/shard_map/ppermute | solution.py:22
  164.9 12.5 %collective-permute-start.24 = (f32[2,1,64,1024]{3,2,1,0:T(8,128)S(1)}, f32[2,1,64,1024]{3,2,1,0:T(8,128)S(1)}, u32[]{:S(2)}, u32[]{:S(2)}) collective-permute-start(f32[2,1,64,1024]{3,2,1,0:T(8,128)S(1)} %fusion.64), channel_id=1, source_target_pairs={{0,64},{8,72},{16,80},{24,88},{32,96},{40,104},{48,112},{56,120},{... | collective-permute-start | bytes 1572872 | tf_op jit(solution)/shard_map/ppermute | solution.py:22
  177.7 8.0 %collective-permute-start.25 = (f32[1,64,1024]{2,1,0:T(8,128)S(1)}, f32[1,64,1024]{2,1,0:T(8,128)S(1)}, u32[]{:S(2)}, u32[]{:S(2)}) collective-permute-start(f32[1,64,1024]{2,1,0:T(8,128)S(1)} %fusion.80), channel_id=1, source_target_pairs={{0,128},{8,136},{16,144},{24,152},{32,160},{40,168},{48,176},{56,1... | collective-permute-start | bytes 786440 | tf_op jit(solution)/shard_map/ppermute | solution.py:22
where the time goes:
time: 187 us; the launch traced here: 186 us
  waiting for transfers between devices  105 us (56%)
  starting transfers between devices  64.2 us (34%)
  other arithmetic  13.9 us (7%)
  between operations  2.42 us (1%)
    ppermute x10, waiting for transfers between devices, from_partner(): return lax.ppermute(value, axis, pairs)  82.1 us
    ppermute x8, starting transfers between devices, padded_2(): lax.ppermute(lax.slice_in_dim(block, block.shape[dim] - width, None, axis...  28.1 us
    ppermute x8, waiting for transfers between devices, padded_2(): lax.ppermute(lax.slice_in_dim(block, block.shape[dim] - width, None, axis...  21.6 us
    ppermute x8, starting transfers between devices, padded_2(): lax.ppermute(lax.slice_in_dim(block, 0, width, axis=dim), axis, backward)  21.5 us
    ppermute x10, starting transfers between devices, from_partner(): return lax.ppermute(value, axis, pairs)  14.6 us
  transfers between devices with their start and end apart: 26, of which 17 were waited for; matrix products, arithmetic and copies ran while one was open for 0% of the time, Pallas kernels for 0%

commit v1 on v0

--- a/solution.py
+++ b/solution.py
@@ -7,6 +7,7 @@
 
 SWEEPS = 2
 DEGREE = 4
+HALO = 8
 
 
 circulant_alpha = 0.05
@@ -20,19 +21,6 @@
     mask = 2**bit
     pairs = [(source, source ^ mask) for source in range(lax.axis_size(axis))]
     return lax.ppermute(value, axis, pairs)
-
-
-def padded_2(block, sides, width):
-    for axis, dim in sides:
-        count = lax.axis_size(axis)
-        forward = [(i, i + 1) for i in range(count - 1)]
-        backward = [(target, source) for source, target in forward]
-        low = lax.ppermute(
-            lax.slice_in_dim(block, block.shape[dim] - width, None, axis=dim), axis, forward
-        )
-        high = lax.ppermute(lax.slice_in_dim(block, 0, width, axis=dim), axis, backward)
-        block = jnp.concatenate([low, block, high], axis=dim)
-    return block
 
 
 def step_weights(count):
@@ -162,11 +150,12 @@
     return (shift_real, shift_imag, diag_real / magnitude, -shift_imag / magnitude)
 
 
-def solve_each(spectrum, frequencies, kappa):
+def solve_each(spectrum, frequencies, kappa_rows, inside):
     total_steps = spectrum.shape[1] * lax.axis_size("tm")
-    kappa_rows = padded_2(kappa, (("row", 0),), 1)
-    faces = face_terms(kappa_rows)
+    faces = face_terms(jnp.pad(kappa_rows, ((1, 1), (0, 0))))
     shift_real, shift_imag, inv_real, inv_imag = shift_terms(frequencies, faces, total_steps)
+    inv_real = inv_real * inside
+    inv_imag = inv_imag * inside
     state = jnp.zeros_like(spectrum)
     first = True
     for sweep in range(SWEEPS):
@@ -175,7 +164,7 @@
                 residual = spectrum
                 first = False
             else:
-                extended = padded_2(state, (("row", 2),), 1)
+                extended = jnp.pad(state, ((0, 0), (0, 0), (1, 1), (0, 0)))
                 image = spatial(extended, faces)
                 image_real = shift_real * state[0] - shift_imag * state[1] + image[0]
                 image_imag = shift_real * state[1] + shift_imag * state[0] + image[1]
@@ -186,12 +175,24 @@
     return state
 
 
-def solve_block(spectrum, frequencies, kappa):
-    return solve_each(spectrum, frequencies, kappa)
+def with_halo(right_side, kappa, width):
+    rows = kappa.shape[0]
+    count = lax.axis_size("row")
+    forward = [(i, i + 1) for i in range(count - 1)]
+    backward = [(target, source) for source, target in forward]
+    joined = jnp.concatenate([right_side, kappa[None]], axis=0)
+    low = lax.ppermute(joined[:, rows - width :], "row", forward)
+    high = lax.ppermute(joined[:, :width], "row", backward)
+    joined = jnp.concatenate([low, joined, high], axis=1)
+    place = lax.axis_index("row") * rows - width + jnp.arange(rows + 2 * width)
+    inside = ((place >= 0) & (place < rows * count)).astype(jnp.float32)[:, None]
+    return joined[:-1], joined[-1], inside
 
 
 def body(right_side, kappa):
     steps_dev = right_side.shape[0]
+    rows = kappa.shape[0]
+    width = HALO
     tm_size = lax.axis_size("tm")
     total_steps = steps_dev * tm_size
     device = lax.axis_index("tm")
@@ -199,10 +200,12 @@
     global_steps = device * steps_dev + local_steps
     log_alpha = math.log(circulant_alpha)
     step_float = global_steps.astype(jnp.float32)
-    scaled = right_side * jnp.exp(log_alpha * step_float / total_steps)[:, None, None]
+    wide_side, kappa_rows, inside = with_halo(right_side, kappa, width)
+    scaled = wide_side * jnp.exp(log_alpha * step_float / total_steps)[:, None, None]
     levels = tm_size.bit_length() - 1
     spectrum, frequencies = forward_pairs(scaled, device, levels, tm_size, total_steps)
-    solved = solve_block(spectrum, frequencies, kappa)
+    solved = solve_each(spectrum, frequencies, kappa_rows, inside)
+    solved = solved[:, :, width : width + rows]
     signal = backward_pairs(solved, device, levels, total_steps)
     return signal * jnp.exp(-log_alpha * step_float / total_steps)[:, None, None]
 

time: 187 us -> 138 us (0.74)
  the two profiles are of different devices: /device:TPU:134 before, /device:TPU:102 now
where the time goes in v1:
time: 138 us; the launch traced here: 137 us
  waiting for transfers between devices  92.6 us (67%)
  starting transfers between devices  22 us (16%)
  other arithmetic  19 us (14%)
  between operations  2.2 us (2%)
  local copies, waits for them, and re-layouts  1.49 us (1%)
    ppermute x10, waiting for transfers between devices, from_partner(): return lax.ppermute(value, axis, pairs)  87.2 us
    ppermute x10, starting transfers between devices, from_partner(): return lax.ppermute(value, axis, pairs)  15.1 us
    sub x7, other arithmetic, spatial(): diagonal * centre - coupled - courant_rows * below - courant_cols * before  5.69 us
    ppermute x1, waiting for transfers between devices, with_halo(): high = lax.ppermute(joined[:, :width], 'row', backward)  5.38 us
    ppermute x1, starting transfers between devices, with_halo(): low = lax.ppermute(joined[:, rows - width:], 'row', forward)  5.04 us
  transfers between devices with their start and end apart: 12, of which 11 were waited for; matrix products, arithmetic and copies ran while one was open for 0% of the time, Pallas kernels for 0%

profile of v1, /device:TPU:102, one launch (start us, length us, event | category | flops | bytes accessed | tf_op | source)
XLA Modules:
  0.0 137.4 jit_solution(16500425264476521055)
XLA Ops:
  0.0 0.9 pad_maximum_fusion.6
  0.9 5.0 %collective-permute-start = (f32[2,8,1024]{2,1,0:T(8,128)S(1)}, f32[2,8,1024]{2,1,0:T(8,128)S(1)}, u32[]{:S(2)}, u32[]{:S(2)}) collective-permute-start(f32[2,8,1024]{2,1,0:T(8,128)S(1)} %get-tuple-element.76), channel_id=1, source_target_pairs={{0,1},{1,2},{2,3},{3,4},{4,5},{5,6},{6,7},{8,9},{9,10},{10,11},{11... | collective-permute-start | bytes 196616 | tf_op jit(solution)/shard_map/ppermute | solution.py:184
  5.9 1.9 %collective-permute-start.1 = (f32[2,8,1024]{2,1,0:T(8,128)S(1)}, f32[2,8,1024]{2,1,0:T(8,128)S(1)}, u32[]{:S(2)}, u32[]{:S(2)}) collective-permute-start(f32[2,8,1024]{2,1,0:T(8,128)S(1)} %get-tuple-element.77), channel_id=1, source_target_pairs={{1,0},{2,1},{3,2},{4,3},{5,4},{6,5},{7,6},{9,8},{10,9},{11,10},{12... | collective-permute-start | bytes 196616 | tf_op jit(solution)/shard_map/ppermute | solution.py:185
  7.9 5.4 %collective-permute-done.1 = f32[2,8,1024]{2,1,0:T(8,128)S(1)} collective-permute-done((f32[2,8,1024]{2,1,0:T(8,128)S(1)}, f32[2,8,1024]{2,1,0:T(8,128)S(1)}, u32[]{:S(2)}, u32[]{:S(2)}) %collective-permute-start.1) | collective-permute-done | bytes 65568 | tf_op jit(solution)/shard_map/ppermute | solution.py:185
  13.4 0.8 slice_bitcast_fusion.14
  14.1 1.4 %collective-permute-start.2 = (f32[1,80,1024]{2,1,0:T(8,128)S(1)}, f32[1,80,1024]{2,1,0:T(8,128)S(1)}, u32[]{:S(2)}, u32[]{:S(2)}) collective-permute-start(f32[1,80,1024]{2,1,0:T(8,128)S(1)} %get-tuple-element.51), channel_id=1, source_target_pairs={{0,128},{8,136},{16,144},{24,152},{32,160},{40,168},{48,176},{56,1... | collective-permute-start | bytes 983048 | tf_op jit(solution)/shard_map/ppermute | solution.py:23
  15.7 8.0 %collective-permute-done.2 = f32[1,80,1024]{2,1,0:T(8,128)S(1)} collective-permute-done((f32[1,80,1024]{2,1,0:T(8,128)S(1)}, f32[1,80,1024]{2,1,0:T(8,128)S(1)}, u32[]{:S(2)}, u32[]{:S(2)}) %collective-permute-start.2) | collective-permute-done | bytes 327712 | tf_op jit(solution)/shard_map/ppermute | solution.py:23
  23.8 0.9 collective-permute-start.3
  24.9 13.1 %collective-permute-done.3 = f32[2,1,80,1024]{3,2,1,0:T(8,128)S(1)} collective-permute-done((f32[2,1,80,1024]{3,2,1,0:T(8,128)S(1)}, f32[2,1,80,1024]{3,2,1,0:T(8,128)S(1)}, u32[]{:S(2)}, u32[]{:S(2)}) %collective-permute-start.3) | collective-permute-done | bytes 655392 | tf_op jit(solution)/shard_map/ppermute | solution.py:23
  38.2 1.0 maximum_select_fusion
  39.2 3.2 %collective-permute-start.4 = (f32[2,1,80,1024]{3,2,1,0:T(8,128)}, f32[2,1,80,1024]{3,2,1,0:T(8,128)S(1)}, u32[]{:S(2)}, u32[]{:S(2)}) collective-permute-start(f32[2,1,80,1024]{3,2,1,0:T(8,128)} %maximum_select_fusion), channel_id=1, source_target_pairs={{0,32},{8,40},{16,48},{24,56},{32,0},{40,8},{48,16},{56,24},{64,96... | collective-permute-start | bytes 1966088 | tf_op jit(solution)/shard_map/ppermute | solution.py:23
  42.6 11.5 %collective-permute-done.4 = f32[2,1,80,1024]{3,2,1,0:T(8,128)S(1)} collective-permute-done((f32[2,1,80,1024]{3,2,1,0:T(8,128)}, f32[2,1,80,1024]{3,2,1,0:T(8,128)S(1)}, u32[]{:S(2)}, u32[]{:S(2)}) %collective-permute-start.4) | collective-permute-done | bytes 655392 | tf_op jit(solution)/shard_map/ppermute | solution.py:23
  54.1 0.2 fusion.79
  54.3 0.6 copy-done.1
  55.0 1.4 %maximum_select_fusion.1 = f32[2,1,80,1024]{3,2,1,0:T(8,128)S(1)} fusion(f32[1,1,80,1024]{3,2,1,0:T(8,128)S(1)} %get-tuple-element.57, f32[1,1,80,1024]{3,2,1,0:T(8,128)S(1)} %get-tuple-element.56, f32[2,1,80,1024]{3,2,1,0:T(8,128)} %copy-done.1, pred[]{:T(512)S(6)} %eq.54, f32[2,1,80,1024]{3,2,1,0:T(8,128)S(1)} %collective-permute-done.3, ...), kind=kLoop, calls=%fused_computation.59 | loop fusion | flops 1146880 | bytes 3932162 | tf_op jit(solution)/shard_map/jit(_where)/select_n | solution.py:101
  56.4 1.7 %collective-permute-start.5 = (f32[2,1,80,1024]{3,2,1,0:T(8,128)S(1)}, f32[2,1,80,1024]{3,2,1,0:T(8,128)S(1)}, u32[]{:S(2)}, u32[]{:S(2)}) collective-permute-start(f32[2,1,80,1024]{3,2,1,0:T(8,128)S(1)} %maximum_select_fusion.1), channel_id=1, source_target_pairs={{0,16},{8,24},{16,0},{24,8},{32,48},{40,56},{48,32},{56,40},{64,80... | collective-permute-start | bytes 1966088 | tf_op jit(solution)/shard_map/ppermute | solution.py:23
  58.3 10.5 %collective-permute-done.5 = f32[2,1,80,1024]{3,2,1,0:T(8,128)S(1)} collective-permute-done((f32[2,1,80,1024]{3,2,1,0:T(8,128)S(1)}, f32[2,1,80,1024]{3,2,1,0:T(8,128)S(1)}, u32[]{:S(2)}, u32[]{:S(2)}) %collective-permute-start.5) | collective-permute-done | bytes 655392 | tf_op jit(solution)/shard_map/ppermute | solution.py:23
  69.0 0.1 maximum_select_fusion.2
  69.1 0.3 collective-permute-start.6
  69.6 0.3 copy-done
  70.0 0.3 add_add_fusion
  70.3 1.2 collective-permute-done.6
  71.7 0.2 maximum_select_fusion.3
  71.8 0.3 subtract_bitcast_fusion.7
  72.1 0.2 fusion.75
  72.4 0.6 fusion.5
  73.0 0.1 slice_add_fusion.13
  73.3 0.1 subtract_bitcast_fusion.6
  73.6 0.7 fusion.11
  74.3 0.1 slice_add_fusion.11
  74.5 0.1 subtract_bitcast_fusion.5
  74.7 0.2 fusion.43
  74.9 0.8 fusion.17
  75.9 0.1 subtract_bitcast_fusion.4
  76.1 0.3 fusion.44
  76.4 0.8 fusion.23
  77.2 0.1 slice_add_fusion.7
  77.4 0.1 subtract_bitcast_fusion.3
  77.6 0.3 fusion.45
  78.0 0.9 fusion.29
  79.1 0.1 subtract_bitcast_fusion.2
  79.2 0.4 fusion.46
  79.8 1.0 fusion.35
  80.9 0.1 subtract_bitcast_fusion.1
  81.0 0.5 fusion.47
  81.7 1.0 fusion.41
  82.9 0.1 subtract_bitcast_fusion
  83.0 0.6 fusion.48
  83.6 0.2 subtract_bitcast_fusion.8
  83.9 0.4 collective-permute-start.7
  84.3 1.8 %collective-permute-done.7 = f32[2,1,64,1024]{3,2,1,0:T(8,128)S(1)} collective-permute-done((f32[2,1,64,1024]{3,2,1,0:T(8,128)S(1)}, f32[2,1,64,1024]{3,2,1,0:T(8,128)S(1)}, u32[]{:S(2)}, u32[]{:S(2)}) %collective-permute-start.7) | collective-permute-done | bytes 524320 | tf_op jit(solution)/shard_map/ppermute | solution.py:23
  86.1 0.2 fusion.51
  86.3 1.7 %collective-permute-start.8 = (f32[2,1,64,1024]{3,2,1,0:T(8,128)S(1)}, f32[2,1,64,1024]{3,2,1,0:T(8,128)S(1)}, u32[]{:S(2)}, u32[]{:S(2)}) collective-permute-start(f32[2,1,64,1024]{3,2,1,0:T(8,128)S(1)} %fusion.51), channel_id=1, source_target_pairs={{0,16},{8,24},{16,0},{24,8},{32,48},{40,56},{48,32},{56,40},{64,80... | collective-permute-start | bytes 1572872 | tf_op jit(solution)/shard_map/ppermute | solution.py:23
  88.2 12.2 %collective-permute-done.8 = f32[2,1,64,1024]{3,2,1,0:T(8,128)S(1)} collective-permute-done((f32[2,1,64,1024]{3,2,1,0:T(8,128)S(1)}, f32[2,1,64,1024]{3,2,1,0:T(8,128)S(1)}, u32[]{:S(2)}, u32[]{:S(2)}) %collective-permute-start.8) | collective-permute-done | bytes 524320 | tf_op jit(solution)/shard_map/ppermute | solution.py:23
  100.4 0.4 fusion.54
  100.8 3.3 %collective-permute-start.9 = (f32[2,1,64,1024]{3,2,1,0:T(8,128)S(1)}, f32[2,1,64,1024]{3,2,1,0:T(8,128)S(1)}, u32[]{:S(2)}, u32[]{:S(2)}) collective-permute-start(f32[2,1,64,1024]{3,2,1,0:T(8,128)S(1)} %fusion.54), channel_id=1, source_target_pairs={{0,32},{8,40},{16,48},{24,56},{32,0},{40,8},{48,16},{56,24},{64,96... | collective-permute-start | bytes 1572872 | tf_op jit(solution)/shard_map/ppermute | solution.py:23
  104.4 11.2 %collective-permute-done.9 = f32[2,1,64,1024]{3,2,1,0:T(8,128)S(1)} collective-permute-done((f32[2,1,64,1024]{3,2,1,0:T(8,128)S(1)}, f32[2,1,64,1024]{3,2,1,0:T(8,128)S(1)}, u32[]{:S(2)}, u32[]{:S(2)}) %collective-permute-start.9) | collective-permute-done | bytes 524320 | tf_op jit(solution)/shard_map/ppermute | solution.py:23
  115.6 0.2 fusion.57
  115.8 0.9 collective-permute-start.10
  117.2 11.1 %collective-permute-done.10 = f32[2,1,64,1024]{3,2,1,0:T(8,128)S(1)} collective-permute-done((f32[2,1,64,1024]{3,2,1,0:T(8,128)S(1)}, f32[2,1,64,1024]{3,2,1,0:T(8,128)S(1)}, u32[]{:S(2)}, u32[]{:S(2)}) %collective-permute-start.10) | collective-permute-done | bytes 524320 | tf_op jit(solution)/shard_map/ppermute | solution.py:23
  128.4 0.2 fusion.60
  128.6 1.3 collective-permute-start.11
  130.0 6.6 %collective-permute-done.11 = f32[1,64,1024]{2,1,0:T(8,128)S(1)} collective-permute-done((f32[1,64,1024]{2,1,0:T(8,128)S(1)}, f32[1,64,1024]{2,1,0:T(8,128)S(1)}, u32[]{:S(2)}, u32[]{:S(2)}) %collective-permute-start.11) | collective-permute-done | bytes 262176 | tf_op jit(solution)/shard_map/ppermute | solution.py:23
  136.6 0.8 select_multiply_fusion
  (48 shorter events, 3.1 us)
Async XLA Ops:
  0.0 13.3 %copy-start.2 = (f32[64,1024]{1,0:T(8,128)S(1)}, f32[64,1024]{1,0:T(8,128)}, u32[]{:S(2)}) copy-start(f32[64,1024]{1,0:T(8,128)} %param.3) | copy-start | bytes 786436
  0.0 13.3 %copy-start.3 = (f32[1,64,1024]{2,1,0:T(8,128)S(1)}, f32[1,64,1024]{2,1,0:T(8,128)}, u32[]{:S(2)}) copy-start(f32[1,64,1024]{2,1,0:T(8,128)} %param.2) | copy-start | bytes 786436
  0.9 7.0 %collective-permute-start = (f32[2,8,1024]{2,1,0:T(8,128)S(1)}, f32[2,8,1024]{2,1,0:T(8,128)S(1)}, u32[]{:S(2)}, u32[]{:S(2)}) collective-permute-start(f32[2,8,1024]{2,1,0:T(8,128)S(1)} %get-tuple-element.76), channel_id=1, source_target_pairs={{0,1},{1,2},{2,3},{3,4},{4,5},{5,6},{6,7},{8,9},{9,10},{10,11},{11... | collective-permute-start | bytes 196616 | tf_op jit(solution)/shard_map/ppermute | solution.py:184
  5.9 7.4 %collective-permute-start.1 = (f32[2,8,1024]{2,1,0:T(8,128)S(1)}, f32[2,8,1024]{2,1,0:T(8,128)S(1)}, u32[]{:S(2)}, u32[]{:S(2)}) collective-permute-start(f32[2,8,1024]{2,1,0:T(8,128)S(1)} %get-tuple-element.77), channel_id=1, source_target_pairs={{1,0},{2,1},{3,2},{4,3},{5,4},{6,5},{7,6},{9,8},{10,9},{11,10},{12... | collective-permute-start | bytes 196616 | tf_op jit(solution)/shard_map/ppermute | solution.py:185
  14.1 9.5 %collective-permute-start.2 = (f32[1,80,1024]{2,1,0:T(8,128)S(1)}, f32[1,80,1024]{2,1,0:T(8,128)S(1)}, u32[]{:S(2)}, u32[]{:S(2)}) collective-permute-start(f32[1,80,1024]{2,1,0:T(8,128)S(1)} %get-tuple-element.51), channel_id=1, source_target_pairs={{0,128},{8,136},{16,144},{24,152},{32,160},{40,168},{48,176},{56,1... | collective-permute-start | bytes 983048 | tf_op jit(solution)/shard_map/ppermute | solution.py:23
  23.8 14.2 %collective-permute-start.3 = (f32[2,1,80,1024]{3,2,1,0:T(8,128)S(1)}, f32[2,1,80,1024]{3,2,1,0:T(8,128)S(1)}, u32[]{:S(2)}, u32[]{:S(2)}) collective-permute-start(f32[2,1,80,1024]{3,2,1,0:T(8,128)S(1)} %pad_maximum_fusion.1), channel_id=1, source_target_pairs={{0,64},{8,72},{16,80},{24,88},{32,96},{40,104},{48,112},{56,120},{... | collective-permute-start | bytes 1966088 | tf_op jit(solution)/shard_map/ppermute | solution.py:23
  39.2 14.9 %collective-permute-start.4 = (f32[2,1,80,1024]{3,2,1,0:T(8,128)}, f32[2,1,80,1024]{3,2,1,0:T(8,128)S(1)}, u32[]{:S(2)}, u32[]{:S(2)}) collective-permute-start(f32[2,1,80,1024]{3,2,1,0:T(8,128)} %maximum_select_fusion), channel_id=1, source_target_pairs={{0,32},{8,40},{16,48},{24,56},{32,0},{40,8},{48,16},{56,24},{64,96... | collective-permute-start | bytes 1966088 | tf_op jit(solution)/shard_map/ppermute | solution.py:23
  54.1 0.8 copy-start.1
  56.4 12.4 %collective-permute-start.5 = (f32[2,1,80,1024]{3,2,1,0:T(8,128)S(1)}, f32[2,1,80,1024]{3,2,1,0:T(8,128)S(1)}, u32[]{:S(2)}, u32[]{:S(2)}) collective-permute-start(f32[2,1,80,1024]{3,2,1,0:T(8,128)S(1)} %maximum_select_fusion.1), channel_id=1, source_target_pairs={{0,16},{8,24},{16,0},{24,8},{32,48},{40,56},{48,32},{56,40},{64,80... | collective-permute-start | bytes 1966088 | tf_op jit(solution)/shard_map/ppermute | solution.py:23
  69.0 1.0 copy-start
  69.1 2.4 %collective-permute-start.6 = (f32[2,1,80,1024]{3,2,1,0:T(8,128)S(1)}, f32[2,1,80,1024]{3,2,1,0:T(8,128)S(1)}, u32[]{:S(2)}, u32[]{:S(2)}) collective-permute-start(f32[2,1,80,1024]{3,2,1,0:T(8,128)S(1)} %maximum_select_fusion.2), channel_id=1, source_target_pairs={{0,8},{8,0},{16,24},{24,16},{32,40},{40,32},{48,56},{56,48},{64,72... | collective-permute-start | bytes 1966088 | tf_op jit(solution)/shard_map/ppermute | solution.py:23
  83.9 2.2 %collective-permute-start.7 = (f32[2,1,64,1024]{3,2,1,0:T(8,128)S(1)}, f32[2,1,64,1024]{3,2,1,0:T(8,128)S(1)}, u32[]{:S(2)}, u32[]{:S(2)}) collective-permute-start(f32[2,1,64,1024]{3,2,1,0:T(8,128)S(1)} %pad_maximum_fusion.4), channel_id=1, source_target_pairs={{0,8},{8,0},{16,24},{24,16},{32,40},{40,32},{48,56},{56,48},{64,72... | collective-permute-start | bytes 1572872 | tf_op jit(solution)/shard_map/ppermute | solution.py:23
  86.3 14.1 %collective-permute-start.8 = (f32[2,1,64,1024]{3,2,1,0:T(8,128)S(1)}, f32[2,1,64,1024]{3,2,1,0:T(8,128)S(1)}, u32[]{:S(2)}, u32[]{:S(2)}) collective-permute-start(f32[2,1,64,1024]{3,2,1,0:T(8,128)S(1)} %fusion.51), channel_id=1, source_target_pairs={{0,16},{8,24},{16,0},{24,8},{32,48},{40,56},{48,32},{56,40},{64,80... | collective-permute-start | bytes 1572872 | tf_op jit(solution)/shard_map/ppermute | solution.py:23
  100.8 14.7 %collective-permute-start.9 = (f32[2,1,64,1024]{3,2,1,0:T(8,128)S(1)}, f32[2,1,64,1024]{3,2,1,0:T(8,128)S(1)}, u32[]{:S(2)}, u32[]{:S(2)}) collective-permute-start(f32[2,1,64,1024]{3,2,1,0:T(8,128)S(1)} %fusion.54), channel_id=1, source_target_pairs={{0,32},{8,40},{16,48},{24,56},{32,0},{40,8},{48,16},{56,24},{64,96... | collective-permute-start | bytes 1572872 | tf_op jit(solution)/shard_map/ppermute | solution.py:23
  115.8 12.5 %collective-permute-start.10 = (f32[2,1,64,1024]{3,2,1,0:T(8,128)S(1)}, f32[2,1,64,1024]{3,2,1,0:T(8,128)S(1)}, u32[]{:S(2)}, u32[]{:S(2)}) collective-permute-start(f32[2,1,64,1024]{3,2,1,0:T(8,128)S(1)} %fusion.57), channel_id=1, source_target_pairs={{0,64},{8,72},{16,80},{24,88},{32,96},{40,104},{48,112},{56,120},{... | collective-permute-start | bytes 1572872 | tf_op jit(solution)/shard_map/ppermute | solution.py:23
  128.6 8.0 %collective-permute-start.11 = (f32[1,64,1024]{2,1,0:T(8,128)S(1)}, f32[1,64,1024]{2,1,0:T(8,128)S(1)}, u32[]{:S(2)}, u32[]{:S(2)}) collective-permute-start(f32[1,64,1024]{2,1,0:T(8,128)S(1)} %fusion.71), channel_id=1, source_target_pairs={{0,128},{8,136},{16,144},{24,152},{32,160},{40,168},{48,176},{56,1... | collective-permute-start | bytes 786440 | tf_op jit(solution)/shard_map/ppermute | solution.py:23

commit v2 on v0

v2 whole, which is shorter than its diff:
```python
import math

import jax
import jax.numpy as jnp
import numpy as np
from jax import lax
from jax.sharding import PartitionSpec as P

SWEEPS = 2
DEGREE = 4
HALO = 8


circulant_alpha = 0.05
courant_rows = 0.5
courant_cols = 0.25
cheb_centre = 1.0
cheb_half = 0.7


def step_weights(count):
    return [
        1.0 / (cheb_centre + cheb_half * math.cos(math.pi * (2 * number + 1) / (2 * count)))
        for number in range(count)
    ]


def with_halo(right_side, kappa, width):
    rows = kappa.shape[0]
    count = lax.axis_size("row")
    forward = [(i, i + 1) for i in range(count - 1)]
    backward = [(target, source) for source, target in forward]
    joined = jnp.concatenate([right_side, kappa[None]], axis=0)
    low = lax.ppermute(joined[:, rows - width :], "row", forward)
    high = lax.ppermute(joined[:, :width], "row", backward)
    joined = jnp.concatenate([low, joined, high], axis=1)
    place = lax.axis_index("row") * rows - width + jnp.arange(rows + 2 * width)
    inside = (place >= 0) & (place < rows * count)
    return joined[0], joined[1], inside


def transform_matrices(total):
    half = total // 2
    steps = np.arange(total)
    scale = circulant_alpha ** (steps / total)
    forward = np.zeros((total, total))
    inverse = np.zeros((total, total))
    forward[0] = 1.0
    forward[half] = (-1.0) ** steps
    inverse[:, 0] = 1.0
    inverse[:, half] = (-1.0) ** steps
    for slot in range(1, half):
        angle = 2.0 * np.pi * slot * steps / total
        forward[slot] = np.cos(angle)
        forward[half + slot] = -np.sin(angle)
        inverse[:, slot] = 2.0 * np.cos(angle)
        inverse[:, half + slot] = -2.0 * np.sin(angle)
    forward = forward * scale[None, :]
    inverse = inverse / total / scale[:, None]
    return forward.astype(np.float32), inverse.astype(np.float32)


def slot_shifts(half, total, width):
    decay = circulant_alpha ** (1.0 / total)
    slots = np.arange(half)
    theta = 2.0 * np.pi / total * slots
    real_a = 1.0 - decay * np.cos(theta)
    real_b = real_a.copy()
    imag = decay * np.sin(theta)
    real_b[0] = 1.0 + decay
    imag[0] = 0.0
    spread = lambda v: np.repeat(v.astype(np.float32), width)[None, :]
    return spread(real_a), spread(real_b), spread(imag)


def tile_faces(kappa_rows, tile, tiles, width, margin):
    rows, cols = kappa_rows.shape
    span = cols // tiles
    padded = jnp.pad(kappa_rows, ((1, 1), (margin + 1, width - span - margin + 1)))
    block = lax.dynamic_slice_in_dim(padded, tile * span, width + 2, axis=1)
    centre = block[1:-1, 1:-1]
    north = 0.5 * (centre + block[2:, 1:-1])
    south = 0.5 * (centre + block[:-2, 1:-1])
    east = 0.5 * (centre + block[1:-1, 2:])
    west = 0.5 * (centre + block[1:-1, :-2])
    diagonal = north + south + east + west + (courant_rows + courant_cols)
    return (north, south, east, west, diagonal)


def column_tiles(field, tiles, width, margin):
    rows, cols = field.shape
    span = cols // tiles
    padded = jnp.pad(field, ((0, 0), (margin, 2 * span - margin)))
    main = padded[:, :cols].reshape(rows, tiles, span)
    extra = padded[:, span : cols + span].reshape(rows, tiles, span)[:, :, : width - span]
    return jnp.concatenate([main, extra], axis=2).transpose(1, 0, 2)


def spatial(state, faces):
    north, south, east, west, diagonal = faces
    rows_padded = jnp.pad(state, ((0, 0), (1, 1), (0, 0)))
    cols_padded = jnp.pad(state, ((0, 0), (0, 0), (1, 1)))
    above = rows_padded[:, 2:]
    below = rows_padded[:, :-2]
    after = cols_padded[:, :, 2:]
    before = cols_padded[:, :, :-2]
    coupled = north * above + south * below + east * after + west * before
    return diagonal * state - coupled - courant_rows * below - courant_cols * before


def solve_slots(spectrum, faces, shifts, inside):
    real_a, real_b, imag = shifts
    diag_a = real_a + faces[4]
    diag_b = real_b + faces[4]
    mag_a = diag_a * diag_a + imag * imag
    mag_b = diag_b * diag_b + imag * imag
    inv_a = jnp.where(inside, diag_a / mag_a, 0.0)
    inv_b = jnp.where(inside, diag_b / mag_b, 0.0)
    inv_imag = jnp.where(inside, -imag / mag_a, 0.0)
    state = jnp.zeros_like(spectrum)
    first = True
    for sweep in range(SWEEPS):
        for weight in step_weights(DEGREE):
            if first:
                residual = spectrum
                first = False
            else:
                image = spatial(state, faces)
                image_real = real_a * state[0] - imag * state[1] + image[0]
                image_imag = real_b * state[1] + imag * state[0] + image[1]
                residual = spectrum - jnp.stack([image_real, image_imag])
            corr_real = inv_a * residual[0] - inv_imag * residual[1]
            corr_imag = inv_b * residual[1] + inv_imag * residual[0]
            state = state + weight * jnp.stack([corr_real, corr_imag])
    return state


def body(right_side, kappa):
    steps_dev, rows, cols = right_side.shape
    tiles = lax.axis_size("tm")
    total = steps_dev * tiles
    half = total // 2
    margin = HALO
    span = cols // tiles
    width = span + 2 * margin
    tile = lax.axis_index("tm")
    highest = lax.Precision.HIGHEST
    forward, inverse = transform_matrices(total)

    wide_side, kappa_rows, inside_rows = with_halo(right_side, kappa, margin)
    extended = rows + 2 * margin
    sent = column_tiles(wide_side, tiles, width, margin)
    gathered = lax.all_to_all(sent, "tm", 0, 0, tiled=True)
    spectrum = jnp.einsum("pt,trc->prc", forward, gathered, precision=highest)
    spectrum = spectrum.reshape(2, half, extended, width).transpose(0, 2, 1, 3)
    spectrum = spectrum.reshape(2, extended, half * width)

    place = tile * span - margin + jnp.arange(width)
    inside_cols = (place >= 0) & (place < cols)
    inside = inside_rows[:, None] & inside_cols[None, :]
    inside = jnp.tile(inside, (1, half))
    faces = tuple(jnp.tile(f, (1, half)) for f in tile_faces(kappa_rows, tile, tiles, width, margin))
    shifts = slot_shifts(half, total, width)
    solved = solve_slots(spectrum, faces, shifts, inside)

    solved = solved.reshape(2, extended, half, width)[:, margin : margin + rows, :, margin : margin + span]
    solved = solved.transpose(0, 2, 1, 3).reshape(total, rows, span)
    signal = jnp.einsum("tp,prc->trc", inverse, solved, precision=highest)
    returned = lax.all_to_all(signal, "tm", 0, 0, tiled=True)
    return returned.transpose(1, 0, 2).reshape(steps_dev, rows, cols)


def solution(mesh):
    placed = (P("tm", "row", None), P("row", None))
    return jax.shard_map(
        body, mesh=mesh, in_specs=placed, out_specs=P("tm", "row", None), check_vma=False
    )
```

time: 187 us -> 71.7 us (0.38)
  the two profiles are of different devices: /device:TPU:134 before, /device:TPU:97 now
where the time goes in v2:
time: 71.7 us; the launch traced here: 70.8 us
  other arithmetic  19 us (26%)
  starting transfers between devices  15.6 us (22%)
  waiting for transfers between devices  14.7 us (21%)
  blocking collectives  12.6 us (18%)
  local copies, waits for them, and re-layouts  6.84 us (10%)
  matrix products  1.52 us (2%)
    all_to_all x1, waiting for transfers between devices, body(): gathered = lax.all_to_all(sent, 'tm', 0, 0, tiled=True)  13.7 us
    all_to_all x1, blocking collectives, body(): returned = lax.all_to_all(signal, 'tm', 0, 0, tiled=True)  12.6 us
    all_to_all x1, starting transfers between devices, body(): gathered = lax.all_to_all(sent, 'tm', 0, 0, tiled=True)  8.89 us
    ppermute x1, starting transfers between devices, with_halo(): low = lax.ppermute(joined[:, rows - width:], 'row', forward)  4.76 us
    sub x7, other arithmetic, spatial(): diagonal * state - coupled - courant_rows * below - courant_cols * before  4.25 us
    sub x8, other arithmetic, solve_slots(): corr_real = inv_a * residual[0] - inv_imag * residual[1]  3.88 us
    unnamed x28, local copies, waits for them, and re-layouts  2.82 us
    add x7, other arithmetic, solve_slots(): image_real = real_a * state[0] - imag * state[1] + image[0]  2.61 us
  transfers between devices with their start and end apart: 3, of which 2 were waited for; matrix products, arithmetic and copies ran while one was open for 1% of the time, Pallas kernels for 0%

profile of v2, /device:TPU:97, one launch (start us, length us, event | category | flops | bytes accessed | tf_op | source)
XLA Modules:
  0.0 70.8 jit_solution(6349892699650363046)
XLA Ops:
  0.0 1.2 %copy.21 = f32[64,1024]{0,1:T(8,128)S(1)} copy(f32[64,1024]{1,0:T(8,128)} %param.11) | data formatting | bytes 524288 | tf_op args[1]
  1.2 0.2 copy.22
  1.4 0.4 slice_maximum_fusion
  1.8 0.3 copy.24
  2.1 1.9 %collective-permute-start.1 = (f32[2,8,1024]{2,1,0:T(8,128)S(1)}, f32[2,8,1024]{2,1,0:T(8,128)S(1)}, u32[]{:S(2)}, u32[]{:S(2)}) collective-permute-start(f32[2,8,1024]{2,1,0:T(8,128)S(1)} %copy.24), channel_id=1, source_target_pairs={{1,0},{2,1},{3,2},{4,3},{5,4},{6,5},{7,6},{9,8},{10,9},{11,10},{12... | collective-permute-start | bytes 196616 | tf_op jit(solution)/shard_map/ppermute | solution.py:35
  4.0 0.3 copy.23
  4.3 4.8 %collective-permute-start = (f32[2,8,1024]{2,1,0:T(8,128)S(1)}, f32[2,8,1024]{2,1,0:T(8,128)S(1)}, u32[]{:S(2)}, u32[]{:S(2)}) collective-permute-start(f32[2,8,1024]{2,1,0:T(8,128)S(1)} %copy.23), channel_id=1, source_target_pairs={{0,1},{1,2},{2,3},{3,4},{4,5},{5,6},{6,7},{8,9},{9,10},{10,11},{11... | collective-permute-start | bytes 196616 | tf_op jit(solution)/shard_map/ppermute | solution.py:34
  9.1 0.3 copy.26
  9.4 1.0 %collective-permute-done = f32[2,8,1024]{2,1,0:T(8,128)S(1)} collective-permute-done((f32[2,8,1024]{2,1,0:T(8,128)S(1)}, f32[2,8,1024]{2,1,0:T(8,128)S(1)}, u32[]{:S(2)}, u32[]{:S(2)}) %collective-permute-start) | collective-permute-done | bytes 65568 | tf_op jit(solution)/shard_map/ppermute | solution.py:34
  10.4 0.3 copy.25
  10.7 0.6 pad_maximum_fusion.1
  11.5 1.0 %maximum_bitcast_fusion = f32[32,80,48]{1,2,0:T(8,128)} fusion(f32[80,32,16]{0,2,1:T(8,128)S(1)} %slice.376, f32[80,32,32]{0,2,1:T(8,128)S(1)} %bitcast.279), kind=kLoop, calls=%fused_computation.3 | loop fusion | flops 122880 | bytes 983040 | tf_op jit(solution)/shard_map/transpose | solution.py:96
  12.5 8.9 %all-to-all-start = ((f32[32,80,48]{1,2,0:T(8,128)}), f32[32,80,48]{1,2,0:T(8,128)S(1)}, u32[]{:S(2)}, u32[]{:S(2)}) async-start(f32[32,80,48]{1,2,0:T(8,128)} %maximum_bitcast_fusion), calls=%async_computation | async-start | bytes 1572864 | tf_op jit(solution)/shard_map/all_to_all | solution.py:153
  21.5 0.2 add_add_fusion
  21.7 13.7 %all-to-all-done = f32[32,80,48]{1,2,0:T(8,128)S(1)} async-done(((f32[32,80,48]{1,2,0:T(8,128)}), f32[32,80,48]{1,2,0:T(8,128)S(1)}, u32[]{:S(2)}, u32[]{:S(2)}) %all-to-all-start) | async-done | bytes 491552 | tf_op jit(solution)/shard_map/all_to_all | solution.py:153
  35.4 0.9 %fusion.7 = f32[32,80,48]{1,0,2:T(8,128)S(1)} fusion(f32[32,32,1]{1,0,2:T(8,128)S(1)} %copy-done.7, f32[32,80,48]{1,2,0:T(8,128)S(1)} %all-to-all-done), kind=kOutput, calls=%fused_computation.30 | convolution fusion | flops 47185920 | bytes 987136 | tf_op jit(solution)/shard_map/pt,trc->prc/dot_general | solution.py:154
  36.4 0.5 copy.37
  36.9 0.2 copy-done.8
  37.1 0.5 fusion.31
  37.6 0.1 copy-done
  37.8 0.5 fusion.39
  38.6 0.6 multiply_subtract_fusion.6
  39.2 0.4 slice_add_fusion.14
  39.6 0.1 maximum_subtract_fusion
  39.7 0.5 multiply_subtract_fusion.13
  40.2 0.2 fusion.1
  40.4 0.6 multiply_subtract_fusion.5
  41.0 0.4 slice_add_fusion.12
  41.4 0.1 maximum_subtract_fusion.1
  41.5 0.5 multiply_subtract_fusion.12
  42.0 0.2 fusion.2
  42.2 0.6 multiply_subtract_fusion.4
  42.8 0.4 slice_add_fusion.10
  43.2 0.1 maximum_subtract_fusion.2
  43.3 0.5 multiply_add_fusion.4
  43.8 0.3 fusion.3
  44.1 0.6 multiply_subtract_fusion.3
  44.7 0.4 slice_add_fusion.8
  45.1 0.1 maximum_subtract_fusion.3
  45.2 0.5 multiply_subtract_fusion.10
  45.7 0.4 fusion.4
  46.1 0.6 multiply_subtract_fusion.2
  46.7 0.4 slice_add_fusion.6
  47.2 0.5 multiply_subtract_fusion.9
  47.6 0.7 fusion.5
  48.3 0.6 multiply_subtract_fusion.1
  48.9 0.4 slice_add_fusion.4
  49.4 0.5 multiply_subtract_fusion.8
  49.9 0.5 fusion.6
  50.4 0.6 multiply_subtract_fusion
  51.0 0.4 slice_add_fusion.2
  51.5 0.5 multiply_subtract_fusion.7
  52.0 0.2 fusion
  52.2 1.0 %fusion.21 = f32[2,16,64,32]{2,3,1,0:T(8,128)S(1)} fusion(f32[1,80,16,48]{1,3,2,0:T(8,128)S(1)} %bitcast.269, f32[1,80,16,48]{1,3,2,0:T(8,128)S(1)} %bitcast.268, f32[1,80,16,48]{1,3,2,0:T(8,128)S(1)} %bitcast.284, f32[1,80,16,48]{1,3,2,0:T(8,128)S(1)} %bitcast.283, f32[1,80,16,48]{1,3,2,0:T(8,128)S(1)} %bitcast.277, f32[1,80,16,48]{1,3,2,0:T(8,128)S(1)} %bitcast.276, ...), kind=kLoop, calls=%fused_computation.62 | loop fusion | flops 1048576 | bytes 3244032 | tf_op jit(solution)/shard_map/transpose | solution.py:167
  53.3 0.3 copy.29
  53.6 0.4 copy-done.6
  54.0 0.6 fusion.54
  54.6 0.3 copy.38
  54.9 0.3 reshape.1292
  55.2 12.6 %all_to_all.10 = f32[32,1,2048]{2,1,0:T(1,128)S(1)} all-to-all(f32[32,1,2048]{2,1,0:T(1,128)S(1)} %reshape.1292), channel_id=1, replica_groups=mesh['tm'=32,'row'=8] {'tm'}, dimensions={0} | all-to-all | bytes 524288 | tf_op jit(solution)/shard_map/all_to_all | solution.py:169
  67.9 0.5 broadcast.1031
  68.4 1.3 %reduce = f32[32,2048]{1,0:T(8,128)S(1)} reduce(f32[32,1,2048]{2,1,0:T(1,128)S(1)} %all_to_all.10, f32[]{:T(128)} %broadcast.1031), dimensions={1}, to_apply=%all_to_all.7.reduce_sub_computation | reduce | bytes 524292 | tf_op jit(solution)/shard_map/all_to_all | solution.py:169
  69.6 0.2 reshape.1293
  69.9 0.9 %copy.31 = f32[1,64,1024]{2,1,0:T(8,128)} copy(f32[1,64,1024]{1,2,0:T(8,128)S(1)} %bitcast.280) | data formatting | bytes 524288 | tf_op jit(solution)/shard_map/reshape | solution.py:170
  (38 shorter events, 1.0 us)
Async XLA Ops:
  0.0 1.2 %copy-start.4 = (f32[1,64,1024]{2,1,0:T(8,128)S(1)}, f32[1,64,1024]{2,1,0:T(8,128)}, u32[]{:S(2)}) copy-start(f32[1,64,1024]{2,1,0:T(8,128)} %param.10) | copy-start | bytes 786436
  2.1 7.0 %collective-permute-start.1 = (f32[2,8,1024]{2,1,0:T(8,128)S(1)}, f32[2,8,1024]{2,1,0:T(8,128)S(1)}, u32[]{:S(2)}, u32[]{:S(2)}) collective-permute-start(f32[2,8,1024]{2,1,0:T(8,128)S(1)} %copy.24), channel_id=1, source_target_pairs={{1,0},{2,1},{3,2},{4,3},{5,4},{6,5},{7,6},{9,8},{10,9},{11,10},{12... | collective-permute-start | bytes 196616 | tf_op jit(solution)/shard_map/ppermute | solution.py:35
  4.3 6.1 %collective-permute-start = (f32[2,8,1024]{2,1,0:T(8,128)S(1)}, f32[2,8,1024]{2,1,0:T(8,128)S(1)}, u32[]{:S(2)}, u32[]{:S(2)}) collective-permute-start(f32[2,8,1024]{2,1,0:T(8,128)S(1)} %copy.23), channel_id=1, source_target_pairs={{0,1},{1,2},{2,3},{3,4},{4,5},{5,6},{6,7},{8,9},{9,10},{10,11},{11... | collective-permute-start | bytes 196616 | tf_op jit(solution)/shard_map/ppermute | solution.py:34
  12.5 22.9 %all-to-all-start = ((f32[32,80,48]{1,2,0:T(8,128)}), f32[32,80,48]{1,2,0:T(8,128)S(1)}, u32[]{:S(2)}, u32[]{:S(2)}) async-start(f32[32,80,48]{1,2,0:T(8,128)} %maximum_bitcast_fusion), calls=%async_computation | async-start | bytes 1572864 | tf_op jit(solution)/shard_map/all_to_all | solution.py:153
  21.6 13.8 %copy-start.7 = (f32[32,32,1]{1,0,2:T(8,128)S(1)}, f32[32,32,1]{1,0,2:T(8,128)}, u32[]{:S(2)}) copy-start(f32[32,32,1]{1,0,2:T(8,128)} %constant.109) | copy-start | bytes 12292
  36.4 0.7 copy-start.8
  36.4 0.7 copy-start.9
  36.4 0.7 copy-start.10
  36.4 0.7 %copy-start.11 = (f32[16,48]{1,0:T(8,128)S(1)}, f32[16,48]{1,0:T(8,128)}, u32[]{:S(2)}) copy-start(f32[16,48]{1,0:T(8,128)} %constant.102) | copy-start | bytes 9220
  37.1 0.7 copy-start
  37.1 0.7 copy-start.1
  37.1 0.7 %copy-start.2 = (f32[768]{0:T(1024)S(1)}, f32[768]{0:T(1024)}, u32[]{:S(2)}) copy-start(f32[768]{0:T(1024)} %constant.104) | copy-start | bytes 9220
  37.1 0.7 %copy-start.3 = (f32[768]{0:T(1024)S(1)}, f32[768]{0:T(1024)}, u32[]{:S(2)}) copy-start(f32[768]{0:T(1024)} %constant.105) | copy-start | bytes 9220
  38.6 0.7 copy-start.5
  53.3 0.7 %copy-start.6 = (f32[32,32,1]{1,0,2:T(8,128)S(1)}, f32[32,32,1]{1,0,2:T(8,128)}, u32[]{:S(2)}) copy-start(f32[32,32,1]{1,0,2:T(8,128)} %constant.108) | copy-start | bytes 12292

commit v3 on v2

--- a/solution.py
+++ b/solution.py
@@ -4,6 +4,8 @@
 import jax.numpy as jnp
 import numpy as np
 from jax import lax
+from jax.experimental import pallas as pl
+from jax.experimental.pallas import tpu as pltpu
 from jax.sharding import PartitionSpec as P
 
 SWEEPS = 2
@@ -96,16 +98,43 @@
     return jnp.concatenate([main, extra], axis=2).transpose(1, 0, 2)
 
 
-def spatial(state, faces):
-    north, south, east, west, diagonal = faces
-    rows_padded = jnp.pad(state, ((0, 0), (1, 1), (0, 0)))
-    cols_padded = jnp.pad(state, ((0, 0), (0, 0), (1, 1)))
-    above = rows_padded[:, 2:]
-    below = rows_padded[:, :-2]
-    after = cols_padded[:, :, 2:]
-    before = cols_padded[:, :, :-2]
-    coupled = north * above + south * below + east * after + west * before
-    return diagonal * state - coupled - courant_rows * below - courant_cols * before
+def solve_kernel(spec_ref, north_ref, south_ref, east_ref, west_ref, diag_ref,
+                 inva_ref, invb_ref, invi_ref, reala_ref, realb_ref, imag_ref, out_ref):
+    rows, lanes = north_ref.shape
+
+    def spatial(x):
+        above = pltpu.roll(x, rows - 1, 0)
+        below = pltpu.roll(x, 1, 0)
+        after = pltpu.roll(x, lanes - 1, 1)
+        before = pltpu.roll(x, 1, 1)
+        coupled = (north_ref[...] * above + south_ref[...] * below
+                   + east_ref[...] * after + west_ref[...] * before)
+        return diag_ref[...] * x - coupled - courant_rows * below - courant_cols * before
+
+    first = True
+    for sweep in range(SWEEPS):
+        for weight in step_weights(DEGREE):
+            if first:
+                res_real = spec_ref[0]
+                res_imag = spec_ref[1]
+            else:
+                state_real = out_ref[0]
+                state_imag = out_ref[1]
+                image_real = (reala_ref[...] * state_real - imag_ref[...] * state_imag
+                              + spatial(state_real))
+                image_imag = (realb_ref[...] * state_imag + imag_ref[...] * state_real
+                              + spatial(state_imag))
+                res_real = spec_ref[0] - image_real
+                res_imag = spec_ref[1] - image_imag
+            corr_real = inva_ref[...] * res_real - invi_ref[...] * res_imag
+            corr_imag = invb_ref[...] * res_imag + invi_ref[...] * res_real
+            if first:
+                out_ref[0] = weight * corr_real
+                out_ref[1] = weight * corr_imag
+                first = False
+            else:
+                out_ref[0] = out_ref[0] + weight * corr_real
+                out_ref[1] = out_ref[1] + weight * corr_imag
 
 
 def solve_slots(spectrum, faces, shifts, inside):
@@ -117,22 +146,13 @@
     inv_a = jnp.where(inside, diag_a / mag_a, 0.0)
     inv_b = jnp.where(inside, diag_b / mag_b, 0.0)
     inv_imag = jnp.where(inside, -imag / mag_a, 0.0)
-    state = jnp.zeros_like(spectrum)
-    first = True
-    for sweep in range(SWEEPS):
-        for weight in step_weights(DEGREE):
-            if first:
-                residual = spectrum
-                first = False
-            else:
-                image = spatial(state, faces)
-                image_real = real_a * state[0] - imag * state[1] + image[0]
-                image_imag = real_b * state[1] + imag * state[0] + image[1]
-                residual = spectrum - jnp.stack([image_real, image_imag])
-            corr_real = inv_a * residual[0] - inv_imag * residual[1]
-            corr_imag = inv_b * residual[1] + inv_imag * residual[0]
-            state = state + weight * jnp.stack([corr_real, corr_imag])
-    return state
+    operands = (spectrum,) + tuple(faces) + (inv_a, inv_b, inv_imag) + tuple(
+        jnp.asarray(s) for s in shifts
+    )
+    return pl.pallas_call(
+        solve_kernel,
+        out_shape=jax.ShapeDtypeStruct(spectrum.shape, spectrum.dtype),
+    )(*operands)
 
 
 def body(right_side, kappa):

time: 71.7 us -> 64.2 us (0.90)
  other arithmetic: 19 us -> 4.42 us
  Pallas kernels: 0 us -> 6.45 us
  local copies, waits for them, and re-layouts: 6.84 us -> 13.2 us
  waiting for transfers between devices: 14.7 us -> 9.42 us
    sub x22 -> x0, other arithmetic: 8.84 us -> none  [the longest x7 4.25 us: spatial(): diagonal * state - coupled - courant_rows * below - courant_cols * before]
    pallas_call x0 -> x1, Pallas kernels: none -> 6.45 us  [solve_slots(): pl.pallas_call(solve_kernel, out_shape=jax.ShapeDtypeStruct(spectrum.shap...]
    add x15 -> x0, other arithmetic: 5.58 us -> none  [the longest x7 2.61 us: solve_slots(): image_real = real_a * state[0] - imag * state[1] + image[0]]
    all_to_all x1, waiting for transfers between devices: 13.7 us -> 8.49 us  [body(): gathered = lax.all_to_all(sent, 'tm', 0, 0, tiled=True)]
    another operation x5 -> x10, local copies, waits for them, and re-layouts: 0.14 us -> 3.68 us  [body(): jnp.tile(f, (1, half))]
    pallas_call x0 -> x1, local copies, waits for them, and re-layouts: none -> 1.29 us  [solve_slots(): pl.pallas_call(solve_kernel, out_shape=jax.ShapeDtypeStruct(spectrum.shap...]
    transpose x1 -> x0, other arithmetic: 1.05 us -> none  [body(): solved = solved.transpose(0, 2, 1, 3).reshape(total, rows, span)]
    reshape x0 -> x1, local copies, waits for them, and re-layouts: none -> 1.04 us  [body(): spectrum = spectrum.reshape(2, extended, half * width)]
  transfers between devices with their start and end apart: 3 -> 3, of which waited for: 2 -> 2; matrix products, arithmetic and copies ran while one was open for 1% -> 9% of each run, Pallas kernels for 0% -> 0%
where the time goes in v3:
time: 64.2 us; the launch traced here: 63.3 us
  starting transfers between devices  15.4 us (24%)
  local copies, waits for them, and re-layouts  13.2 us (21%)
  blocking collectives  12.6 us (20%)
  waiting for transfers between devices  9.42 us (15%)
  Pallas kernels  6.45 us (10%)
  other arithmetic  4.42 us (7%)
  matrix products  1.52 us (2%)
    all_to_all x1, blocking collectives, body(): returned = lax.all_to_all(signal, 'tm', 0, 0, tiled=True)  12.6 us
    all_to_all x1, starting transfers between devices, body(): gathered = lax.all_to_all(sent, 'tm', 0, 0, tiled=True)  8.71 us
    all_to_all x1, waiting for transfers between devices, body(): gathered = lax.all_to_all(sent, 'tm', 0, 0, tiled=True)  8.49 us
    pallas_call x1, Pallas kernels, solve_slots(): pl.pallas_call(solve_kernel, out_shape=jax.ShapeDtypeStruct(spectrum.shap...  6.45 us
    ppermute x1, starting transfers between devices, with_halo(): low = lax.ppermute(joined[:, rows - width:], 'row', forward)  4.76 us
    another operation x10, local copies, waits for them, and re-layouts, body(): jnp.tile(f, (1, half))  3.68 us
    unnamed x20, local copies, waits for them, and re-layouts  2.87 us
    ppermute x1, starting transfers between devices, with_halo(): high = lax.ppermute(joined[:, :width], 'row', backward)  1.92 us
  transfers between devices with their start and end apart: 3, of which 2 were waited for; matrix products, arithmetic and copies ran while one was open for 9% of the time, Pallas kernels for 0%

profile of v3, /device:TPU:97, one launch (start us, length us, event | category | flops | bytes accessed | tf_op | source)
XLA Modules:
  0.0 63.3 jit_solution(7468293379584987259)
XLA Ops:
  0.0 0.0 copy-start.1
  0.0 1.2 %copy.33 = f32[64,1024]{0,1:T(8,128)S(1)} copy(f32[64,1024]{1,0:T(8,128)} %param.11) | data formatting | bytes 524288 | tf_op args[1]
  1.2 0.0 copy-done.1
  1.2 0.2 copy.34
  1.4 0.4 slice_maximum_fusion
  1.8 0.3 copy.36
  2.1 1.9 %collective-permute-start.1 = (f32[2,8,1024]{2,1,0:T(8,128)S(1)}, f32[2,8,1024]{2,1,0:T(8,128)S(1)}, u32[]{:S(2)}, u32[]{:S(2)}) collective-permute-start(f32[2,8,1024]{2,1,0:T(8,128)S(1)} %copy.36), channel_id=1, source_target_pairs={{1,0},{2,1},{3,2},{4,3},{5,4},{6,5},{7,6},{9,8},{10,9},{11,10},{12... | collective-permute-start | bytes 196616 | tf_op jit(solution)/shard_map/ppermute | solution.py:37
  4.0 0.3 copy.35
  4.3 4.8 %collective-permute-start = (f32[2,8,1024]{2,1,0:T(8,128)S(1)}, f32[2,8,1024]{2,1,0:T(8,128)S(1)}, u32[]{:S(2)}, u32[]{:S(2)}) collective-permute-start(f32[2,8,1024]{2,1,0:T(8,128)S(1)} %copy.35), channel_id=1, source_target_pairs={{0,1},{1,2},{2,3},{3,4},{4,5},{5,6},{6,7},{8,9},{9,10},{10,11},{11... | collective-permute-start | bytes 196616 | tf_op jit(solution)/shard_map/ppermute | solution.py:36
  9.1 0.0 collective-permute-done.1
  9.1 0.3 copy.38
  9.4 0.9 %collective-permute-done = f32[2,8,1024]{2,1,0:T(8,128)S(1)} collective-permute-done((f32[2,8,1024]{2,1,0:T(8,128)S(1)}, f32[2,8,1024]{2,1,0:T(8,128)S(1)}, u32[]{:S(2)}, u32[]{:S(2)}) %collective-permute-start) | collective-permute-done | bytes 65568 | tf_op jit(solution)/shard_map/ppermute | solution.py:36
  10.4 0.3 copy.37
  10.7 0.6 pad_maximum_fusion.1
  11.3 0.1 slice_bitcast_fusion.1
  11.4 0.1 pad_slice_fusion.1
  11.5 1.0 %maximum_bitcast_fusion = f32[32,80,48]{1,2,0:T(8,128)} fusion(f32[80,32,16]{0,2,1:T(8,128)S(1)} %slice.55, f32[80,32,32]{0,2,1:T(8,128)S(1)} %bitcast.40), kind=kLoop, calls=%fused_computation.3 | loop fusion | flops 122880 | bytes 983040 | tf_op jit(solution)/shard_map/transpose | solution.py:98
  12.5 8.7 %all-to-all-start = ((f32[32,80,48]{1,2,0:T(8,128)}), f32[32,80,48]{1,2,0:T(8,128)S(1)}, u32[]{:S(2)}, u32[]{:S(2)}) async-start(f32[32,80,48]{1,2,0:T(8,128)} %maximum_bitcast_fusion), calls=%async_computation | async-start | bytes 1572864 | tf_op jit(solution)/shard_map/all_to_all | solution.py:173
  21.2 0.1 broadcast_and_fusion
  21.3 0.2 copy.42
  21.5 0.2 add_add_fusion
  21.7 0.8 %copy.47.north_ref = f32[80,768]{1,0:T(8,128)} copy(f32[80,768]{0,1:T(8,128)S(1)} %bitcast.44) | data formatting | bytes 491520 | tf_op jit(solution)/shard_map/tile | solution.py:182
  22.6 0.9 %copy.48.south_ref = f32[80,768]{1,0:T(8,128)} copy(f32[80,768]{0,1:T(8,128)S(1)} %bitcast.45) | data formatting | bytes 491520 | tf_op jit(solution)/shard_map/tile | solution.py:182
  23.4 0.8 %copy.49.east_ref = f32[80,768]{1,0:T(8,128)} copy(f32[80,768]{0,1:T(8,128)S(1)} %bitcast.46) | data formatting | bytes 491520 | tf_op jit(solution)/shard_map/tile | solution.py:182
  24.3 0.8 %copy.50.west_ref = f32[80,768]{1,0:T(8,128)} copy(f32[80,768]{0,1:T(8,128)S(1)} %bitcast.47) | data formatting | bytes 491520 | tf_op jit(solution)/shard_map/tile | solution.py:182
  25.2 0.0 copy-start.4
  25.2 0.0 copy-start.5
  25.2 0.0 copy-start.6
  25.2 0.0 copy-start.7
  25.2 0.1 copy.51.diag_ref
  25.4 0.5 copy-done.4
  25.9 0.0 copy-done.5
  25.9 0.0 copy-done.6
  25.9 0.0 copy-done.7
  25.9 0.0 copy-start
  25.9 0.0 copy-start.3
  25.9 1.0 %divide_select_fusion = (f32[80,768]{1,0:T(8,128)}, f32[80,768]{1,0:T(8,128)}, f32[80,768]{1,0:T(8,128)}) fusion(pred[80,768]{1,0:T(8,128)(4,1)S(1)} %copy.42, f32[80,768]{1,0:T(8,128)S(1)} %copy.51.diag_ref, f32[768]{0:T(1024)S(1)} %copy-done.4, f32[768]{0:T(1024)S(1)} %copy-done.5, f32[768]{0:T(1024)S(1)} %copy-done.6, f32[768]{0:T(1024)S(1)} %copy-done.7), kind=kLoop, calls=%fused_computation.16 | loop fusion | flops 737280 | bytes 1056768 | tf_op jit(solution)/shard_map/jit(_where)/select_n | solution.py:148
  26.9 0.0 copy-done
  26.9 8.5 %all-to-all-done = f32[32,80,48]{1,2,0:T(8,128)S(1)} async-done(((f32[32,80,48]{1,2,0:T(8,128)}), f32[32,80,48]{1,2,0:T(8,128)S(1)}, u32[]{:S(2)}, u32[]{:S(2)}) %all-to-all-start) | async-done | bytes 491552 | tf_op jit(solution)/shard_map/all_to_all | solution.py:173
  35.4 0.0 copy-done.3
  35.4 0.9 %fusion = f32[32,80,48]{1,0,2:T(8,128)S(1)} fusion(f32[32,32,1]{1,0,2:T(8,128)S(1)} %copy-done.3, f32[32,80,48]{1,2,0:T(8,128)S(1)} %all-to-all-done), kind=kOutput, calls=%fused_computation.4 | convolution fusion | flops 47185920 | bytes 987136 | tf_op jit(solution)/shard_map/pt,trc->prc/dot_general | solution.py:174
  36.4 0.5 copy.40
  36.8 1.0 %copy.46.spec_ref = f32[2,80,768]{2,1,0:T(8,128)} copy(f32[2,80,768]{1,2,0:T(8,128)S(1)} %bitcast.38) | data formatting | bytes 983040 | tf_op jit(solution)/shard_map/reshape | solution.py:176
  37.9 6.4 %shard_map.100 = f32[2,80,768]{2,1,0:T(8,128)} custom-call(f32[2,80,768]{2,1,0:T(8,128)} %copy.46.spec_ref, f32[80,768]{1,0:T(8,128)} %copy.47.north_ref, f32[80,768]{1,0:T(8,128)} %copy.48.south_ref, f32[80,768]{1,0:T(8,128)} %copy.49.east_ref, f32[80,768]{1,0:T(8,128)} %copy.50.west_ref, f32[80,768]{1,0:T(8,128)} %copy-done, ...), custom_call_target="tpu_custom_call" | custom-call | tf_op jit(solution)/shard_map/pallas_call | solution.py:152
  44.3 1.3 %copy.52 = f32[2,80,768]{1,2,0:T(8,128)S(1)} copy(f32[2,80,768]{2,1,0:T(8,128)} %shard_map.100) | data formatting | bytes 983040 | tf_op jit(solution)/shard_map/pallas_call | solution.py:152
  45.6 0.2 slice_bitcast_fusion
  45.8 0.0 copy-start.2
  45.8 0.3 copy.53
  46.1 0.4 copy-done.2
  46.5 0.6 fusion.14
  47.1 0.3 copy.59
  47.4 0.3 reshape.93
  47.8 12.6 %all_to_all.10 = f32[32,1,2048]{2,1,0:T(1,128)S(1)} all-to-all(f32[32,1,2048]{2,1,0:T(1,128)S(1)} %reshape.93), channel_id=1, replica_groups=mesh['tm'=32,'row'=8] {'tm'}, dimensions={0} | all-to-all | bytes 524288 | tf_op jit(solution)/shard_map/all_to_all | solution.py:189
  60.4 0.5 broadcast.77
  60.9 1.3 %reduce = f32[32,2048]{1,0:T(8,128)S(1)} reduce(f32[32,1,2048]{2,1,0:T(1,128)S(1)} %all_to_all.10, f32[]{:T(128)} %broadcast.77), dimensions={1}, to_apply=%all_to_all.7.reduce_sub_computation | reduce | bytes 524292 | tf_op jit(solution)/shard_map/all_to_all | solution.py:189
  62.2 0.2 reshape.94
  62.4 0.9 %copy.55 = f32[1,64,1024]{2,1,0:T(8,128)} copy(f32[1,64,1024]{1,2,0:T(8,128)S(1)} %bitcast.41) | data formatting | bytes 524288 | tf_op jit(solution)/shard_map/reshape | solution.py:190
  (9 shorter events, 0.2 us)
Async XLA Ops:
  0.0 1.2 %copy-start.1 = (f32[1,64,1024]{2,1,0:T(8,128)S(1)}, f32[1,64,1024]{2,1,0:T(8,128)}, u32[]{:S(2)}) copy-start(f32[1,64,1024]{2,1,0:T(8,128)} %param.10) | copy-start | bytes 786436
  2.1 7.0 %collective-permute-start.1 = (f32[2,8,1024]{2,1,0:T(8,128)S(1)}, f32[2,8,1024]{2,1,0:T(8,128)S(1)}, u32[]{:S(2)}, u32[]{:S(2)}) collective-permute-start(f32[2,8,1024]{2,1,0:T(8,128)S(1)} %copy.36), channel_id=1, source_target_pairs={{1,0},{2,1},{3,2},{4,3},{5,4},{6,5},{7,6},{9,8},{10,9},{11,10},{12... | collective-permute-start | bytes 196616 | tf_op jit(solution)/shard_map/ppermute | solution.py:37
  4.3 6.1 %collective-permute-start = (f32[2,8,1024]{2,1,0:T(8,128)S(1)}, f32[2,8,1024]{2,1,0:T(8,128)S(1)}, u32[]{:S(2)}, u32[]{:S(2)}) collective-permute-start(f32[2,8,1024]{2,1,0:T(8,128)S(1)} %copy.35), channel_id=1, source_target_pairs={{0,1},{1,2},{2,3},{3,4},{4,5},{5,6},{6,7},{8,9},{9,10},{10,11},{11... | collective-permute-start | bytes 196616 | tf_op jit(solution)/shard_map/ppermute | solution.py:36
  12.5 22.9 %all-to-all-start = ((f32[32,80,48]{1,2,0:T(8,128)}), f32[32,80,48]{1,2,0:T(8,128)S(1)}, u32[]{:S(2)}, u32[]{:S(2)}) async-start(f32[32,80,48]{1,2,0:T(8,128)} %maximum_bitcast_fusion), calls=%async_computation | async-start | bytes 1572864 | tf_op jit(solution)/shard_map/all_to_all | solution.py:173
  25.2 0.7 %copy-start.4 = (f32[768]{0:T(1024)S(1)}, f32[768]{0:T(1024)}, u32[]{:S(2)}) copy-start(f32[768]{0:T(1024)} %constant.63) | copy-start | bytes 9220
  25.2 0.7 %copy-start.5 = (f32[768]{0:T(1024)S(1)}, f32[768]{0:T(1024)}, u32[]{:S(2)}) copy-start(f32[768]{0:T(1024)} %constant.61) | copy-start | bytes 9220
  25.2 0.7 %copy-start.6 = (f32[768]{0:T(1024)S(1)}, f32[768]{0:T(1024)}, u32[]{:S(2)}) copy-start(f32[768]{0:T(1024)} %constant.60) | copy-start | bytes 9220
  25.2 0.7 %copy-start.7 = (f32[768]{0:T(1024)S(1)}, f32[768]{0:T(1024)}, u32[]{:S(2)}) copy-start(f32[768]{0:T(1024)} %constant.62) | copy-start | bytes 9220
  25.9 1.0 %copy-start = (f32[80,768]{1,0:T(8,128)}, f32[80,768]{1,0:T(8,128)S(1)}, u32[]{:S(2)}) copy-start(f32[80,768]{1,0:T(8,128)S(1)} %copy.51.diag_ref) | copy-start | bytes 737284
  25.9 9.5 %copy-start.3 = (f32[32,32,1]{1,0,2:T(8,128)S(1)}, f32[32,32,1]{1,0,2:T(8,128)}, u32[]{:S(2)}) copy-start(f32[32,32,1]{1,0,2:T(8,128)} %constant.65) | copy-start | bytes 12292
  45.8 0.7 %copy-start.2 = (f32[32,32,1]{1,0,2:T(8,128)S(1)}, f32[32,32,1]{1,0,2:T(8,128)}, u32[]{:S(2)}) copy-start(f32[32,32,1]{1,0,2:T(8,128)} %constant.64) | copy-start | bytes 12292

commit v4 on v3

--- a/solution.py
+++ b/solution.py
@@ -27,18 +27,34 @@
     ]
 
 
-def with_halo(right_side, kappa, width):
-    rows = kappa.shape[0]
+def row_pairs():
     count = lax.axis_size("row")
     forward = [(i, i + 1) for i in range(count - 1)]
     backward = [(target, source) for source, target in forward]
-    joined = jnp.concatenate([right_side, kappa[None]], axis=0)
-    low = lax.ppermute(joined[:, rows - width :], "row", forward)
-    high = lax.ppermute(joined[:, :width], "row", backward)
-    joined = jnp.concatenate([low, joined, high], axis=1)
+    return forward, backward
+
+
+def with_halo(kappa, width):
+    rows = kappa.shape[0]
+    count = lax.axis_size("row")
+    forward, backward = row_pairs()
+    low = lax.ppermute(kappa[rows - width :], "row", forward)
+    high = lax.ppermute(kappa[:width], "row", backward)
     place = lax.axis_index("row") * rows - width + jnp.arange(rows + 2 * width)
     inside = (place >= 0) & (place < rows * count)
-    return joined[0], joined[1], inside
+    return jnp.concatenate([low, kappa, high], axis=0), inside
+
+
+def add_spill(solved, width):
+    rows = solved.shape[1] - 2 * width
+    forward, backward = row_pairs()
+    from_low = lax.ppermute(solved[:, rows + width :], "row", forward)
+    from_high = lax.ppermute(solved[:, :width], "row", backward)
+    own = solved[:, width : rows + width]
+    spill = jnp.concatenate(
+        [from_low, jnp.zeros_like(own[:, : rows - 2 * width]), from_high], axis=1
+    )
+    return own + spill
 
 
 def transform_matrices(total):
@@ -164,16 +180,17 @@
     span = cols // tiles
     width = span + 2 * margin
     tile = lax.axis_index("tm")
-    highest = lax.Precision.HIGHEST
+    precision = lax.Precision.HIGH
     forward, inverse = transform_matrices(total)
 
-    wide_side, kappa_rows, inside_rows = with_halo(right_side, kappa, margin)
+    kappa_rows, inside_rows = with_halo(kappa, margin)
     extended = rows + 2 * margin
-    sent = column_tiles(wide_side, tiles, width, margin)
+    sent = column_tiles(right_side[0], tiles, width, margin)
     gathered = lax.all_to_all(sent, "tm", 0, 0, tiled=True)
-    spectrum = jnp.einsum("pt,trc->prc", forward, gathered, precision=highest)
-    spectrum = spectrum.reshape(2, half, extended, width).transpose(0, 2, 1, 3)
-    spectrum = spectrum.reshape(2, extended, half * width)
+    spectrum = jnp.einsum("pt,trc->prc", forward, gathered, precision=precision)
+    spectrum = spectrum.reshape(2, half, rows, width).transpose(0, 2, 1, 3)
+    spectrum = spectrum.reshape(2, rows, half * width)
+    spectrum = jnp.pad(spectrum, ((0, 0), (margin, margin), (0, 0)))
 
     place = tile * span - margin + jnp.arange(width)
     inside_cols = (place >= 0) & (place < cols)
@@ -181,13 +198,14 @@
     inside = jnp.tile(inside, (1, half))
     faces = tuple(jnp.tile(f, (1, half)) for f in tile_faces(kappa_rows, tile, tiles, width, margin))
     shifts = slot_shifts(half, total, width)
-    solved = solve_slots(spectrum, faces, shifts, inside)
-
-    solved = solved.reshape(2, extended, half, width)[:, margin : margin + rows, :, margin : margin + span]
-    solved = solved.transpose(0, 2, 1, 3).reshape(total, rows, span)
-    signal = jnp.einsum("tp,prc->trc", inverse, solved, precision=highest)
+    solved = add_spill(solve_slots(spectrum, faces, shifts, inside), margin)
+
+    solved = solved.reshape(2, rows, half, width)[..., margin : margin + span]
+    solved = solved.transpose(0, 2, 1, 3).reshape(total, rows * span)
+    signal = jnp.dot(inverse, solved, precision=precision)
     returned = lax.all_to_all(signal, "tm", 0, 0, tiled=True)
-    return returned.transpose(1, 0, 2).reshape(steps_dev, rows, cols)
+    returned = returned.reshape(tiles, rows, span).transpose(1, 0, 2)
+    return returned.reshape(steps_dev, rows, cols)
 
 
 def solution(mesh):

time: 64.2 us -> 80.6 us (1.26)
  starting transfers between devices: 15.4 us -> 22 us
  blocking collectives: 12.6 us -> 17.8 us
  local copies, waits for them, and re-layouts: 13.2 us -> 15.5 us
  other arithmetic: 4.42 us -> 6.01 us
  waiting for transfers between devices: 9.42 us -> 10.6 us
    ppermute x2 -> x4, waiting for transfers between devices: 0.93 us -> 10.6 us  [the longest x1 8.65 us: with_halo(): high = lax.ppermute(kappa[:width], 'row', backward)]
    all_to_all x1, waiting for transfers between devices: 8.49 us -> 0.01 us  [body(): gathered = lax.all_to_all(sent, 'tm', 0, 0, tiled=True)]
    ppermute x2 -> x4, starting transfers between devices: 6.68 us -> 14.1 us  [the longest x1 5.5 us: add_spill(): from_low = lax.ppermute(solved[:, rows + width:], 'row', forward)]
    all_to_all x1, blocking collectives: 12.6 us -> 17.8 us  [body(): returned = lax.all_to_all(signal, 'tm', 0, 0, tiled=True)]
    all_to_all x0 -> x1, other arithmetic: none -> 1.55 us  [body(): gathered = lax.all_to_all(sent, 'tm', 0, 0, tiled=True)]
    pallas_call x1 -> x0, local copies, waits for them, and re-layouts: 1.29 us -> none  [solve_slots(): pl.pallas_call(solve_kernel, out_shape=jax.ShapeDtypeStruct(spectrum.shap...]
    unnamed x20, local copies, waits for them, and re-layouts: 2.87 us -> 4.07 us
    reshape x3 -> x6, local copies, waits for them, and re-layouts: 2.4 us -> 3.49 us  [the longest x1 0.9 us: body(): return returned.reshape(steps_dev, rows, cols)]
  transfers between devices with their start and end apart: 3 -> 5, of which waited for: 2 -> 3; matrix products, arithmetic and copies ran while one was open for 9% -> 9% of each run, Pallas kernels for 0% -> 0%
where the time goes in v4:
time: 80.6 us; the launch traced here: 79.5 us
  starting transfers between devices  22 us (27%)
  blocking collectives  17.8 us (22%)
  local copies, waits for them, and re-layouts  15.5 us (19%)
  waiting for transfers between devices  10.6 us (13%)
  Pallas kernels  6.45 us (8%)
  other arithmetic  6.01 us (7%)
  matrix products  0.87 us (1%)
    all_to_all x1, blocking collectives, body(): returned = lax.all_to_all(signal, 'tm', 0, 0, tiled=True)  17.8 us
    ppermute x1, waiting for transfers between devices, with_halo(): high = lax.ppermute(kappa[:width], 'row', backward)  8.65 us
    all_to_all x1, starting transfers between devices, body(): gathered = lax.all_to_all(sent, 'tm', 0, 0, tiled=True)  7.89 us
    pallas_call x1, Pallas kernels, solve_slots(): pl.pallas_call(solve_kernel, out_shape=jax.ShapeDtypeStruct(spectrum.shap...  6.45 us
    ppermute x1, starting transfers between devices, add_spill(): from_low = lax.ppermute(solved[:, rows + width:], 'row', forward)  5.5 us
    ppermute x1, starting transfers between devices, with_halo(): low = lax.ppermute(kappa[rows - width:], 'row', forward)  4.76 us
    unnamed x20, local copies, waits for them, and re-layouts  4.07 us
    another operation x10, local copies, waits for them, and re-layouts, body(): jnp.tile(f, (1, half))  3.68 us
  transfers between devices with their start and end apart: 5, of which 3 were waited for; matrix products, arithmetic and copies ran while one was open for 9% of the time, Pallas kernels for 0%

profile of v4, /device:TPU:97, one launch (start us, length us, event | category | flops | bytes accessed | tf_op | source)
XLA Modules:
  0.0 79.5 jit_solution(9116858785097225288)
XLA Ops:
  0.0 1.1 %copy.57 = f32[1,64,1024]{1,2,0:T(8,128)S(1)} copy(f32[1,64,1024]{2,1,0:T(8,128)} %param.10) | data formatting | bytes 524288 | tf_op args[0]
  1.2 0.1 pad_slice_fusion.1
  1.3 0.1 fusion.22
  1.3 1.2 %reshape.100 = f32[32,1,3072]{2,1,0:T(1,128)} reshape(f32[32,48,64]{2,1,0:T(8,128)S(1)} %fusion.22) | data formatting | bytes 786432
  2.6 7.9 %all-to-all-start = ((f32[32,1,3072]{2,1,0:T(1,128)}), f32[32,1,3072]{2,1,0:T(1,128)S(1)}, u32[]{:S(2)}, u32[]{:S(2)}) async-start(f32[32,1,3072]{2,1,0:T(1,128)} %reshape.100), calls=%async_computation | async-start | bytes 786432 | tf_op jit(solution)/shard_map/all_to_all | solution.py:189
  10.4 0.0 copy-done.1
  10.5 0.2 copy.61
  10.7 1.9 %collective-permute-start.1 = (f32[8,1024]{0,1:T(8,128)S(1)}, f32[8,1024]{0,1:T(8,128)S(1)}, u32[]{:S(2)}, u32[]{:S(2)}) collective-permute-start(f32[8,1024]{0,1:T(8,128)S(1)} %copy.61), channel_id=1, source_target_pairs={{1,0},{2,1},{3,2},{4,3},{5,4},{6,5},{7,6},{9,8},{10,9},{11,10},{12... | collective-permute-start | bytes 98312 | tf_op jit(solution)/shard_map/ppermute | solution.py:42
  12.6 0.2 copy.60
  12.8 4.8 %collective-permute-start = (f32[8,1024]{0,1:T(8,128)S(1)}, f32[8,1024]{0,1:T(8,128)S(1)}, u32[]{:S(2)}, u32[]{:S(2)}) collective-permute-start(f32[8,1024]{0,1:T(8,128)S(1)} %copy.60), channel_id=1, source_target_pairs={{0,1},{1,2},{2,3},{3,4},{4,5},{5,6},{6,7},{8,9},{9,10},{10,11},{11... | collective-permute-start | bytes 98312 | tf_op jit(solution)/shard_map/ppermute | solution.py:41
  17.6 0.7 iota_compare_fusion
  18.3 0.1 broadcast_and_fusion
  18.4 0.2 copy.62
  18.6 0.2 copy.64
  18.8 8.6 %collective-permute-done.1 = f32[8,1024]{0,1:T(8,128)S(1)} collective-permute-done((f32[8,1024]{0,1:T(8,128)S(1)}, f32[8,1024]{0,1:T(8,128)S(1)}, u32[]{:S(2)}, u32[]{:S(2)}) %collective-permute-start.1) | collective-permute-done | bytes 32800 | tf_op jit(solution)/shard_map/ppermute | solution.py:42
  27.5 1.1 %collective-permute-done = f32[8,1024]{0,1:T(8,128)S(1)} collective-permute-done((f32[8,1024]{0,1:T(8,128)S(1)}, f32[8,1024]{0,1:T(8,128)S(1)}, u32[]{:S(2)}, u32[]{:S(2)}) %collective-permute-start) | collective-permute-done | bytes 32800 | tf_op jit(solution)/shard_map/ppermute | solution.py:41
  28.5 0.8 %select_maximum_fusion = f32[82,50]{0,1:T(8,128)S(1)} fusion(s32[]{:T(128)S(6)} %select_n.13, f32[8,1024]{0,1:T(8,128)S(1)} %collective-permute-done.1, f32[64,1024]{0,1:T(8,128)S(1)} %copy.62, f32[8,1024]{0,1:T(8,128)S(1)} %collective-permute-done, pred[82,1042]{0,1:T(8,128)(4,1)S(1)} %get-tuple-element.19, pred[82,1042]{0,1:T(8,128)(4,1)} %get-tuple-element.20), kind=kLoop, calls=%fused_computation.29 | loop fusion | flops 77900 | bytes 353304 | tf_op jit(solution)/shard_map/concatenate | solution.py:45
  29.3 0.1 add_add_fusion
  29.5 0.8 %copy.68.north_ref = f32[80,768]{1,0:T(8,128)} copy(f32[80,768]{0,1:T(8,128)S(1)} %bitcast.39) | data formatting | bytes 491520 | tf_op jit(solution)/shard_map/tile | solution.py:199
  30.3 0.9 %copy.69.south_ref = f32[80,768]{1,0:T(8,128)} copy(f32[80,768]{0,1:T(8,128)S(1)} %bitcast.40) | data formatting | bytes 491520 | tf_op jit(solution)/shard_map/tile | solution.py:199
  31.2 0.8 %copy.70.east_ref = f32[80,768]{1,0:T(8,128)} copy(f32[80,768]{0,1:T(8,128)S(1)} %bitcast.41) | data formatting | bytes 491520 | tf_op jit(solution)/shard_map/tile | solution.py:199
  32.1 0.8 %copy.71.west_ref = f32[80,768]{1,0:T(8,128)} copy(f32[80,768]{0,1:T(8,128)S(1)} %bitcast.42) | data formatting | bytes 491520 | tf_op jit(solution)/shard_map/tile | solution.py:199
  33.0 0.0 copy-start.4
  33.0 0.0 copy-start.5
  33.0 0.0 copy-start.6
  33.0 0.0 copy-start.7
  33.0 0.1 copy.72.diag_ref
  33.2 0.5 copy-done.4
  33.7 0.0 copy-done.5
  33.7 0.0 copy-done.6
  33.7 0.0 copy-done.7
  33.8 1.0 %divide_select_fusion = (f32[80,768]{1,0:T(8,128)}, f32[80,768]{1,0:T(8,128)}, f32[80,768]{1,0:T(8,128)}) fusion(pred[80,768]{1,0:T(8,128)(4,1)S(1)} %copy.64, f32[80,768]{1,0:T(8,128)S(1)} %copy.72.diag_ref, f32[768]{0:T(1024)S(1)} %copy-done.4, f32[768]{0:T(1024)S(1)} %copy-done.5, f32[768]{0:T(1024)S(1)} %copy-done.6, f32[768]{0:T(1024)S(1)} %copy-done.7), kind=kLoop, calls=%fused_computation.13 | loop fusion | flops 737280 | bytes 1056768 | tf_op jit(solution)/shard_map/jit(_where)/select_n | solution.py:164
  34.7 0.0 copy-done
  34.7 0.0 all-to-all-done
  34.7 0.5 broadcast.125
  35.3 1.6 %reduce.1 = f32[32,3072]{1,0:T(8,128)S(1)} reduce(f32[32,1,3072]{2,1,0:T(1,128)S(1)} %all-to-all-done, f32[]{:T(128)} %broadcast.125), dimensions={1}, to_apply=%all_to_all.9.reduce_sub_computation | reduce | bytes 786436 | tf_op jit(solution)/shard_map/all_to_all | solution.py:189
  36.8 0.0 copy-start.2
  36.9 0.2 reshape.101
  37.1 0.5 copy-done.2
  37.6 0.6 fusion
  38.2 0.8 copy.59
  39.0 0.5 reshape.93
  39.4 0.8 %pad.13.spec_ref = f32[2,80,768]{2,1,0:T(8,128)} pad(f32[2,64,768]{2,1,0:T(8,128)S(1)} %reshape.93, f32[]{:T(128)} %constant.20.clone.1), padding=0_0x8_8x0_0 | pad | bytes 884740 | tf_op jit(solution)/shard_map/jit(_pad)/pad | solution.py:193
  40.3 6.4 %shard_map.100 = f32[2,80,768]{2,1,0:T(8,128)} custom-call(f32[2,80,768]{2,1,0:T(8,128)} %pad.13.spec_ref, f32[80,768]{1,0:T(8,128)} %copy.68.north_ref, f32[80,768]{1,0:T(8,128)} %copy.69.south_ref, f32[80,768]{1,0:T(8,128)} %copy.70.east_ref, f32[80,768]{1,0:T(8,128)} %copy.71.west_ref, f32[80,768]{1,0:T(8,128)} %copy-done, ...), custom_call_target="tpu_custom_call" | custom-call | tf_op jit(solution)/shard_map/pallas_call | solution.py:168
  46.7 0.8 %fusion.20 = (f32[2,8,768]{2,1,0:T(8,128)S(1)}, f32[2,8,768]{2,1,0:T(8,128)S(1)}) fusion(f32[2,80,768]{2,1,0:T(8,128)} %shard_map.100), kind=kLoop, calls=%fused_computation.45 | loop fusion | bytes 196608 | tf_op jit(solution)/shard_map/slice | solution.py:51
  47.5 1.9 %collective-permute-start.3 = (f32[2,8,768]{2,1,0:T(8,128)S(1)}, f32[2,8,768]{2,1,0:T(8,128)S(1)}, u32[]{:S(2)}, u32[]{:S(2)}) collective-permute-start(f32[2,8,768]{2,1,0:T(8,128)S(1)} %get-tuple-element.13), channel_id=1, source_target_pairs={{1,0},{2,1},{3,2},{4,3},{5,4},{6,5},{7,6},{9,8},{10,9},{11,10},{12... | collective-permute-start | bytes 147464 | tf_op jit(solution)/shard_map/ppermute | solution.py:52
  49.5 5.5 %collective-permute-start.2 = (f32[2,8,768]{2,1,0:T(8,128)S(1)}, f32[2,8,768]{2,1,0:T(8,128)S(1)}, u32[]{:S(2)}, u32[]{:S(2)}) collective-permute-start(f32[2,8,768]{2,1,0:T(8,128)S(1)} %get-tuple-element.12), channel_id=1, source_target_pairs={{0,1},{1,2},{2,3},{3,4},{4,5},{5,6},{6,7},{8,9},{9,10},{10,11},{11... | collective-permute-start | bytes 147464 | tf_op jit(solution)/shard_map/ppermute | solution.py:51
  55.0 0.1 pad.16.clone
  55.1 0.0 collective-permute-done.3
  55.1 0.9 %collective-permute-done.2 = f32[2,8,768]{2,1,0:T(8,128)S(1)} collective-permute-done((f32[2,8,768]{2,1,0:T(8,128)S(1)}, f32[2,8,768]{2,1,0:T(8,128)S(1)}, u32[]{:S(2)}, u32[]{:S(2)}) %collective-permute-start.2) | collective-permute-done | bytes 49184 | tf_op jit(solution)/shard_map/ppermute | solution.py:51
  55.9 1.1 %slice_add_fusion = f32[2,64,768]{2,1,0:T(8,128)S(1)} fusion(f32[2,80,768]{2,1,0:T(8,128)} %shard_map.100, f32[2,8,768]{2,1,0:T(8,128)S(1)} %collective-permute-done.3, f32[2,8,768]{2,1,0:T(8,128)S(1)} %collective-permute-done.2, f32[64]{0:T(128)S(1)} %pad.16.clone), kind=kLoop, calls=%fused_computation.12 | loop fusion | flops 294912 | bytes 884992 | tf_op jit(solution)/shard_map/add | solution.py:57
  57.0 0.5 reshape.94
  57.6 0.3 slice_bitcast_fusion
  57.9 0.3 copy.73
  58.2 0.0 copy-start.3
  58.3 0.5 reshape.95
  58.7 0.2 copy-done.3
  59.0 0.2 convolution_bitcast_fusion
  59.2 0.3 copy.74
  59.5 17.8 %all_to_all.14 = f32[32,1,2048]{2,1,0:T(1,128)S(1)} all-to-all(f32[32,1,2048]{2,1,0:T(1,128)S(1)} %copy.74), channel_id=1, replica_groups=mesh['tm'=32,'row'=8] {'tm'}, dimensions={0} | all-to-all | bytes 524288 | tf_op jit(solution)/shard_map/all_to_all | solution.py:206
  77.3 0.6 reduce
  77.9 0.3 reshape.96
  78.3 0.3 copy.75
  78.6 0.9 %copy.76 = f32[1,64,1024]{2,1,0:T(8,128)} copy(f32[1,64,1024]{1,2,0:T(8,128)S(1)} %bitcast.38) | data formatting | bytes 524288 | tf_op jit(solution)/shard_map/reshape | solution.py:208
  (13 shorter events, 0.2 us)
Async XLA Ops:
  2.6 7.9 %copy-start.1 = (f32[64,1024]{1,0:T(8,128)S(1)}, f32[64,1024]{1,0:T(8,128)}, u32[]{:S(2)}) copy-start(f32[64,1024]{1,0:T(8,128)} %param.11) | copy-start | bytes 786436
  2.6 32.2 %all-to-all-start = ((f32[32,1,3072]{2,1,0:T(1,128)}), f32[32,1,3072]{2,1,0:T(1,128)S(1)}, u32[]{:S(2)}, u32[]{:S(2)}) async-start(f32[32,1,3072]{2,1,0:T(1,128)} %reshape.100), calls=%async_computation | async-start | bytes 786432 | tf_op jit(solution)/shard_map/all_to_all | solution.py:189
  10.7 16.8 %collective-permute-start.1 = (f32[8,1024]{0,1:T(8,128)S(1)}, f32[8,1024]{0,1:T(8,128)S(1)}, u32[]{:S(2)}, u32[]{:S(2)}) collective-permute-start(f32[8,1024]{0,1:T(8,128)S(1)} %copy.61), channel_id=1, source_target_pairs={{1,0},{2,1},{3,2},{4,3},{5,4},{6,5},{7,6},{9,8},{10,9},{11,10},{12... | collective-permute-start | bytes 98312 | tf_op jit(solution)/shard_map/ppermute | solution.py:42
  12.8 15.7 %collective-permute-start = (f32[8,1024]{0,1:T(8,128)S(1)}, f32[8,1024]{0,1:T(8,128)S(1)}, u32[]{:S(2)}, u32[]{:S(2)}) collective-permute-start(f32[8,1024]{0,1:T(8,128)S(1)} %copy.60), channel_id=1, source_target_pairs={{0,1},{1,2},{2,3},{3,4},{4,5},{5,6},{6,7},{8,9},{9,10},{10,11},{11... | collective-permute-start | bytes 98312 | tf_op jit(solution)/shard_map/ppermute | solution.py:41
  33.0 0.7 copy-start.4
  33.0 0.7 copy-start.5
  33.0 0.7 copy-start.6
  33.0 0.7 copy-start.7
  33.7 1.0 %copy-start = (f32[80,768]{1,0:T(8,128)}, f32[80,768]{1,0:T(8,128)S(1)}, u32[]{:S(2)}) copy-start(f32[80,768]{1,0:T(8,128)S(1)} %copy.72.diag_ref) | copy-start | bytes 737284
  36.8 0.7 copy-start.2
  47.5 7.5 %collective-permute-start.3 = (f32[2,8,768]{2,1,0:T(8,128)S(1)}, f32[2,8,768]{2,1,0:T(8,128)S(1)}, u32[]{:S(2)}, u32[]{:S(2)}) collective-permute-start(f32[2,8,768]{2,1,0:T(8,128)S(1)} %get-tuple-element.13), channel_id=1, source_target_pairs={{1,0},{2,1},{3,2},{4,3},{5,4},{6,5},{7,6},{9,8},{10,9},{11,10},{12... | collective-permute-start | bytes 147464 | tf_op jit(solution)/shard_map/ppermute | solution.py:52
  49.5 6.5 %collective-permute-start.2 = (f32[2,8,768]{2,1,0:T(8,128)S(1)}, f32[2,8,768]{2,1,0:T(8,128)S(1)}, u32[]{:S(2)}, u32[]{:S(2)}) collective-permute-start(f32[2,8,768]{2,1,0:T(8,128)S(1)} %get-tuple-element.12), channel_id=1, source_target_pairs={{0,1},{1,2},{2,3},{3,4},{4,5},{5,6},{6,7},{8,9},{9,10},{10,11},{11... | collective-permute-start | bytes 147464 | tf_op jit(solution)/shard_map/ppermute | solution.py:51
  58.2 0.7 copy-start.3

commit v5 on v3

--- a/solution.py
+++ b/solution.py
@@ -169,9 +169,9 @@
 
     wide_side, kappa_rows, inside_rows = with_halo(right_side, kappa, margin)
     extended = rows + 2 * margin
-    sent = column_tiles(wide_side, tiles, width, margin)
+    sent = column_tiles(wide_side, tiles, width, margin).reshape(tiles, extended * width)
     gathered = lax.all_to_all(sent, "tm", 0, 0, tiled=True)
-    spectrum = jnp.einsum("pt,trc->prc", forward, gathered, precision=highest)
+    spectrum = jnp.dot(forward, gathered, precision=highest)
     spectrum = spectrum.reshape(2, half, extended, width).transpose(0, 2, 1, 3)
     spectrum = spectrum.reshape(2, extended, half * width)
 
@@ -184,10 +184,11 @@
     solved = solve_slots(spectrum, faces, shifts, inside)
 
     solved = solved.reshape(2, extended, half, width)[:, margin : margin + rows, :, margin : margin + span]
-    solved = solved.transpose(0, 2, 1, 3).reshape(total, rows, span)
-    signal = jnp.einsum("tp,prc->trc", inverse, solved, precision=highest)
+    solved = solved.transpose(0, 2, 1, 3).reshape(total, rows * span)
+    signal = jnp.dot(inverse, solved, precision=highest)
     returned = lax.all_to_all(signal, "tm", 0, 0, tiled=True)
-    return returned.transpose(1, 0, 2).reshape(steps_dev, rows, cols)
+    returned = returned.reshape(tiles, rows, span).transpose(1, 0, 2)
+    return returned.reshape(steps_dev, rows, cols)
 
 
 def solution(mesh):

time: 64.2 us -> 62.6 us (0.975)
  local copies, waits for them, and re-layouts: 13.2 us -> 16.5 us
  waiting for transfers between devices: 9.42 us -> 6.96 us
  other arithmetic: 4.42 us -> 2.87 us
    all_to_all x1, waiting for transfers between devices: 8.49 us -> 6.03 us  [body(): gathered = lax.all_to_all(sent, 'tm', 0, 0, tiled=True)]
    all_to_all x0 -> x1, local copies, waits for them, and re-layouts: none -> 2.08 us  [body(): gathered = lax.all_to_all(sent, 'tm', 0, 0, tiled=True)]
    transpose x2 -> x5, local copies, waits for them, and re-layouts: 0.51 us -> 1.67 us  [the longest x2 0.56 us: body(): solved = solved.transpose(0, 2, 1, 3).reshape(total, rows * span)]
    transpose x1, other arithmetic: 0.97 us -> 0.06 us  [column_tiles(): return jnp.concatenate([main, extra], axis=2).transpose(1, 0, 2)]
    reshape x1 -> x3, local copies, waits for them, and re-layouts: 0.89 us -> 1.72 us  [the longest x1 0.9 us: body(): return returned.reshape(steps_dev, rows, cols)]
    dot_general x2, matrix products: 1.52 us -> 0.88 us  [the longest x1 0.53 us: body(): spectrum = jnp.dot(forward, gathered, precision=highest)]
    all_to_all x1, other arithmetic: 1.26 us -> 0.61 us  [body(): returned = lax.all_to_all(signal, 'tm', 0, 0, tiled=True)]
    unnamed x20 -> x16, local copies, waits for them, and re-layouts: 2.87 us -> 2.33 us
where the time goes in v5:
time: 62.6 us; the launch traced here: 61.8 us
  local copies, waits for them, and re-layouts  16.5 us (26%)
  starting transfers between devices  15.4 us (25%)
  blocking collectives  12.4 us (20%)
  waiting for transfers between devices  6.96 us (11%)
  Pallas kernels  6.45 us (10%)
  other arithmetic  2.87 us (5%)
  matrix products  0.88 us (1%)
    all_to_all x1, blocking collectives, body(): returned = lax.all_to_all(signal, 'tm', 0, 0, tiled=True)  12.4 us
    all_to_all x1, starting transfers between devices, body(): gathered = lax.all_to_all(sent, 'tm', 0, 0, tiled=True)  8.72 us
    pallas_call x1, Pallas kernels, solve_slots(): pl.pallas_call(solve_kernel, out_shape=jax.ShapeDtypeStruct(spectrum.shap...  6.45 us
    all_to_all x1, waiting for transfers between devices, body(): gathered = lax.all_to_all(sent, 'tm', 0, 0, tiled=True)  6.03 us
    ppermute x1, starting transfers between devices, with_halo(): low = lax.ppermute(joined[:, rows - width:], 'row', forward)  4.76 us
    another operation x10, local copies, waits for them, and re-layouts, body(): jnp.tile(f, (1, half))  3.68 us
    unnamed x16, local copies, waits for them, and re-layouts  2.33 us
    all_to_all x1, local copies, waits for them, and re-layouts, body(): gathered = lax.all_to_all(sent, 'tm', 0, 0, tiled=True)  2.08 us
  transfers between devices with their start and end apart: 3, of which 2 were waited for; matrix products, arithmetic and copies ran while one was open for 9% of the time, Pallas kernels for 0%

profile of v5, /device:TPU:97, one launch (start us, length us, event | category | flops | bytes accessed | tf_op | source)
XLA Modules:
  0.0 61.8 jit_solution(17090790551994497132)
XLA Ops:
  0.0 1.1 %copy.32 = f32[64,1024]{0,1:T(8,128)S(1)} copy(f32[64,1024]{1,0:T(8,128)} %param.11) | data formatting | bytes 524288 | tf_op args[1]
  1.2 1.1 %copy.33 = f32[1,64,1024]{1,2,0:T(8,128)S(1)} copy(f32[1,64,1024]{2,1,0:T(8,128)} %param.10) | data formatting | bytes 524288 | tf_op args[0]
  2.3 0.4 slice_maximum_fusion
  2.7 0.3 copy.35
  3.0 1.9 %collective-permute-start.1 = (f32[2,8,1024]{2,1,0:T(8,128)S(1)}, f32[2,8,1024]{2,1,0:T(8,128)S(1)}, u32[]{:S(2)}, u32[]{:S(2)}) collective-permute-start(f32[2,8,1024]{2,1,0:T(8,128)S(1)} %copy.35), channel_id=1, source_target_pairs={{1,0},{2,1},{3,2},{4,3},{5,4},{6,5},{7,6},{9,8},{10,9},{11,10},{12... | collective-permute-start | bytes 196616 | tf_op jit(solution)/shard_map/ppermute | solution.py:37
  4.9 0.3 copy.34
  5.2 4.8 %collective-permute-start = (f32[2,8,1024]{2,1,0:T(8,128)S(1)}, f32[2,8,1024]{2,1,0:T(8,128)S(1)}, u32[]{:S(2)}, u32[]{:S(2)}) collective-permute-start(f32[2,8,1024]{2,1,0:T(8,128)S(1)} %copy.34), channel_id=1, source_target_pairs={{0,1},{1,2},{2,3},{3,4},{4,5},{5,6},{6,7},{8,9},{9,10},{10,11},{11... | collective-permute-start | bytes 196616 | tf_op jit(solution)/shard_map/ppermute | solution.py:36
  10.0 0.0 collective-permute-done.1
  10.0 0.3 copy.37
  10.3 0.9 %collective-permute-done = f32[2,8,1024]{2,1,0:T(8,128)S(1)} collective-permute-done((f32[2,8,1024]{2,1,0:T(8,128)S(1)}, f32[2,8,1024]{2,1,0:T(8,128)S(1)}, u32[]{:S(2)}, u32[]{:S(2)}) %collective-permute-start) | collective-permute-done | bytes 65568 | tf_op jit(solution)/shard_map/ppermute | solution.py:36
  11.3 0.3 copy.36
  11.6 0.6 pad_maximum_fusion.1
  12.2 0.1 slice_bitcast_fusion.1
  12.3 0.1 pad_slice_fusion.1
  12.4 0.1 maximum_bitcast_fusion
  12.5 0.4 copy.38
  12.9 2.1 %all_to_all.19 = f32[32,1,3840]{2,1,0:T(1,128)} reshape(f32[32,80,48]{2,1,0:T(8,128)S(1)} %copy.38) | data formatting | bytes 983040 | tf_op jit(solution)/shard_map/all_to_all | solution.py:173
  14.9 8.7 %all-to-all-start = ((f32[32,1,3840]{2,1,0:T(1,128)}), f32[32,1,3840]{2,1,0:T(1,128)S(1)}, u32[]{:S(2)}, u32[]{:S(2)}) async-start(f32[32,1,3840]{2,1,0:T(1,128)} %all_to_all.19), calls=%async_computation | async-start | bytes 983040 | tf_op jit(solution)/shard_map/all_to_all | solution.py:173
  23.7 0.1 broadcast_and_fusion
  23.8 0.2 copy.42
  24.0 0.2 add_add_fusion
  24.2 0.8 %copy.47.north_ref = f32[80,768]{1,0:T(8,128)} copy(f32[80,768]{0,1:T(8,128)S(1)} %bitcast.40) | data formatting | bytes 491520 | tf_op jit(solution)/shard_map/tile | solution.py:182
  25.0 0.9 %copy.48.south_ref = f32[80,768]{1,0:T(8,128)} copy(f32[80,768]{0,1:T(8,128)S(1)} %bitcast.41) | data formatting | bytes 491520 | tf_op jit(solution)/shard_map/tile | solution.py:182
  25.9 0.0 copy-start.3
  26.0 0.0 copy-start.4
  26.0 0.0 copy-start.5
  26.0 0.0 copy-start.6
  26.0 0.8 %copy.49.east_ref = f32[80,768]{1,0:T(8,128)} copy(f32[80,768]{0,1:T(8,128)S(1)} %bitcast.42) | data formatting | bytes 491520 | tf_op jit(solution)/shard_map/tile | solution.py:182
  26.9 0.0 copy-start.1
  26.9 0.8 %copy.50.west_ref = f32[80,768]{1,0:T(8,128)} copy(f32[80,768]{0,1:T(8,128)S(1)} %bitcast.43) | data formatting | bytes 491520 | tf_op jit(solution)/shard_map/tile | solution.py:182
  27.7 0.1 copy.51.diag_ref
  27.9 0.0 copy-done.3
  27.9 0.0 copy-done.4
  27.9 0.0 copy-done.5
  27.9 0.0 copy-done.6
  27.9 0.0 copy-start
  28.0 1.0 %divide_select_fusion = (f32[80,768]{1,0:T(8,128)}, f32[80,768]{1,0:T(8,128)}, f32[80,768]{1,0:T(8,128)}) fusion(pred[80,768]{1,0:T(8,128)(4,1)S(1)} %copy.42, f32[80,768]{1,0:T(8,128)S(1)} %copy.51.diag_ref, f32[768]{0:T(1024)S(1)} %copy-done.3, f32[768]{0:T(1024)S(1)} %copy-done.4, f32[768]{0:T(1024)S(1)} %copy-done.5, f32[768]{0:T(1024)S(1)} %copy-done.6), kind=kLoop, calls=%fused_computation.18 | loop fusion | flops 737280 | bytes 1056768 | tf_op jit(solution)/shard_map/jit(_where)/select_n | solution.py:148
  28.9 6.0 %all-to-all-done = f32[32,1,3840]{2,1,0:T(1,128)S(1)} async-done(((f32[32,1,3840]{2,1,0:T(1,128)}), f32[32,1,3840]{2,1,0:T(1,128)S(1)}, u32[]{:S(2)}, u32[]{:S(2)}) %all-to-all-start) | async-done | bytes 491552 | tf_op jit(solution)/shard_map/all_to_all | solution.py:173
  35.0 0.0 copy-done.1
  35.0 0.5 fusion
  35.5 0.8 %reshape.96 = f32[2,16,80,48]{3,2,1,0:T(8,128)S(1)} reshape(f32[32,3840]{1,0:T(8,128)S(1)} %fusion) | data formatting | bytes 983040 | tf_op jit(solution)/shard_map/reshape | solution.py:175
  36.3 0.0 copy-done
  36.3 0.4 copy.40
  36.7 1.0 %copy.46.spec_ref = f32[2,80,768]{2,1,0:T(8,128)} copy(f32[2,80,768]{1,2,0:T(8,128)S(1)} %bitcast.36) | data formatting | bytes 983040 | tf_op jit(solution)/shard_map/reshape | solution.py:176
  37.8 6.4 %shard_map.100 = f32[2,80,768]{2,1,0:T(8,128)} custom-call(f32[2,80,768]{2,1,0:T(8,128)} %copy.46.spec_ref, f32[80,768]{1,0:T(8,128)} %copy.47.north_ref, f32[80,768]{1,0:T(8,128)} %copy.48.south_ref, f32[80,768]{1,0:T(8,128)} %copy.49.east_ref, f32[80,768]{1,0:T(8,128)} %copy.50.west_ref, f32[80,768]{1,0:T(8,128)} %copy-done, ...), custom_call_target="tpu_custom_call" | custom-call | tf_op jit(solution)/shard_map/pallas_call | solution.py:152
  44.2 1.3 %copy.52 = f32[2,80,768]{1,2,0:T(8,128)S(1)} copy(f32[2,80,768]{2,1,0:T(8,128)} %shard_map.100) | data formatting | bytes 983040 | tf_op jit(solution)/shard_map/pallas_call | solution.py:152
  45.5 0.2 slice_bitcast_fusion
  45.7 0.0 copy-start.2
  45.7 0.4 copy.53
  46.1 0.5 reshape.99
  46.6 0.0 copy-done.2
  46.6 0.4 convolution_bitcast_fusion
  46.9 0.3 copy.54
  47.2 12.4 %all_to_all.22 = f32[32,1,2048]{2,1,0:T(1,128)S(1)} all-to-all(f32[32,1,2048]{2,1,0:T(1,128)S(1)} %copy.54), channel_id=1, replica_groups=mesh['tm'=32,'row'=8] {'tm'}, dimensions={0} | all-to-all | bytes 524288 | tf_op jit(solution)/shard_map/all_to_all | solution.py:189
  59.6 0.6 reduce
  60.2 0.3 reshape.100
  60.6 0.3 copy.55
  60.9 0.9 %copy.56 = f32[1,64,1024]{2,1,0:T(8,128)} copy(f32[1,64,1024]{1,2,0:T(8,128)S(1)} %bitcast.39) | data formatting | bytes 524288 | tf_op jit(solution)/shard_map/reshape | solution.py:191
  (9 shorter events, 0.2 us)
Async XLA Ops:
  3.0 7.0 %collective-permute-start.1 = (f32[2,8,1024]{2,1,0:T(8,128)S(1)}, f32[2,8,1024]{2,1,0:T(8,128)S(1)}, u32[]{:S(2)}, u32[]{:S(2)}) collective-permute-start(f32[2,8,1024]{2,1,0:T(8,128)S(1)} %copy.35), channel_id=1, source_target_pairs={{1,0},{2,1},{3,2},{4,3},{5,4},{6,5},{7,6},{9,8},{10,9},{11,10},{12... | collective-permute-start | bytes 196616 | tf_op jit(solution)/shard_map/ppermute | solution.py:37
  5.2 6.1 %collective-permute-start = (f32[2,8,1024]{2,1,0:T(8,128)S(1)}, f32[2,8,1024]{2,1,0:T(8,128)S(1)}, u32[]{:S(2)}, u32[]{:S(2)}) collective-permute-start(f32[2,8,1024]{2,1,0:T(8,128)S(1)} %copy.34), channel_id=1, source_target_pairs={{0,1},{1,2},{2,3},{3,4},{4,5},{5,6},{6,7},{8,9},{9,10},{10,11},{11... | collective-permute-start | bytes 196616 | tf_op jit(solution)/shard_map/ppermute | solution.py:36
  14.9 20.0 %all-to-all-start = ((f32[32,1,3840]{2,1,0:T(1,128)}), f32[32,1,3840]{2,1,0:T(1,128)S(1)}, u32[]{:S(2)}, u32[]{:S(2)}) async-start(f32[32,1,3840]{2,1,0:T(1,128)} %all_to_all.19), calls=%async_computation | async-start | bytes 983040 | tf_op jit(solution)/shard_map/all_to_all | solution.py:173
  25.9 2.0 %copy-start.3 = (f32[768]{0:T(1024)S(1)}, f32[768]{0:T(1024)}, u32[]{:S(2)}) copy-start(f32[768]{0:T(1024)} %constant.63) | copy-start | bytes 9220
  26.0 2.0 %copy-start.4 = (f32[768]{0:T(1024)S(1)}, f32[768]{0:T(1024)}, u32[]{:S(2)}) copy-start(f32[768]{0:T(1024)} %constant.61) | copy-start | bytes 9220
  26.0 2.0 %copy-start.5 = (f32[768]{0:T(1024)S(1)}, f32[768]{0:T(1024)}, u32[]{:S(2)}) copy-start(f32[768]{0:T(1024)} %constant.60) | copy-start | bytes 9220
  26.0 2.0 %copy-start.6 = (f32[768]{0:T(1024)S(1)}, f32[768]{0:T(1024)}, u32[]{:S(2)}) copy-start(f32[768]{0:T(1024)} %constant.62) | copy-start | bytes 9220
  26.9 8.1 %copy-start.1 = (f32[32,32]{1,0:T(8,128)S(1)}, f32[32,32]{1,0:T(8,128)}, u32[]{:S(2)}) copy-start(f32[32,32]{1,0:T(8,128)} %constant.48.clone) | copy-start | bytes 12292
  27.9 8.4 %copy-start = (f32[80,768]{1,0:T(8,128)}, f32[80,768]{1,0:T(8,128)S(1)}, u32[]{:S(2)}) copy-start(f32[80,768]{1,0:T(8,128)S(1)} %copy.51.diag_ref) | copy-start | bytes 737284
  45.7 0.9 %copy-start.2 = (f32[32,32]{1,0:T(8,128)S(1)}, f32[32,32]{1,0:T(8,128)}, u32[]{:S(2)}) copy-start(f32[32,32]{1,0:T(8,128)} %constant.54.clone) | copy-start | bytes 12292

commit v6 on v5

--- a/solution.py
+++ b/solution.py
@@ -1,3 +1,4 @@
+import functools
 import math
 
 import jax
@@ -62,7 +63,7 @@
     return forward.astype(np.float32), inverse.astype(np.float32)
 
 
-def slot_shifts(half, total, width):
+def slot_shifts(half, total):
     decay = circulant_alpha ** (1.0 / total)
     slots = np.arange(half)
     theta = 2.0 * np.pi / total * slots
@@ -71,8 +72,8 @@
     imag = decay * np.sin(theta)
     real_b[0] = 1.0 + decay
     imag[0] = 0.0
-    spread = lambda v: np.repeat(v.astype(np.float32), width)[None, :]
-    return spread(real_a), spread(real_b), spread(imag)
+    column = lambda v: v.astype(np.float32)[:, None]
+    return column(real_a), column(real_b), column(imag)
 
 
 def tile_faces(kappa_rows, tile, tiles, width, margin):
@@ -98,59 +99,68 @@
     return jnp.concatenate([main, extra], axis=2).transpose(1, 0, 2)
 
 
-def solve_kernel(spec_ref, north_ref, south_ref, east_ref, west_ref, diag_ref,
-                 inva_ref, invb_ref, invi_ref, reala_ref, realb_ref, imag_ref, out_ref):
-    rows, lanes = north_ref.shape
-
-    def spatial(x):
-        above = pltpu.roll(x, rows - 1, 0)
-        below = pltpu.roll(x, 1, 0)
+def solve_kernel(step, spec_ref, north_ref, south_ref, east_ref, west_ref, diag_a_ref, diag_b_ref,
+                 imag_ref, inva_ref, invb_ref, invi_ref, out_ref):
+    group = north_ref.shape[0]
+    half, lanes = inva_ref.shape
+
+    def coupled(x):
+        above = pltpu.roll(x, lanes - step, 1)
+        below = pltpu.roll(x, step, 1)
         after = pltpu.roll(x, lanes - 1, 1)
         before = pltpu.roll(x, 1, 1)
-        coupled = (north_ref[...] * above + south_ref[...] * below
-                   + east_ref[...] * after + west_ref[...] * before)
-        return diag_ref[...] * x - coupled - courant_rows * below - courant_cols * before
-
-    first = True
-    for sweep in range(SWEEPS):
-        for weight in step_weights(DEGREE):
-            if first:
-                res_real = spec_ref[0]
-                res_imag = spec_ref[1]
-            else:
-                state_real = out_ref[0]
-                state_imag = out_ref[1]
-                image_real = (reala_ref[...] * state_real - imag_ref[...] * state_imag
-                              + spatial(state_real))
-                image_imag = (realb_ref[...] * state_imag + imag_ref[...] * state_real
-                              + spatial(state_imag))
-                res_real = spec_ref[0] - image_real
-                res_imag = spec_ref[1] - image_imag
-            corr_real = inva_ref[...] * res_real - invi_ref[...] * res_imag
-            corr_imag = invb_ref[...] * res_imag + invi_ref[...] * res_real
-            if first:
-                out_ref[0] = weight * corr_real
-                out_ref[1] = weight * corr_imag
-                first = False
-            else:
-                out_ref[0] = out_ref[0] + weight * corr_real
-                out_ref[1] = out_ref[1] + weight * corr_imag
-
-
-def solve_slots(spectrum, faces, shifts, inside):
+        return (north_ref[...] * above + south_ref[...] * below + east_ref[...] * after
+                + west_ref[...] * before + courant_rows * below + courant_cols * before)
+
+    for start in range(0, half, group):
+        part = slice(start, start + group)
+        real = slice(start, start + group)
+        imag = slice(half + start, half + start + group)
+        first = True
+        for sweep in range(SWEEPS):
+            for weight in step_weights(DEGREE):
+                if first:
+                    res_real = spec_ref[real]
+                    res_imag = spec_ref[imag]
+                else:
+                    state_real = out_ref[real]
+                    state_imag = out_ref[imag]
+                    image_real = (diag_a_ref[part] * state_real - imag_ref[part] * state_imag
+                                  - coupled(state_real))
+                    image_imag = (diag_b_ref[part] * state_imag + imag_ref[part] * state_real
+                                  - coupled(state_imag))
+                    res_real = spec_ref[real] - image_real
+                    res_imag = spec_ref[imag] - image_imag
+                corr_real = inva_ref[part] * res_real - invi_ref[part] * res_imag
+                corr_imag = invb_ref[part] * res_imag + invi_ref[part] * res_real
+                if first:
+                    out_ref[real] = weight * corr_real
+                    out_ref[imag] = weight * corr_imag
+                    first = False
+                else:
+                    out_ref[real] = out_ref[real] + weight * corr_real
+                    out_ref[imag] = out_ref[imag] + weight * corr_imag
+
+
+def solve_slots(spectrum, faces, shifts, inside, width):
     real_a, real_b, imag = shifts
-    diag_a = real_a + faces[4]
-    diag_b = real_b + faces[4]
+    group = 8
+    north, south, east, west, diagonal = (f.reshape(1, -1) for f in faces)
+    inside = inside.reshape(1, -1)
+    diag_a = real_a + diagonal
+    diag_b = real_b + diagonal
     mag_a = diag_a * diag_a + imag * imag
     mag_b = diag_b * diag_b + imag * imag
     inv_a = jnp.where(inside, diag_a / mag_a, 0.0)
     inv_b = jnp.where(inside, diag_b / mag_b, 0.0)
     inv_imag = jnp.where(inside, -imag / mag_a, 0.0)
-    operands = (spectrum,) + tuple(faces) + (inv_a, inv_b, inv_imag) + tuple(
-        jnp.asarray(s) for s in shifts
-    )
+    imag = jnp.broadcast_to(imag, inv_a.shape)
+    lanes = north.shape[1]
+    spread = lambda f: jnp.broadcast_to(f, (group, lanes))
+    operands = (spectrum,) + tuple(spread(f) for f in (north, south, east, west)) + (
+        diag_a, diag_b, imag, inv_a, inv_b, inv_imag)
     return pl.pallas_call(
-        solve_kernel,
+        functools.partial(solve_kernel, width),
         out_shape=jax.ShapeDtypeStruct(spectrum.shape, spectrum.dtype),
     )(*operands)
 
@@ -172,21 +182,16 @@
     sent = column_tiles(wide_side, tiles, width, margin).reshape(tiles, extended * width)
     gathered = lax.all_to_all(sent, "tm", 0, 0, tiled=True)
     spectrum = jnp.dot(forward, gathered, precision=highest)
-    spectrum = spectrum.reshape(2, half, extended, width).transpose(0, 2, 1, 3)
-    spectrum = spectrum.reshape(2, extended, half * width)
 
     place = tile * span - margin + jnp.arange(width)
     inside_cols = (place >= 0) & (place < cols)
     inside = inside_rows[:, None] & inside_cols[None, :]
-    inside = jnp.tile(inside, (1, half))
-    faces = tuple(jnp.tile(f, (1, half)) for f in tile_faces(kappa_rows, tile, tiles, width, margin))
-    shifts = slot_shifts(half, total, width)
-    solved = solve_slots(spectrum, faces, shifts, inside)
-
-    solved = solved.reshape(2, extended, half, width)[:, margin : margin + rows, :, margin : margin + span]
-    solved = solved.transpose(0, 2, 1, 3).reshape(total, rows * span)
+    faces = tile_faces(kappa_rows, tile, tiles, width, margin)
+    solved = solve_slots(spectrum, faces, slot_shifts(half, total), inside, width)
+
     signal = jnp.dot(inverse, solved, precision=highest)
-    returned = lax.all_to_all(signal, "tm", 0, 0, tiled=True)
+    signal = signal.reshape(total, extended, width)[:, margin : margin + rows, margin : margin + span]
+    returned = lax.all_to_all(signal.reshape(total, rows * span), "tm", 0, 0, tiled=True)
     returned = returned.reshape(tiles, rows, span).transpose(1, 0, 2)
     return returned.reshape(steps_dev, rows, cols)
 

time: 62.6 us -> 66.3 us (1.059)
  waiting for transfers between devices: 6.96 us -> 9.78 us
  local copies, waits for them, and re-layouts: 16.5 us -> 13.7 us
  matrix products: 0.88 us -> 2.86 us
  Pallas kernels: 6.45 us -> 7.83 us
    another operation x12 -> x0, local copies, waits for them, and re-layouts: 3.88 us -> none  [the longest x10 3.68 us: body(): jnp.tile(f, (1, half))]
    broadcast_in_dim x0 -> x9, local copies, waits for them, and re-layouts: none -> 3.74 us  [the longest x8 2.95 us: solve_slots(): spread = lambda f: jnp.broadcast_to(f, (group, lanes))]
    all_to_all x1, waiting for transfers between devices: 6.03 us -> 9.04 us  [body(): gathered = lax.all_to_all(sent, 'tm', 0, 0, tiled=True)]
    reshape x3 -> x1, local copies, waits for them, and re-layouts: 2.36 us -> 0.82 us  [body(): signal.reshape(total, extended, width)]
    pallas_call x1, Pallas kernels: 6.45 us -> 7.83 us  [solve_slots(): pl.pallas_call(functools.partial(solve_kernel, width), out_shape=jax.Shap...]
    pallas_call x1 -> x0, local copies, waits for them, and re-layouts: 1.29 us -> none  [solve_slots(): pl.pallas_call(solve_kernel, out_shape=jax.ShapeDtypeStruct(spectrum.shap...]
    dot_general x1, matrix products: 0.35 us -> 1.55 us  [body(): signal = jnp.dot(inverse, solved, precision=highest)]
    transpose x3 -> x0, local copies, waits for them, and re-layouts: 0.93 us -> none  [the longest x2 0.56 us: body(): solved = solved.transpose(0, 2, 1, 3).reshape(total, rows * span)]
  transfers between devices with their start and end apart: 3 -> 3, of which waited for: 2 -> 2; matrix products, arithmetic and copies ran while one was open for 9% -> 5% of each run, Pallas kernels for 0% -> 0%
where the time goes in v6:
time: 66.3 us; the launch traced here: 65.4 us
  starting transfers between devices  15.5 us (23%)
  local copies, waits for them, and re-layouts  13.7 us (21%)
  blocking collectives  12.4 us (19%)
  waiting for transfers between devices  9.78 us (15%)
  Pallas kernels  7.83 us (12%)
  other arithmetic  3.04 us (5%)
  matrix products  2.86 us (4%)
    all_to_all x1, blocking collectives, body(): lax.all_to_all(signal.reshape(total, rows * span), 'tm', 0, 0, tiled=True)  12.4 us
    all_to_all x1, waiting for transfers between devices, body(): gathered = lax.all_to_all(sent, 'tm', 0, 0, tiled=True)  9.04 us
    all_to_all x1, starting transfers between devices, body(): gathered = lax.all_to_all(sent, 'tm', 0, 0, tiled=True)  8.86 us
    pallas_call x1, Pallas kernels, solve_slots(): pl.pallas_call(functools.partial(solve_kernel, width), out_shape=jax.Shap...  7.83 us
    ppermute x1, starting transfers between devices, with_halo(): low = lax.ppermute(joined[:, rows - width:], 'row', forward)  4.76 us
    broadcast_in_dim x8, local copies, waits for them, and re-layouts, solve_slots(): spread = lambda f: jnp.broadcast_to(f, (group, lanes))  2.95 us
    unnamed x16, local copies, waits for them, and re-layouts  2.32 us
    all_to_all x1, local copies, waits for them, and re-layouts, body(): gathered = lax.all_to_all(sent, 'tm', 0, 0, tiled=True)  2.08 us
  transfers between devices with their start and end apart: 3, of which 2 were waited for; matrix products, arithmetic and copies ran while one was open for 5% of the time, Pallas kernels for 0%

profile of v6, /device:TPU:97, one launch (start us, length us, event | category | flops | bytes accessed | tf_op | source)
XLA Modules:
  0.0 65.4 jit_solution(10731261883398472742)
XLA Ops:
  0.0 1.1 %copy.21 = f32[64,1024]{0,1:T(8,128)S(1)} copy(f32[64,1024]{1,0:T(8,128)} %param.11) | data formatting | bytes 524288 | tf_op args[1]
  1.2 1.1 %copy.22 = f32[1,64,1024]{1,2,0:T(8,128)S(1)} copy(f32[1,64,1024]{2,1,0:T(8,128)} %param.10) | data formatting | bytes 524288 | tf_op args[0]
  2.3 0.4 slice_maximum_fusion
  2.7 0.3 copy.24
  3.0 1.9 %collective-permute-start.1 = (f32[2,8,1024]{2,1,0:T(8,128)S(1)}, f32[2,8,1024]{2,1,0:T(8,128)S(1)}, u32[]{:S(2)}, u32[]{:S(2)}) collective-permute-start(f32[2,8,1024]{2,1,0:T(8,128)S(1)} %copy.24), channel_id=1, source_target_pairs={{1,0},{2,1},{3,2},{4,3},{5,4},{6,5},{7,6},{9,8},{10,9},{11,10},{12... | collective-permute-start | bytes 196616 | tf_op jit(solution)/shard_map/ppermute | solution.py:38
  4.9 0.3 copy.23
  5.2 4.8 %collective-permute-start = (f32[2,8,1024]{2,1,0:T(8,128)S(1)}, f32[2,8,1024]{2,1,0:T(8,128)S(1)}, u32[]{:S(2)}, u32[]{:S(2)}) collective-permute-start(f32[2,8,1024]{2,1,0:T(8,128)S(1)} %copy.23), channel_id=1, source_target_pairs={{0,1},{1,2},{2,3},{3,4},{4,5},{5,6},{6,7},{8,9},{9,10},{10,11},{11... | collective-permute-start | bytes 196616 | tf_op jit(solution)/shard_map/ppermute | solution.py:37
  10.0 0.1 broadcast_and_fusion
  10.1 0.1 and.41
  10.2 0.0 collective-permute-done.1
  10.2 0.3 copy.26
  10.5 0.7 %collective-permute-done = f32[2,8,1024]{2,1,0:T(8,128)S(1)} collective-permute-done((f32[2,8,1024]{2,1,0:T(8,128)S(1)}, f32[2,8,1024]{2,1,0:T(8,128)S(1)}, u32[]{:S(2)}, u32[]{:S(2)}) %collective-permute-start) | collective-permute-done | bytes 65568 | tf_op jit(solution)/shard_map/ppermute | solution.py:37
  11.3 0.3 copy.25
  11.6 0.6 pad_maximum_fusion.1
  12.2 0.1 slice_bitcast_fusion
  12.3 0.1 pad_slice_fusion.1
  12.4 0.1 maximum_bitcast_fusion
  12.5 0.4 copy.27
  12.9 2.1 %all_to_all.19 = f32[32,1,3840]{2,1,0:T(1,128)} reshape(f32[32,80,48]{2,1,0:T(8,128)S(1)} %copy.27) | data formatting | bytes 983040 | tf_op jit(solution)/shard_map/all_to_all | solution.py:183
  14.9 0.0 copy-start.2
  14.9 0.0 copy-start.3
  15.0 0.0 copy-start.4
  15.0 0.0 copy-start.5
  15.0 8.9 %all-to-all-start = ((f32[32,1,3840]{2,1,0:T(1,128)}), f32[32,1,3840]{2,1,0:T(1,128)S(1)}, u32[]{:S(2)}, u32[]{:S(2)}) async-start(f32[32,1,3840]{2,1,0:T(1,128)} %all_to_all.19), calls=%async_computation | async-start | bytes 983040 | tf_op jit(solution)/shard_map/all_to_all | solution.py:183
  23.8 0.0 copy-start.1
  23.8 0.2 add_add_fusion
  24.0 0.1 copy.29
  24.1 0.1 broadcast_in_dim.61
  24.2 0.1 copy.30
  24.3 0.1 broadcast_in_dim.63
  24.4 0.1 copy.31
  24.4 0.1 broadcast_in_dim.65
  24.5 0.1 copy.32
  24.6 0.1 broadcast_in_dim.67
  24.7 0.1 copy.33
  24.8 0.1 add.118
  24.9 0.0 copy-done.2
  24.9 0.0 copy-done.3
  24.9 0.0 copy-done.4
  24.9 0.0 copy-done.5
  24.9 0.0 copy-start.6
  24.9 1.1 %divide_select_fusion = (f32[16,3840]{1,0:T(8,128)}, f32[16,3840]{1,0:T(8,128)}, f32[16,3840]{1,0:T(8,128)}, f32[16,3840]{1,0:T(8,128)}, f32[16,3840]{1,0:T(8,128)}) fusion(f32[16]{0:T(128)S(1)} %copy-done.2, f32[16]{0:T(128)S(1)} %copy-done.3, f32[3840]{0:T(1024)S(1)} %add.118, f32[16]{0:T(128)S(1)} %copy-done.4, pred[3840]{0:T(1024)(128)(4,1)S(1)} %and.41, ...), kind=kLoop, calls=%fused_computation.16 | loop fusion | flops 737280 | bytes 1248256 | tf_op jit(solution)/shard_map/jit(_where)/select_n | solution.py:156
  26.1 9.0 %all-to-all-done = f32[32,1,3840]{2,1,0:T(1,128)S(1)} async-done(((f32[32,1,3840]{2,1,0:T(1,128)}), f32[32,1,3840]{2,1,0:T(1,128)S(1)}, u32[]{:S(2)}, u32[]{:S(2)}) %all-to-all-start) | async-done | bytes 491552 | tf_op jit(solution)/shard_map/all_to_all | solution.py:183
  35.1 0.0 copy-done.1
  35.1 1.3 %fusion.spec_ref = f32[32,3840]{1,0:T(8,128)} fusion(f32[32,32]{1,0:T(8,128)S(1)} %copy-done.1, f32[32,1,3840]{2,1,0:T(1,128)S(1)} %all-to-all-done), kind=kOutput, calls=%fused_computation.8 | convolution fusion | flops 47185920 | bytes 987136 | tf_op jit(solution)/shard_map/dot_general | solution.py:184
  36.4 0.6 broadcast_in_dim.62.north_ref
  37.1 0.6 broadcast_in_dim.64.south_ref
  37.7 0.7 %broadcast_in_dim.66.east_ref = f32[8,3840]{1,0:T(8,128)} broadcast(f32[3840]{0:T(1024)S(1)} %broadcast_in_dim.65), dimensions={1} | broadcast | bytes 138240 | tf_op jit(solution)/shard_map/broadcast_in_dim | solution.py:159
  38.4 0.7 broadcast_in_dim.68.west_ref
  39.0 0.0 copy-done.6
  39.0 0.8 %broadcast_in_dim.70.imag_ref = f32[16,3840]{1,0:T(8,128)} broadcast(f32[16]{0:T(128)S(1)} %copy-done.6), dimensions={0} | broadcast | bytes 245824 | tf_op jit(solution)/shard_map/broadcast_in_dim | solution.py:157
  39.8 0.0 copy-start
  39.8 7.8 %shard_map.100 = f32[32,3840]{1,0:T(8,128)} custom-call(f32[32,3840]{1,0:T(8,128)} %fusion.spec_ref, f32[8,3840]{1,0:T(8,128)} %broadcast_in_dim.62.north_ref, f32[8,3840]{1,0:T(8,128)} %broadcast_in_dim.64.south_ref, f32[8,3840]{1,0:T(8,128)} %broadcast_in_dim.66.east_ref, f32[8,3840]{1,0:T(8,128)} %broadcast_in_dim.68.west_ref, ...), custom_call_target="tpu_custom_call" | custom-call | tf_op jit(solution)/shard_map/pallas_call | solution.py:162
  47.7 0.0 copy-done
  47.7 1.6 %fusion.15 = f32[32,3840]{1,0:T(8,128)S(1)} fusion(f32[32,32]{1,0:T(8,128)S(1)} %copy-done, f32[32,3840]{1,0:T(8,128)} %shard_map.100), kind=kOutput, calls=%fused_computation.34 | convolution fusion | flops 47185920 | bytes 987136 | tf_op jit(solution)/shard_map/dot_general | solution.py:192
  49.2 0.8 %reshape.65 = f32[32,80,48]{2,1,0:T(8,128)S(1)} reshape(f32[32,3840]{1,0:T(8,128)S(1)} %fusion.15) | data formatting | bytes 983040 | tf_op jit(solution)/shard_map/reshape | solution.py:193
  50.1 0.3 slice.57
  50.4 0.5 all_to_all.20
  50.8 12.4 %all_to_all.23 = f32[32,1,2048]{2,1,0:T(1,128)S(1)} all-to-all(f32[32,1,2048]{2,1,0:T(1,128)S(1)} %all_to_all.20), channel_id=1, replica_groups=mesh['tm'=32,'row'=8] {'tm'}, dimensions={0} | all-to-all | bytes 524288 | tf_op jit(solution)/shard_map/all_to_all | solution.py:194
  63.2 0.6 reduce
  63.9 0.3 reshape.66
  64.2 0.3 copy.35
  64.5 0.9 %copy.36 = f32[1,64,1024]{2,1,0:T(8,128)} copy(f32[1,64,1024]{1,2,0:T(8,128)S(1)} %bitcast.21) | data formatting | bytes 524288 | tf_op jit(solution)/shard_map/reshape | solution.py:196
  (3 shorter events, 0.0 us)
Async XLA Ops:
  3.0 7.2 %collective-permute-start.1 = (f32[2,8,1024]{2,1,0:T(8,128)S(1)}, f32[2,8,1024]{2,1,0:T(8,128)S(1)}, u32[]{:S(2)}, u32[]{:S(2)}) collective-permute-start(f32[2,8,1024]{2,1,0:T(8,128)S(1)} %copy.24), channel_id=1, source_target_pairs={{1,0},{2,1},{3,2},{4,3},{5,4},{6,5},{7,6},{9,8},{10,9},{11,10},{12... | collective-permute-start | bytes 196616 | tf_op jit(solution)/shard_map/ppermute | solution.py:38
  5.2 6.1 %collective-permute-start = (f32[2,8,1024]{2,1,0:T(8,128)S(1)}, f32[2,8,1024]{2,1,0:T(8,128)S(1)}, u32[]{:S(2)}, u32[]{:S(2)}) collective-permute-start(f32[2,8,1024]{2,1,0:T(8,128)S(1)} %copy.23), channel_id=1, source_target_pairs={{0,1},{1,2},{2,3},{3,4},{4,5},{5,6},{6,7},{8,9},{9,10},{10,11},{11... | collective-permute-start | bytes 196616 | tf_op jit(solution)/shard_map/ppermute | solution.py:37
  14.9 9.9 %copy-start.2 = (f32[16]{0:T(128)S(1)}, f32[16]{0:T(128)}, u32[]{:S(2)}) copy-start(f32[16]{0:T(128)} %constant.64) | copy-start | bytes 196
  14.9 9.9 %copy-start.3 = (f32[16]{0:T(128)S(1)}, f32[16]{0:T(128)}, u32[]{:S(2)}) copy-start(f32[16]{0:T(128)} %constant.63) | copy-start | bytes 196
  15.0 9.9 %copy-start.4 = (f32[16]{0:T(128)S(1)}, f32[16]{0:T(128)}, u32[]{:S(2)}) copy-start(f32[16]{0:T(128)} %constant.60) | copy-start | bytes 196
  15.0 10.0 %copy-start.5 = (f32[16]{0:T(128)S(1)}, f32[16]{0:T(128)}, u32[]{:S(2)}) copy-start(f32[16]{0:T(128)} %constant.61) | copy-start | bytes 196
  15.0 20.2 %all-to-all-start = ((f32[32,1,3840]{2,1,0:T(1,128)}), f32[32,1,3840]{2,1,0:T(1,128)S(1)}, u32[]{:S(2)}, u32[]{:S(2)}) async-start(f32[32,1,3840]{2,1,0:T(1,128)} %all_to_all.19), calls=%async_computation | async-start | bytes 983040 | tf_op jit(solution)/shard_map/all_to_all | solution.py:183
  23.8 11.3 %copy-start.1 = (f32[32,32]{1,0:T(8,128)S(1)}, f32[32,32]{1,0:T(8,128)}, u32[]{:S(2)}) copy-start(f32[32,32]{1,0:T(8,128)} %constant.48.clone) | copy-start | bytes 12292
  24.9 14.1 %copy-start.6 = (f32[16]{0:T(128)S(1)}, f32[16]{0:T(128)}, u32[]{:S(2)}) copy-start(f32[16]{0:T(128)} %constant.62) | copy-start | bytes 196
  39.8 7.8 %copy-start = (f32[32,32]{1,0:T(8,128)S(1)}, f32[32,32]{1,0:T(8,128)}, u32[]{:S(2)}) copy-start(f32[32,32]{1,0:T(8,128)} %constant.54.clone) | copy-start | bytes 12292

commit v7 on v5

--- a/solution.py
+++ b/solution.py
@@ -169,8 +169,9 @@
 
     wide_side, kappa_rows, inside_rows = with_halo(right_side, kappa, margin)
     extended = rows + 2 * margin
-    sent = column_tiles(wide_side, tiles, width, margin).reshape(tiles, extended * width)
-    gathered = lax.all_to_all(sent, "tm", 0, 0, tiled=True)
+    lane = 128
+    sent = column_tiles(wide_side, tiles, width, margin).reshape(tiles, -1, lane)
+    gathered = lax.all_to_all(sent, "tm", 0, 0, tiled=True).reshape(tiles, extended * width)
     spectrum = jnp.dot(forward, gathered, precision=highest)
     spectrum = spectrum.reshape(2, half, extended, width).transpose(0, 2, 1, 3)
     spectrum = spectrum.reshape(2, extended, half * width)
@@ -186,6 +187,7 @@
     solved = solved.reshape(2, extended, half, width)[:, margin : margin + rows, :, margin : margin + span]
     solved = solved.transpose(0, 2, 1, 3).reshape(total, rows * span)
     signal = jnp.dot(inverse, solved, precision=highest)
+    signal = signal.reshape(total, -1, lane)
     returned = lax.all_to_all(signal, "tm", 0, 0, tiled=True)
     returned = returned.reshape(tiles, rows, span).transpose(1, 0, 2)
     return returned.reshape(steps_dev, rows, cols)

time: 62.6 us -> 61.5 us (0.982)
  local copies, waits for them, and re-layouts: 16.5 us -> 15.4 us
  other arithmetic: 2.87 us -> 2.24 us
    all_to_all x2 -> x0, local copies, waits for them, and re-layouts: 2.35 us -> none  [the longest x1 2.08 us: body(): gathered = lax.all_to_all(sent, 'tm', 0, 0, tiled=True)]
    reshape x0 -> x1, local copies, waits for them, and re-layouts: none -> 1.26 us  [body(): column_tiles(wide_side, tiles, width, margin).reshape(tiles, -1, lane)]
    unnamed x16 -> x17, local copies, waits for them, and re-layouts: 2.33 us -> 2.38 us
where the time goes in v7:
time: 61.5 us; the launch traced here: 60.7 us
  local copies, waits for them, and re-layouts  15.4 us (25%)
  starting transfers between devices  15.4 us (25%)
  blocking collectives  12.4 us (20%)
  waiting for transfers between devices  7.3 us (12%)
  Pallas kernels  6.45 us (10%)
  other arithmetic  2.24 us (4%)
  matrix products  1.16 us (2%)
    all_to_all x1, blocking collectives, body(): returned = lax.all_to_all(signal, 'tm', 0, 0, tiled=True)  12.4 us
    all_to_all x1, starting transfers between devices, body(): lax.all_to_all(sent, 'tm', 0, 0, tiled=True)  8.72 us
    pallas_call x1, Pallas kernels, solve_slots(): pl.pallas_call(solve_kernel, out_shape=jax.ShapeDtypeStruct(spectrum.shap...  6.45 us
    all_to_all x1, waiting for transfers between devices, body(): lax.all_to_all(sent, 'tm', 0, 0, tiled=True)  6.37 us
    ppermute x1, starting transfers between devices, with_halo(): low = lax.ppermute(joined[:, rows - width:], 'row', forward)  4.76 us
    another operation x10, local copies, waits for them, and re-layouts, body(): jnp.tile(f, (1, half))  3.68 us
    unnamed x17, local copies, waits for them, and re-layouts  2.38 us
    ppermute x1, starting transfers between devices, with_halo(): high = lax.ppermute(joined[:, :width], 'row', backward)  1.92 us
  transfers between devices with their start and end apart: 3, of which 2 were waited for; matrix products, arithmetic and copies ran while one was open for 9% of the time, Pallas kernels for 0%

profile of v7, /device:TPU:97, one launch (start us, length us, event | category | flops | bytes accessed | tf_op | source)
XLA Modules:
  0.0 60.7 jit_solution(13604117631500603750)
XLA Ops:
  0.0 1.1 %copy.32 = f32[64,1024]{0,1:T(8,128)S(1)} copy(f32[64,1024]{1,0:T(8,128)} %param.11) | data formatting | bytes 524288 | tf_op args[1]
  1.2 1.1 %copy.33 = f32[1,64,1024]{1,2,0:T(8,128)S(1)} copy(f32[1,64,1024]{2,1,0:T(8,128)} %param.10) | data formatting | bytes 524288 | tf_op args[0]
  2.3 0.4 slice_maximum_fusion
  2.7 0.3 copy.35
  3.0 1.9 %collective-permute-start.1 = (f32[2,8,1024]{2,1,0:T(8,128)S(1)}, f32[2,8,1024]{2,1,0:T(8,128)S(1)}, u32[]{:S(2)}, u32[]{:S(2)}) collective-permute-start(f32[2,8,1024]{2,1,0:T(8,128)S(1)} %copy.35), channel_id=1, source_target_pairs={{1,0},{2,1},{3,2},{4,3},{5,4},{6,5},{7,6},{9,8},{10,9},{11,10},{12... | collective-permute-start | bytes 196616 | tf_op jit(solution)/shard_map/ppermute | solution.py:37
  4.9 0.3 copy.34
  5.2 4.8 %collective-permute-start = (f32[2,8,1024]{2,1,0:T(8,128)S(1)}, f32[2,8,1024]{2,1,0:T(8,128)S(1)}, u32[]{:S(2)}, u32[]{:S(2)}) collective-permute-start(f32[2,8,1024]{2,1,0:T(8,128)S(1)} %copy.34), channel_id=1, source_target_pairs={{0,1},{1,2},{2,3},{3,4},{4,5},{5,6},{6,7},{8,9},{9,10},{10,11},{11... | collective-permute-start | bytes 196616 | tf_op jit(solution)/shard_map/ppermute | solution.py:36
  10.0 0.0 collective-permute-done.1
  10.0 0.3 copy.37
  10.3 0.9 %collective-permute-done = f32[2,8,1024]{2,1,0:T(8,128)S(1)} collective-permute-done((f32[2,8,1024]{2,1,0:T(8,128)S(1)}, f32[2,8,1024]{2,1,0:T(8,128)S(1)}, u32[]{:S(2)}, u32[]{:S(2)}) %collective-permute-start) | collective-permute-done | bytes 65568 | tf_op jit(solution)/shard_map/ppermute | solution.py:36
  11.3 0.3 copy.36
  11.6 0.6 %pad_maximum_fusion.1 = f32[2,80,1024]{1,2,0:T(8,128)S(1)} fusion(f32[2,8,1024]{1,2,0:T(8,128)S(1)} %copy.37, f32[1,64,1024]{1,2,0:T(8,128)S(1)} %bitcast.36, f32[1,64,1024]{1,2,0:T(8,128)S(1)} %copy.33, f32[2,8,1024]{1,2,0:T(8,128)S(1)} %copy.36), kind=kLoop, calls=%fused_computation.3 | loop fusion | flops 491520 | bytes 1310720 | tf_op jit(solution)/shard_map/concatenate | solution.py:38
  12.2 0.1 slice_bitcast_fusion.1
  12.3 0.1 pad_slice_fusion.1
  12.4 0.1 maximum_bitcast_fusion
  12.5 0.4 copy.38
  12.9 1.3 %reshape.98 = f32[32,30,128]{2,1,0:T(8,128)} reshape(f32[32,80,48]{2,1,0:T(8,128)S(1)} %copy.38) | data formatting | bytes 983040 | tf_op jit(solution)/shard_map/reshape | solution.py:173
  14.1 8.7 %all-to-all-start = ((f32[32,30,128]{2,1,0:T(8,128)}), f32[32,30,128]{2,1,0:T(8,128)S(1)}, u32[]{:S(2)}, u32[]{:S(2)}) async-start(f32[32,30,128]{2,1,0:T(8,128)} %reshape.98), calls=%async_computation | async-start | bytes 1048576 | tf_op jit(solution)/shard_map/all_to_all | solution.py:174
  22.9 0.1 broadcast_and_fusion
  23.0 0.2 copy.41
  23.1 0.2 add_add_fusion
  23.3 0.8 %copy.46.north_ref = f32[80,768]{1,0:T(8,128)} copy(f32[80,768]{0,1:T(8,128)S(1)} %bitcast.43) | data formatting | bytes 491520 | tf_op jit(solution)/shard_map/tile | solution.py:183
  24.2 0.9 %copy.47.south_ref = f32[80,768]{1,0:T(8,128)} copy(f32[80,768]{0,1:T(8,128)S(1)} %bitcast.44) | data formatting | bytes 491520 | tf_op jit(solution)/shard_map/tile | solution.py:183
  25.1 0.0 copy-start.3
  25.1 0.0 copy-start.4
  25.1 0.0 copy-start.5
  25.1 0.0 copy-start.6
  25.2 0.8 %copy.48.east_ref = f32[80,768]{1,0:T(8,128)} copy(f32[80,768]{0,1:T(8,128)S(1)} %bitcast.45) | data formatting | bytes 491520 | tf_op jit(solution)/shard_map/tile | solution.py:183
  26.0 0.0 copy-start.1
  26.1 0.8 %copy.49.west_ref = f32[80,768]{1,0:T(8,128)} copy(f32[80,768]{0,1:T(8,128)S(1)} %bitcast.46) | data formatting | bytes 491520 | tf_op jit(solution)/shard_map/tile | solution.py:183
  26.9 0.1 copy.50.diag_ref
  27.1 0.0 copy-done.3
  27.1 0.0 copy-done.4
  27.1 0.0 copy-done.5
  27.1 0.0 copy-done.6
  27.1 0.0 copy-start
  27.1 1.0 %divide_select_fusion = (f32[80,768]{1,0:T(8,128)}, f32[80,768]{1,0:T(8,128)}, f32[80,768]{1,0:T(8,128)}) fusion(pred[80,768]{1,0:T(8,128)(4,1)S(1)} %copy.41, f32[80,768]{1,0:T(8,128)S(1)} %copy.50.diag_ref, f32[768]{0:T(1024)S(1)} %copy-done.3, f32[768]{0:T(1024)S(1)} %copy-done.4, f32[768]{0:T(1024)S(1)} %copy-done.5, f32[768]{0:T(1024)S(1)} %copy-done.6), kind=kLoop, calls=%fused_computation.18 | loop fusion | flops 737280 | bytes 1056768 | tf_op jit(solution)/shard_map/jit(_where)/select_n | solution.py:148
  28.1 6.4 %all-to-all-done = f32[32,30,128]{2,1,0:T(8,128)S(1)} async-done(((f32[32,30,128]{2,1,0:T(8,128)}), f32[32,30,128]{2,1,0:T(8,128)S(1)}, u32[]{:S(2)}, u32[]{:S(2)}) %all-to-all-start) | async-done | bytes 491552 | tf_op jit(solution)/shard_map/all_to_all | solution.py:174
  34.5 0.0 copy-done.1
  34.5 0.8 %fusion = f32[32,3840]{1,0:T(8,128)S(1)} fusion(f32[32,32]{1,0:T(8,128)S(1)} %copy-done.1, f32[4,8,30,128]{3,2,1,0:T(8,128)S(1)} %bitcast.42), kind=kOutput, calls=%fused_computation.10 | convolution fusion | flops 47185920 | bytes 987136 | tf_op jit(solution)/shard_map/dot_general | solution.py:175
  35.3 0.8 %reshape.100 = f32[2,16,80,48]{3,2,1,0:T(8,128)S(1)} reshape(f32[32,3840]{1,0:T(8,128)S(1)} %fusion) | data formatting | bytes 983040 | tf_op jit(solution)/shard_map/reshape | solution.py:176
  36.1 0.0 copy-done
  36.1 0.4 copy.39
  36.5 1.1 %copy.45.spec_ref = f32[2,80,768]{2,1,0:T(8,128)} copy(f32[2,80,768]{1,2,0:T(8,128)S(1)} %bitcast.38) | data formatting | bytes 983040 | tf_op jit(solution)/shard_map/reshape | solution.py:177
  37.6 6.5 %shard_map.100 = f32[2,80,768]{2,1,0:T(8,128)} custom-call(f32[2,80,768]{2,1,0:T(8,128)} %copy.45.spec_ref, f32[80,768]{1,0:T(8,128)} %copy.46.north_ref, f32[80,768]{1,0:T(8,128)} %copy.47.south_ref, f32[80,768]{1,0:T(8,128)} %copy.48.east_ref, f32[80,768]{1,0:T(8,128)} %copy.49.west_ref, f32[80,768]{1,0:T(8,128)} %copy-done, ...), custom_call_target="tpu_custom_call" | custom-call | tf_op jit(solution)/shard_map/pallas_call | solution.py:152
  44.0 1.3 %copy.51 = f32[2,80,768]{1,2,0:T(8,128)S(1)} copy(f32[2,80,768]{2,1,0:T(8,128)} %shard_map.100) | data formatting | bytes 983040 | tf_op jit(solution)/shard_map/pallas_call | solution.py:152
  45.3 0.2 slice_bitcast_fusion
  45.5 0.0 copy-start.2
  45.5 0.4 copy.52
  45.9 0.5 reshape.103
  46.4 0.0 copy-done.2
  46.4 0.4 convolution_bitcast_fusion
  46.8 12.4 %all_to_all.10 = f32[32,16,128]{2,1,0:T(8,128)S(1)} all-to-all(f32[32,16,128]{2,1,0:T(8,128)S(1)} %bitcast.49), channel_id=1, replica_groups=mesh['tm'=32,'row'=8] {'tm'}, dimensions={0} | all-to-all | bytes 524288 | tf_op jit(solution)/shard_map/all_to_all | solution.py:191
  59.2 0.3 reshape.105
  59.5 0.3 copy.53
  59.8 0.9 %copy.54 = f32[1,64,1024]{2,1,0:T(8,128)} copy(f32[1,64,1024]{1,2,0:T(8,128)S(1)} %bitcast.41) | data formatting | bytes 524288 | tf_op jit(solution)/shard_map/reshape | solution.py:193
  (10 shorter events, 0.2 us)
Async XLA Ops:
  3.0 7.0 %collective-permute-start.1 = (f32[2,8,1024]{2,1,0:T(8,128)S(1)}, f32[2,8,1024]{2,1,0:T(8,128)S(1)}, u32[]{:S(2)}, u32[]{:S(2)}) collective-permute-start(f32[2,8,1024]{2,1,0:T(8,128)S(1)} %copy.35), channel_id=1, source_target_pairs={{1,0},{2,1},{3,2},{4,3},{5,4},{6,5},{7,6},{9,8},{10,9},{11,10},{12... | collective-permute-start | bytes 196616 | tf_op jit(solution)/shard_map/ppermute | solution.py:37
  5.2 6.1 %collective-permute-start = (f32[2,8,1024]{2,1,0:T(8,128)S(1)}, f32[2,8,1024]{2,1,0:T(8,128)S(1)}, u32[]{:S(2)}, u32[]{:S(2)}) collective-permute-start(f32[2,8,1024]{2,1,0:T(8,128)S(1)} %copy.34), channel_id=1, source_target_pairs={{0,1},{1,2},{2,3},{3,4},{4,5},{5,6},{6,7},{8,9},{9,10},{10,11},{11... | collective-permute-start | bytes 196616 | tf_op jit(solution)/shard_map/ppermute | solution.py:36
  14.1 20.3 %all-to-all-start = ((f32[32,30,128]{2,1,0:T(8,128)}), f32[32,30,128]{2,1,0:T(8,128)S(1)}, u32[]{:S(2)}, u32[]{:S(2)}) async-start(f32[32,30,128]{2,1,0:T(8,128)} %reshape.98), calls=%async_computation | async-start | bytes 1048576 | tf_op jit(solution)/shard_map/all_to_all | solution.py:174
  25.1 2.0 %copy-start.3 = (f32[768]{0:T(1024)S(1)}, f32[768]{0:T(1024)}, u32[]{:S(2)}) copy-start(f32[768]{0:T(1024)} %constant.63) | copy-start | bytes 9220
  25.1 2.0 %copy-start.4 = (f32[768]{0:T(1024)S(1)}, f32[768]{0:T(1024)}, u32[]{:S(2)}) copy-start(f32[768]{0:T(1024)} %constant.61) | copy-start | bytes 9220
  25.1 2.0 %copy-start.5 = (f32[768]{0:T(1024)S(1)}, f32[768]{0:T(1024)}, u32[]{:S(2)}) copy-start(f32[768]{0:T(1024)} %constant.60) | copy-start | bytes 9220
  25.1 2.0 %copy-start.6 = (f32[768]{0:T(1024)S(1)}, f32[768]{0:T(1024)}, u32[]{:S(2)}) copy-start(f32[768]{0:T(1024)} %constant.62) | copy-start | bytes 9220
  26.0 8.4 %copy-start.1 = (f32[32,32]{1,0:T(8,128)S(1)}, f32[32,32]{1,0:T(8,128)}, u32[]{:S(2)}) copy-start(f32[32,32]{1,0:T(8,128)} %constant.48.clone) | copy-start | bytes 12292
  27.1 9.0 %copy-start = (f32[80,768]{1,0:T(8,128)}, f32[80,768]{1,0:T(8,128)S(1)}, u32[]{:S(2)}) copy-start(f32[80,768]{1,0:T(8,128)S(1)} %copy.50.diag_ref) | copy-start | bytes 737284
  45.5 0.9 %copy-start.2 = (f32[32,32]{1,0:T(8,128)S(1)}, f32[32,32]{1,0:T(8,128)}, u32[]{:S(2)}) copy-start(f32[32,32]{1,0:T(8,128)} %constant.54.clone) | copy-start | bytes 12292

commit v8 on v7

--- a/solution.py
+++ b/solution.py
@@ -98,18 +98,17 @@
     return jnp.concatenate([main, extra], axis=2).transpose(1, 0, 2)
 
 
-def solve_kernel(spec_ref, north_ref, south_ref, east_ref, west_ref, diag_ref,
-                 inva_ref, invb_ref, invi_ref, reala_ref, realb_ref, imag_ref, out_ref):
+def solve_kernel(spec_ref, north_ref, south_ref, east_ref, west_ref, diag_a_ref, diag_b_ref,
+                 inva_ref, invb_ref, invi_ref, imag_ref, out_ref):
     rows, lanes = north_ref.shape
 
-    def spatial(x):
+    def coupled(x):
         above = pltpu.roll(x, rows - 1, 0)
         below = pltpu.roll(x, 1, 0)
         after = pltpu.roll(x, lanes - 1, 1)
         before = pltpu.roll(x, 1, 1)
-        coupled = (north_ref[...] * above + south_ref[...] * below
-                   + east_ref[...] * after + west_ref[...] * before)
-        return diag_ref[...] * x - coupled - courant_rows * below - courant_cols * before
+        return (north_ref[...] * above + south_ref[...] * below
+                + east_ref[...] * after + west_ref[...] * before)
 
     first = True
     for sweep in range(SWEEPS):
@@ -120,10 +119,10 @@
             else:
                 state_real = out_ref[0]
                 state_imag = out_ref[1]
-                image_real = (reala_ref[...] * state_real - imag_ref[...] * state_imag
-                              + spatial(state_real))
-                image_imag = (realb_ref[...] * state_imag + imag_ref[...] * state_real
-                              + spatial(state_imag))
+                image_real = (diag_a_ref[...] * state_real - imag_ref[...] * state_imag
+                              - coupled(state_real))
+                image_imag = (diag_b_ref[...] * state_imag + imag_ref[...] * state_real
+                              - coupled(state_imag))
                 res_real = spec_ref[0] - image_real
                 res_imag = spec_ref[1] - image_imag
             corr_real = inva_ref[...] * res_real - invi_ref[...] * res_imag
@@ -138,17 +137,17 @@
 
 
 def solve_slots(spectrum, faces, shifts, inside):
+    north, south, east, west, diagonal = faces
     real_a, real_b, imag = shifts
-    diag_a = real_a + faces[4]
-    diag_b = real_b + faces[4]
+    diag_a = real_a + diagonal
+    diag_b = real_b + diagonal
     mag_a = diag_a * diag_a + imag * imag
     mag_b = diag_b * diag_b + imag * imag
     inv_a = jnp.where(inside, diag_a / mag_a, 0.0)
     inv_b = jnp.where(inside, diag_b / mag_b, 0.0)
     inv_imag = jnp.where(inside, -imag / mag_a, 0.0)
-    operands = (spectrum,) + tuple(faces) + (inv_a, inv_b, inv_imag) + tuple(
-        jnp.asarray(s) for s in shifts
-    )
+    operands = (spectrum, north, south + courant_rows, east, west + courant_cols,
+                diag_a, diag_b, inv_a, inv_b, inv_imag, jnp.asarray(imag))
     return pl.pallas_call(
         solve_kernel,
         out_shape=jax.ShapeDtypeStruct(spectrum.shape, spectrum.dtype),

time: 61.5 us -> 61.1 us (level)
    add x0 -> x2, local copies, waits for them, and re-layouts: none -> 1.7 us  [the longest x1 0.86 us: solve_slots(): south + courant_rows]
    another operation x10 -> x8, local copies, waits for them, and re-layouts: 3.68 us -> 1.98 us  [body(): jnp.tile(f, (1, half))]
    unnamed x17 -> x15, local copies, waits for them, and re-layouts: 2.38 us -> 2.38 us
  transfers between devices with their start and end apart: 3 -> 3, of which waited for: 2 -> 2; matrix products, arithmetic and copies ran while one was open for 9% -> 10% of each run, Pallas kernels for 0% -> 0%
where the time goes in v8:
time: 61.1 us; the launch traced here: 60.2 us
  local copies, waits for them, and re-layouts  15.4 us (25%)
  starting transfers between devices  15.4 us (25%)
  blocking collectives  12.4 us (20%)
  waiting for transfers between devices  7.11 us (12%)
  Pallas kernels  5.98 us (10%)
  other arithmetic  2.45 us (4%)
  matrix products  1.16 us (2%)
    all_to_all x1, blocking collectives, body(): returned = lax.all_to_all(signal, 'tm', 0, 0, tiled=True)  12.4 us
    all_to_all x1, starting transfers between devices, body(): lax.all_to_all(sent, 'tm', 0, 0, tiled=True)  8.71 us
    all_to_all x1, waiting for transfers between devices, body(): lax.all_to_all(sent, 'tm', 0, 0, tiled=True)  6.18 us
    pallas_call x1, Pallas kernels, solve_slots(): pl.pallas_call(solve_kernel, out_shape=jax.ShapeDtypeStruct(spectrum.shap...  5.98 us
    ppermute x1, starting transfers between devices, with_halo(): low = lax.ppermute(joined[:, rows - width:], 'row', forward)  4.76 us
    unnamed x15, local copies, waits for them, and re-layouts  2.38 us
    another operation x8, local copies, waits for them, and re-layouts, body(): jnp.tile(f, (1, half))  1.98 us
    ppermute x1, starting transfers between devices, with_halo(): high = lax.ppermute(joined[:, :width], 'row', backward)  1.92 us
  transfers between devices with their start and end apart: 3, of which 2 were waited for; matrix products, arithmetic and copies ran while one was open for 10% of the time, Pallas kernels for 0%

profile of v8, /device:TPU:97, one launch (start us, length us, event | category | flops | bytes accessed | tf_op | source)
XLA Modules:
  0.0 60.2 jit_solution(12617509993373869771)
XLA Ops:
  0.0 1.1 %copy.31 = f32[64,1024]{0,1:T(8,128)S(1)} copy(f32[64,1024]{1,0:T(8,128)} %param.11) | data formatting | bytes 524288 | tf_op args[1]
  1.2 1.1 %copy.32 = f32[1,64,1024]{1,2,0:T(8,128)S(1)} copy(f32[1,64,1024]{2,1,0:T(8,128)} %param.10) | data formatting | bytes 524288 | tf_op args[0]
  2.3 0.4 slice_maximum_fusion
  2.7 0.3 copy.34
  3.0 1.9 %collective-permute-start.1 = (f32[2,8,1024]{2,1,0:T(8,128)S(1)}, f32[2,8,1024]{2,1,0:T(8,128)S(1)}, u32[]{:S(2)}, u32[]{:S(2)}) collective-permute-start(f32[2,8,1024]{2,1,0:T(8,128)S(1)} %copy.34), channel_id=1, source_target_pairs={{1,0},{2,1},{3,2},{4,3},{5,4},{6,5},{7,6},{9,8},{10,9},{11,10},{12... | collective-permute-start | bytes 196616 | tf_op jit(solution)/shard_map/ppermute | solution.py:37
  4.9 0.3 copy.33
  5.2 4.8 %collective-permute-start = (f32[2,8,1024]{2,1,0:T(8,128)S(1)}, f32[2,8,1024]{2,1,0:T(8,128)S(1)}, u32[]{:S(2)}, u32[]{:S(2)}) collective-permute-start(f32[2,8,1024]{2,1,0:T(8,128)S(1)} %copy.33), channel_id=1, source_target_pairs={{0,1},{1,2},{2,3},{3,4},{4,5},{5,6},{6,7},{8,9},{9,10},{10,11},{11... | collective-permute-start | bytes 196616 | tf_op jit(solution)/shard_map/ppermute | solution.py:36
  10.0 0.0 collective-permute-done.1
  10.0 0.3 copy.36
  10.3 0.9 %collective-permute-done = f32[2,8,1024]{2,1,0:T(8,128)S(1)} collective-permute-done((f32[2,8,1024]{2,1,0:T(8,128)S(1)}, f32[2,8,1024]{2,1,0:T(8,128)S(1)}, u32[]{:S(2)}, u32[]{:S(2)}) %collective-permute-start) | collective-permute-done | bytes 65568 | tf_op jit(solution)/shard_map/ppermute | solution.py:36
  11.3 0.3 copy.35
  11.6 0.6 %pad_maximum_fusion.1 = f32[2,80,1024]{1,2,0:T(8,128)S(1)} fusion(f32[2,8,1024]{1,2,0:T(8,128)S(1)} %copy.36, f32[1,64,1024]{1,2,0:T(8,128)S(1)} %bitcast.36, f32[1,64,1024]{1,2,0:T(8,128)S(1)} %copy.32, f32[2,8,1024]{1,2,0:T(8,128)S(1)} %copy.35), kind=kLoop, calls=%fused_computation.3 | loop fusion | flops 491520 | bytes 1310720 | tf_op jit(solution)/shard_map/concatenate | solution.py:38
  12.2 0.1 slice_bitcast_fusion.1
  12.3 0.1 pad_slice_fusion.1
  12.4 0.1 maximum_bitcast_fusion
  12.5 0.4 copy.37
  12.9 1.3 %reshape.102 = f32[32,30,128]{2,1,0:T(8,128)} reshape(f32[32,80,48]{2,1,0:T(8,128)S(1)} %copy.37) | data formatting | bytes 983040 | tf_op jit(solution)/shard_map/reshape | solution.py:172
  14.1 8.7 %all-to-all-start = ((f32[32,30,128]{2,1,0:T(8,128)}), f32[32,30,128]{2,1,0:T(8,128)S(1)}, u32[]{:S(2)}, u32[]{:S(2)}) async-start(f32[32,30,128]{2,1,0:T(8,128)} %reshape.102), calls=%async_computation | async-start | bytes 1048576 | tf_op jit(solution)/shard_map/all_to_all | solution.py:173
  22.8 0.1 broadcast_and_fusion
  23.0 0.2 copy.41
  23.1 0.2 broadcast_add_fusion.2
  23.4 0.8 %copy.45.north_ref = f32[80,768]{1,0:T(8,128)} copy(f32[80,768]{0,1:T(8,128)S(1)} %bitcast.43) | data formatting | bytes 491520 | tf_op jit(solution)/shard_map/tile | solution.py:182
  24.2 0.9 %copy.46.south_ref = f32[80,768]{1,0:T(8,128)} copy(f32[80,768]{0,1:T(8,128)S(1)} %bitcast.44) | data formatting | bytes 491520 | tf_op jit(solution)/shard_map/add | solution.py:149
  25.1 0.0 copy-start.2
  25.1 0.0 copy-start.3
  25.2 0.0 copy-start.4
  25.2 0.0 copy-start.5
  25.2 0.8 %copy.47.east_ref = f32[80,768]{1,0:T(8,128)} copy(f32[80,768]{0,1:T(8,128)S(1)} %bitcast.45) | data formatting | bytes 491520 | tf_op jit(solution)/shard_map/tile | solution.py:182
  26.1 0.8 %copy.48.west_ref = f32[80,768]{1,0:T(8,128)} copy(f32[80,768]{0,1:T(8,128)S(1)} %bitcast.46) | data formatting | bytes 491520 | tf_op jit(solution)/shard_map/add | solution.py:149
  26.9 0.0 copy-start
  26.9 0.1 copy.39
  27.1 0.0 copy-done.2
  27.1 0.0 copy-done.3
  27.1 0.0 copy-done.4
  27.1 0.0 copy-done.5
  27.1 1.2 %divide_select_fusion = (f32[80,768]{1,0:T(8,128)}, f32[80,768]{1,0:T(8,128)}, f32[80,768]{1,0:T(8,128)}, f32[80,768]{1,0:T(8,128)}, f32[80,768]{1,0:T(8,128)}) fusion(pred[80,768]{1,0:T(8,128)(4,1)S(1)} %copy.41, f32[768]{0:T(1024)S(1)} %copy-done.2, f32[768]{0:T(1024)S(1)} %copy-done.3, f32[80,768]{1,0:T(8,128)S(1)} %copy.39, f32[768]{0:T(1024)S(1)} %copy-done.4, ...), kind=kLoop, calls=%fused_computation.18 | loop fusion | flops 737280 | bytes 1548288 | tf_op jit(solution)/shard_map/jit(_where)/select_n | solution.py:148
  28.3 6.2 %all-to-all-done = f32[32,30,128]{2,1,0:T(8,128)S(1)} async-done(((f32[32,30,128]{2,1,0:T(8,128)}), f32[32,30,128]{2,1,0:T(8,128)S(1)}, u32[]{:S(2)}, u32[]{:S(2)}) %all-to-all-start) | async-done | bytes 491552 | tf_op jit(solution)/shard_map/all_to_all | solution.py:173
  34.5 0.0 copy-done
  34.5 0.8 %fusion = f32[32,3840]{1,0:T(8,128)S(1)} fusion(f32[32,32]{1,0:T(8,128)S(1)} %copy-done, f32[4,8,30,128]{3,2,1,0:T(8,128)S(1)} %bitcast.42), kind=kOutput, calls=%fused_computation.10 | convolution fusion | flops 47185920 | bytes 987136 | tf_op jit(solution)/shard_map/dot_general | solution.py:174
  35.3 0.8 %reshape.104 = f32[2,16,80,48]{3,2,1,0:T(8,128)S(1)} reshape(f32[32,3840]{1,0:T(8,128)S(1)} %fusion) | data formatting | bytes 983040 | tf_op jit(solution)/shard_map/reshape | solution.py:175
  36.1 0.4 copy.38
  36.5 1.1 %copy.44.spec_ref = f32[2,80,768]{2,1,0:T(8,128)} copy(f32[2,80,768]{1,2,0:T(8,128)S(1)} %bitcast.38) | data formatting | bytes 983040 | tf_op jit(solution)/shard_map/reshape | solution.py:176
  37.5 6.0 %shard_map.100 = f32[2,80,768]{2,1,0:T(8,128)} custom-call(f32[2,80,768]{2,1,0:T(8,128)} %copy.44.spec_ref, f32[80,768]{1,0:T(8,128)} %copy.45.north_ref, f32[80,768]{1,0:T(8,128)} %copy.46.south_ref, f32[80,768]{1,0:T(8,128)} %copy.47.east_ref, f32[80,768]{1,0:T(8,128)} %copy.48.west_ref, f32[80,768]{1,0:T(8,128)} %get-tuple-element.23.diag_a_ref, ...), custom_call_target="tpu_custom_call" | custom-call | tf_op jit(solution)/shard_map/pallas_call | solution.py:151
  43.5 1.3 %copy.49 = f32[2,80,768]{1,2,0:T(8,128)S(1)} copy(f32[2,80,768]{2,1,0:T(8,128)} %shard_map.100) | data formatting | bytes 983040 | tf_op jit(solution)/shard_map/pallas_call | solution.py:151
  44.8 0.2 slice_bitcast_fusion
  45.0 0.0 copy-start.1
  45.0 0.4 copy.50
  45.4 0.5 reshape.107
  45.9 0.0 copy-done.1
  45.9 0.4 convolution_bitcast_fusion
  46.3 12.4 %all_to_all.10 = f32[32,16,128]{2,1,0:T(8,128)S(1)} all-to-all(f32[32,16,128]{2,1,0:T(8,128)S(1)} %bitcast.49), channel_id=1, replica_groups=mesh['tm'=32,'row'=8] {'tm'}, dimensions={0} | all-to-all | bytes 524288 | tf_op jit(solution)/shard_map/all_to_all | solution.py:190
  58.7 0.3 reshape.109
  59.0 0.3 copy.51
  59.3 0.9 %copy.52 = f32[1,64,1024]{2,1,0:T(8,128)} copy(f32[1,64,1024]{1,2,0:T(8,128)S(1)} %bitcast.41) | data formatting | bytes 524288 | tf_op jit(solution)/shard_map/reshape | solution.py:192
  (10 shorter events, 0.2 us)
Async XLA Ops:
  3.0 7.0 %collective-permute-start.1 = (f32[2,8,1024]{2,1,0:T(8,128)S(1)}, f32[2,8,1024]{2,1,0:T(8,128)S(1)}, u32[]{:S(2)}, u32[]{:S(2)}) collective-permute-start(f32[2,8,1024]{2,1,0:T(8,128)S(1)} %copy.34), channel_id=1, source_target_pairs={{1,0},{2,1},{3,2},{4,3},{5,4},{6,5},{7,6},{9,8},{10,9},{11,10},{12... | collective-permute-start | bytes 196616 | tf_op jit(solution)/shard_map/ppermute | solution.py:37
  5.2 6.1 %collective-permute-start = (f32[2,8,1024]{2,1,0:T(8,128)S(1)}, f32[2,8,1024]{2,1,0:T(8,128)S(1)}, u32[]{:S(2)}, u32[]{:S(2)}) collective-permute-start(f32[2,8,1024]{2,1,0:T(8,128)S(1)} %copy.33), channel_id=1, source_target_pairs={{0,1},{1,2},{2,3},{3,4},{4,5},{5,6},{6,7},{8,9},{9,10},{10,11},{11... | collective-permute-start | bytes 196616 | tf_op jit(solution)/shard_map/ppermute | solution.py:36
  14.1 20.3 %all-to-all-start = ((f32[32,30,128]{2,1,0:T(8,128)}), f32[32,30,128]{2,1,0:T(8,128)S(1)}, u32[]{:S(2)}, u32[]{:S(2)}) async-start(f32[32,30,128]{2,1,0:T(8,128)} %reshape.102), calls=%async_computation | async-start | bytes 1048576 | tf_op jit(solution)/shard_map/all_to_all | solution.py:173
  25.1 2.0 %copy-start.2 = (f32[768]{0:T(1024)S(1)}, f32[768]{0:T(1024)}, u32[]{:S(2)}) copy-start(f32[768]{0:T(1024)} %constant.66) | copy-start | bytes 9220
  25.1 2.0 %copy-start.3 = (f32[768]{0:T(1024)S(1)}, f32[768]{0:T(1024)}, u32[]{:S(2)}) copy-start(f32[768]{0:T(1024)} %constant.65) | copy-start | bytes 9220
  25.2 2.0 %copy-start.4 = (f32[768]{0:T(1024)S(1)}, f32[768]{0:T(1024)}, u32[]{:S(2)}) copy-start(f32[768]{0:T(1024)} %constant.63) | copy-start | bytes 9220
  25.2 1.9 %copy-start.5 = (f32[768]{0:T(1024)S(1)}, f32[768]{0:T(1024)}, u32[]{:S(2)}) copy-start(f32[768]{0:T(1024)} %constant.64) | copy-start | bytes 9220
  26.9 7.6 %copy-start = (f32[32,32]{1,0:T(8,128)S(1)}, f32[32,32]{1,0:T(8,128)}, u32[]{:S(2)}) copy-start(f32[32,32]{1,0:T(8,128)} %constant.51.clone) | copy-start | bytes 12292
  45.0 0.9 %copy-start.1 = (f32[32,32]{1,0:T(8,128)S(1)}, f32[32,32]{1,0:T(8,128)}, u32[]{:S(2)}) copy-start(f32[32,32]{1,0:T(8,128)} %constant.57.clone) | copy-start | bytes 12292

commit v9 on v8

--- a/solution.py
+++ b/solution.py
@@ -167,28 +167,35 @@
     forward, inverse = transform_matrices(total)
 
     wide_side, kappa_rows, inside_rows = with_halo(right_side, kappa, margin)
-    extended = rows + 2 * margin
     lane = 128
-    sent = column_tiles(wide_side, tiles, width, margin).reshape(tiles, -1, lane)
-    gathered = lax.all_to_all(sent, "tm", 0, 0, tiled=True).reshape(tiles, extended * width)
-    spectrum = jnp.dot(forward, gathered, precision=highest)
-    spectrum = spectrum.reshape(2, half, extended, width).transpose(0, 2, 1, 3)
-    spectrum = spectrum.reshape(2, extended, half * width)
+    tiled = column_tiles(wide_side, tiles, width, margin)
 
     place = tile * span - margin + jnp.arange(width)
     inside_cols = (place >= 0) & (place < cols)
-    inside = inside_rows[:, None] & inside_cols[None, :]
-    inside = jnp.tile(inside, (1, half))
+    inside = jnp.tile(inside_rows[:, None] & inside_cols[None, :], (1, half))
     faces = tuple(jnp.tile(f, (1, half)) for f in tile_faces(kappa_rows, tile, tiles, width, margin))
     shifts = slot_shifts(half, total, width)
-    solved = solve_slots(spectrum, faces, shifts, inside)
-
-    solved = solved.reshape(2, extended, half, width)[:, margin : margin + rows, :, margin : margin + span]
-    solved = solved.transpose(0, 2, 1, 3).reshape(total, rows * span)
-    signal = jnp.dot(inverse, solved, precision=highest)
-    signal = signal.reshape(total, -1, lane)
-    returned = lax.all_to_all(signal, "tm", 0, 0, tiled=True)
-    returned = returned.reshape(tiles, rows, span).transpose(1, 0, 2)
+
+    stages = 2
+    inner = rows // stages
+    depth = inner + 2 * margin
+    sent = [tiled[:, s * inner : s * inner + depth].reshape(tiles, -1, lane) for s in range(stages)]
+    gathered = [lax.all_to_all(x, "tm", 0, 0, tiled=True) for x in sent]
+    outputs = []
+    for s in range(stages):
+        window = slice(s * inner, s * inner + depth)
+        spectrum = jnp.dot(forward, gathered[s].reshape(tiles, depth * width), precision=highest)
+        spectrum = spectrum.reshape(2, half, depth, width).transpose(0, 2, 1, 3)
+        spectrum = spectrum.reshape(2, depth, half * width)
+        solved = solve_slots(
+            spectrum, tuple(f[window] for f in faces), shifts, inside[window]
+        )
+        solved = solved.reshape(2, depth, half, width)[:, margin : margin + inner, :, margin : margin + span]
+        solved = solved.transpose(0, 2, 1, 3).reshape(total, inner * span)
+        signal = jnp.dot(inverse, solved, precision=highest).reshape(total, -1, lane)
+        returned = lax.all_to_all(signal, "tm", 0, 0, tiled=True)
+        outputs.append(returned.reshape(tiles, inner, span))
+    returned = jnp.concatenate(outputs, axis=1).transpose(1, 0, 2)
     return returned.reshape(steps_dev, rows, cols)
 
 

time: 61.1 us -> 85.5 us (1.40)
  starting transfers between devices: 15.4 us -> 37.3 us
  blocking collectives: 12.4 us -> 0 us
  local copies, waits for them, and re-layouts: 15.4 us -> 25.8 us
  Pallas kernels: 5.98 us -> 8.6 us
  waiting for transfers between devices: 7.11 us -> 8.28 us
    all_to_all x1 -> x4, starting transfers between devices: 8.71 us -> 30.6 us  [the longest x2 16.2 us: body(): gathered = [lax.all_to_all(x, 'tm', 0, 0, tiled=True) for x in sent]]
    all_to_all x1 -> x0, blocking collectives: 12.4 us -> none  [body(): returned = lax.all_to_all(signal, 'tm', 0, 0, tiled=True)]
    reshape x5 -> x14, local copies, waits for them, and re-layouts: 3.89 us -> 9.64 us  [the longest x2 2.71 us: body(): solved.reshape(2, depth, half, width)]
    pallas_call x1 -> x2, Pallas kernels: 5.98 us -> 8.6 us  [solve_slots(): pl.pallas_call(solve_kernel, out_shape=jax.ShapeDtypeStruct(spectrum.shap...]
    another operation x8 -> x16, local copies, waits for them, and re-layouts: 1.98 us -> 4.06 us  [body(): jnp.tile(f, (1, half))]
    slice x0 -> x14, local copies, waits for them, and re-layouts: none -> 1.78 us  [the longest x3 0.79 us: body(): tiled[:, s * inner:s * inner + depth].reshape(tiles, -1, lane)]
    all_to_all x1 -> x4, waiting for transfers between devices: 6.18 us -> 7.95 us  [the longest x2 7.53 us: body(): returned = lax.all_to_all(signal, 'tm', 0, 0, tiled=True)]
    transpose x5 -> x1, local copies, waits for them, and re-layouts: 1.67 us -> 0.32 us  [body(): returned = jnp.concatenate(outputs, axis=1).transpose(1, 0, 2)]
  transfers between devices with their start and end apart: 3 -> 6, of which waited for: 2 -> 3; matrix products, arithmetic and copies ran while one was open for 10% -> 27% of each run, Pallas kernels for 0% -> 10%
where the time goes in v9:
time: 85.5 us; the launch traced here: 84.4 us
  starting transfers between devices  37.3 us (44%)
  local copies, waits for them, and re-layouts  25.8 us (30%)
  Pallas kernels  8.6 us (10%)
  waiting for transfers between devices  8.28 us (10%)
  other arithmetic  2.64 us (3%)
  matrix products  1.29 us (2%)
    all_to_all x2, starting transfers between devices, body(): gathered = [lax.all_to_all(x, 'tm', 0, 0, tiled=True) for x in sent]  16.2 us
    all_to_all x2, starting transfers between devices, body(): returned = lax.all_to_all(signal, 'tm', 0, 0, tiled=True)  14.3 us
    pallas_call x2, Pallas kernels, solve_slots(): pl.pallas_call(solve_kernel, out_shape=jax.ShapeDtypeStruct(spectrum.shap...  8.6 us
    all_to_all x2, waiting for transfers between devices, body(): returned = lax.all_to_all(signal, 'tm', 0, 0, tiled=True)  7.53 us
    ppermute x1, starting transfers between devices, with_halo(): low = lax.ppermute(joined[:, rows - width:], 'row', forward)  4.76 us
    another operation x16, local copies, waits for them, and re-layouts, body(): jnp.tile(f, (1, half))  4.06 us
    unnamed x20, local copies, waits for them, and re-layouts  3.56 us
    reshape x2, local copies, waits for them, and re-layouts, body(): solved.reshape(2, depth, half, width)  2.71 us
  transfers between devices with their start and end apart: 6, of which 3 were waited for; matrix products, arithmetic and copies ran while one was open for 27% of the time, Pallas kernels for 10%

profile of v9, /device:TPU:97, one launch (start us, length us, event | category | flops | bytes accessed | tf_op | source)
XLA Modules:
  0.0 84.4 jit_solution(1913340782501525015)
XLA Ops:
  0.0 1.2 %copy.57 = f32[64,1024]{0,1:T(8,128)S(1)} copy(f32[64,1024]{1,0:T(8,128)} %param.14) | data formatting | bytes 524288 | tf_op args[1]
  1.2 0.2 copy.58
  1.4 0.4 slice_maximum_fusion
  1.8 0.3 copy.60
  2.1 1.9 %collective-permute-start.1 = (f32[2,8,1024]{2,1,0:T(8,128)S(1)}, f32[2,8,1024]{2,1,0:T(8,128)S(1)}, u32[]{:S(2)}, u32[]{:S(2)}) collective-permute-start(f32[2,8,1024]{2,1,0:T(8,128)S(1)} %copy.60), channel_id=1, source_target_pairs={{1,0},{2,1},{3,2},{4,3},{5,4},{6,5},{7,6},{9,8},{10,9},{11,10},{12... | collective-permute-start | bytes 196616 | tf_op jit(solution)/shard_map/ppermute | solution.py:37
  4.0 0.3 copy.59
  4.3 4.8 %collective-permute-start = (f32[2,8,1024]{2,1,0:T(8,128)S(1)}, f32[2,8,1024]{2,1,0:T(8,128)S(1)}, u32[]{:S(2)}, u32[]{:S(2)}) collective-permute-start(f32[2,8,1024]{2,1,0:T(8,128)S(1)} %copy.59), channel_id=1, source_target_pairs={{0,1},{1,2},{2,3},{3,4},{4,5},{5,6},{6,7},{8,9},{9,10},{10,11},{11... | collective-permute-start | bytes 196616 | tf_op jit(solution)/shard_map/ppermute | solution.py:36
  9.2 0.2 tile.89
  9.5 0.2 tile.79
  9.7 0.3 copy.62
  10.0 0.3 collective-permute-done
  10.4 0.3 copy.61
  10.7 0.6 pad_maximum_fusion.1
  11.6 0.3 fusion.18
  11.8 0.3 copy.71
  12.1 1.3 %reshape.176 = f32[32,18,128]{2,1,0:T(8,128)} reshape(f32[32,48,48]{2,1,0:T(8,128)S(1)} %copy.71) | data formatting | bytes 589824 | tf_op jit(solution)/shard_map/reshape | solution.py:182
  13.4 8.7 %all-to-all-start.2 = ((f32[32,18,128]{2,1,0:T(8,128)}), f32[32,18,128]{2,1,0:T(8,128)S(1)}, u32[]{:S(2)}, u32[]{:S(2)}) async-start(f32[32,18,128]{2,1,0:T(8,128)} %reshape.176), calls=%async_computation.2 | async-start | bytes 786432 | tf_op jit(solution)/shard_map/all_to_all | solution.py:183
  22.1 0.2 add_add_fusion
  22.6 0.8 %tile.81.north_ref = f32[48,768]{1,0:T(8,128)} reshape(f32[48,16,48]{2,1,0:T(8,128)S(1)} %tile.80) | data formatting | bytes 294912 | tf_op jit(solution)/shard_map/tile | solution.py:176
  23.6 0.8 add.179.south_ref
  24.5 0.8 tile.84.east_ref
  25.5 0.8 %add.181.west_ref = f32[48,768]{1,0:T(8,128)} reshape(f32[48,16,48]{2,1,0:T(8,128)S(1)} %tile.85) | data formatting | bytes 294912 | tf_op jit(solution)/shard_map/add | solution.py:149
  26.4 0.2 tile.87
  26.7 0.2 tile.77
  26.9 0.3 copy.63
  27.2 1.3 %reshape.168 = f32[32,18,128]{2,1,0:T(8,128)} reshape(f32[32,48,48]{2,1,0:T(8,128)S(1)} %copy.63) | data formatting | bytes 589824 | tf_op jit(solution)/shard_map/reshape | solution.py:182
  28.6 0.8 %tile.71.north_ref = f32[48,768]{1,0:T(8,128)} reshape(f32[48,16,48]{2,1,0:T(8,128)S(1)} %tile.70) | data formatting | bytes 294912 | tf_op jit(solution)/shard_map/tile | solution.py:176
  29.6 0.8 add.152.south_ref
  30.5 0.8 tile.74.east_ref
  31.5 0.8 %add.156.west_ref = f32[48,768]{1,0:T(8,128)} reshape(f32[48,16,48]{2,1,0:T(8,128)S(1)} %tile.75) | data formatting | bytes 294912 | tf_op jit(solution)/shard_map/add | solution.py:149
  32.4 1.2 %divide_select_fusion = (f32[48,768]{1,0:T(8,128)}, f32[48,768]{1,0:T(8,128)}, f32[48,768]{1,0:T(8,128)}, f32[48,768]{1,0:T(8,128)}, f32[48,768]{1,0:T(8,128)}, ...) fusion(pred[48,768]{1,0:T(8,128)(4,1)S(1)} %tile.89, ...), kind=kLoop, calls=%fused_computation.26 | loop fusion | flops 884736 | bytes 1855488 | tf_op jit(solution)/shard_map/jit(_where)/select_n | solution.py:148
  33.6 7.5 %all-to-all-start = ((f32[32,18,128]{2,1,0:T(8,128)}), f32[32,18,128]{2,1,0:T(8,128)S(1)}, u32[]{:S(2)}, u32[]{:S(2)}) async-start(f32[32,18,128]{2,1,0:T(8,128)} %reshape.168), calls=%async_computation | async-start | bytes 786432 | tf_op jit(solution)/shard_map/all_to_all | solution.py:183
  41.1 0.4 fusion
  41.5 0.5 reshape.178
  42.0 0.2 copy.99
  42.3 1.0 %reshape.179.spec_ref = f32[2,48,768]{2,1,0:T(8,128)} reshape(f32[2,48,16,48]{3,2,1,0:T(8,128)S(1)} %bitcast.58) | data formatting | bytes 589824 | tf_op jit(solution)/shard_map/reshape | solution.py:189
  43.3 4.3 %shard_map.128 = f32[2,48,768]{2,1,0:T(8,128)} custom-call(f32[2,48,768]{2,1,0:T(8,128)} %reshape.179.spec_ref, f32[48,768]{1,0:T(8,128)} %tile.81.north_ref, f32[48,768]{1,0:T(8,128)} %add.179.south_ref, f32[48,768]{1,0:T(8,128)} %tile.84.east_ref, f32[48,768]{1,0:T(8,128)} %add.181.west_ref, f32[48,768]{1,0:T(8,128)} %get-tuple-element.27.diag_a_ref, ...), custom_call_target="tpu_custom_call" | custom-call | tf_op jit(solution)/shard_map/pallas_call | solution.py:151
  47.6 1.4 %reshape.180 = f32[2,48,16,48]{3,2,1,0:T(8,128)S(1)} reshape(f32[2,48,768]{2,1,0:T(8,128)} %shard_map.128) | data formatting | bytes 589824 | tf_op jit(solution)/shard_map/reshape | solution.py:193
  49.0 0.2 slice.165
  49.2 0.2 copy.101
  49.3 0.2 reshape.181
  49.6 0.5 copy-done.1
  50.0 0.3 convolution_bitcast_fusion
  50.3 0.7 copy.86
  51.0 0.4 all-to-all-done
  51.4 7.0 %all-to-all-start.3 = ((f32[32,8,128]{2,1,0:T(8,128)}), f32[32,8,128]{2,1,0:T(8,128)S(1)}, u32[]{:S(2)}, u32[]{:S(2)}) async-start(f32[32,8,128]{2,1,0:T(8,128)} %bitcast.25), calls=%async_computation.3 | async-start | bytes 262144 | tf_op jit(solution)/shard_map/all_to_all | solution.py:196
  58.4 0.4 fusion.3
  58.8 0.5 reshape.170
  59.3 0.2 copy.100
  59.5 1.0 %reshape.171.spec_ref = f32[2,48,768]{2,1,0:T(8,128)} reshape(f32[2,48,16,48]{3,2,1,0:T(8,128)S(1)} %bitcast.59) | data formatting | bytes 589824 | tf_op jit(solution)/shard_map/reshape | solution.py:189
  60.6 4.3 %shard_map.127 = f32[2,48,768]{2,1,0:T(8,128)} custom-call(f32[2,48,768]{2,1,0:T(8,128)} %reshape.171.spec_ref, f32[48,768]{1,0:T(8,128)} %tile.71.north_ref, f32[48,768]{1,0:T(8,128)} %add.152.south_ref, f32[48,768]{1,0:T(8,128)} %tile.74.east_ref, f32[48,768]{1,0:T(8,128)} %add.156.west_ref, f32[48,768]{1,0:T(8,128)} %get-tuple-element.38.diag_a_ref, ...), custom_call_target="tpu_custom_call" | custom-call | tf_op jit(solution)/shard_map/pallas_call | solution.py:151
  64.9 1.4 %reshape.172 = f32[2,48,16,48]{3,2,1,0:T(8,128)S(1)} reshape(f32[2,48,768]{2,1,0:T(8,128)} %shard_map.127) | data formatting | bytes 589824 | tf_op jit(solution)/shard_map/reshape | solution.py:193
  66.2 0.2 slice.157
  66.4 0.2 copy.102
  66.6 0.2 reshape.173
  66.8 0.2 convolution_bitcast_fusion.1
  67.1 0.7 copy.84
  67.8 7.4 %all-to-all-start.1 = ((f32[32,8,128]{2,1,0:T(8,128)}), f32[32,8,128]{2,1,0:T(8,128)S(1)}, u32[]{:S(2)}, u32[]{:S(2)}) async-start(f32[32,8,128]{2,1,0:T(8,128)} %bitcast.19), calls=%async_computation.1 | async-start | bytes 262144 | tf_op jit(solution)/shard_map/all_to_all | solution.py:196
  75.2 0.2 reshape.183
  75.3 7.5 %all-to-all-done.1 = f32[32,8,128]{2,1,0:T(8,128)S(1)} async-done(((f32[32,8,128]{2,1,0:T(8,128)}), f32[32,8,128]{2,1,0:T(8,128)S(1)}, u32[]{:S(2)}, u32[]{:S(2)}) %all-to-all-start.1) | async-done | bytes 131104 | tf_op jit(solution)/shard_map/all_to_all | solution.py:196
  82.9 0.2 reshape.175
  83.1 0.1 maximum_bitcast_fusion
  83.2 0.3 copy.79
  83.5 0.9 %copy.80 = f32[1,64,1024]{2,1,0:T(8,128)} copy(f32[1,64,1024]{1,2,0:T(8,128)S(1)} %bitcast.61) | data formatting | bytes 524288 | tf_op jit(solution)/shard_map/reshape | solution.py:199
  (49 shorter events, 1.7 us)
Async XLA Ops:
  0.0 1.2 %copy-start = (f32[1,64,1024]{2,1,0:T(8,128)S(1)}, f32[1,64,1024]{2,1,0:T(8,128)}, u32[]{:S(2)}) copy-start(f32[1,64,1024]{2,1,0:T(8,128)} %param.13) | copy-start | bytes 786436
  2.1 7.6 %collective-permute-start.1 = (f32[2,8,1024]{2,1,0:T(8,128)S(1)}, f32[2,8,1024]{2,1,0:T(8,128)S(1)}, u32[]{:S(2)}, u32[]{:S(2)}) collective-permute-start(f32[2,8,1024]{2,1,0:T(8,128)S(1)} %copy.60), channel_id=1, source_target_pairs={{1,0},{2,1},{3,2},{4,3},{5,4},{6,5},{7,6},{9,8},{10,9},{11,10},{12... | collective-permute-start | bytes 196616 | tf_op jit(solution)/shard_map/ppermute | solution.py:37
  4.3 6.1 %collective-permute-start = (f32[2,8,1024]{2,1,0:T(8,128)S(1)}, f32[2,8,1024]{2,1,0:T(8,128)S(1)}, u32[]{:S(2)}, u32[]{:S(2)}) collective-permute-start(f32[2,8,1024]{2,1,0:T(8,128)S(1)} %copy.59), channel_id=1, source_target_pairs={{0,1},{1,2},{2,3},{3,4},{4,5},{5,6},{6,7},{8,9},{9,10},{10,11},{11... | collective-permute-start | bytes 196616 | tf_op jit(solution)/shard_map/ppermute | solution.py:36
  13.4 20.2 %all-to-all-start.2 = ((f32[32,18,128]{2,1,0:T(8,128)}), f32[32,18,128]{2,1,0:T(8,128)S(1)}, u32[]{:S(2)}, u32[]{:S(2)}) async-start(f32[32,18,128]{2,1,0:T(8,128)} %reshape.176), calls=%async_computation.2 | async-start | bytes 786432 | tf_op jit(solution)/shard_map/all_to_all | solution.py:183
  31.5 0.9 %copy-start.3 = (f32[768]{0:T(1024)S(1)}, f32[768]{0:T(1024)}, u32[]{:S(2)}) copy-start(f32[768]{0:T(1024)} %constant.66) | copy-start | bytes 9220
  31.5 0.9 %copy-start.4 = (f32[768]{0:T(1024)S(1)}, f32[768]{0:T(1024)}, u32[]{:S(2)}) copy-start(f32[768]{0:T(1024)} %constant.65) | copy-start | bytes 9220
  31.5 0.9 %copy-start.5 = (f32[768]{0:T(1024)S(1)}, f32[768]{0:T(1024)}, u32[]{:S(2)}) copy-start(f32[768]{0:T(1024)} %constant.63) | copy-start | bytes 9220
  31.5 0.9 %copy-start.6 = (f32[768]{0:T(1024)S(1)}, f32[768]{0:T(1024)}, u32[]{:S(2)}) copy-start(f32[768]{0:T(1024)} %constant.64) | copy-start | bytes 9220
  33.6 7.5 %copy-start.2 = (f32[32,32]{1,0:T(8,128)S(1)}, f32[32,32]{1,0:T(8,128)}, u32[]{:S(2)}) copy-start(f32[32,32]{1,0:T(8,128)} %constant.51.clone) | copy-start | bytes 12292
  33.6 17.8 %all-to-all-start = ((f32[32,18,128]{2,1,0:T(8,128)}), f32[32,18,128]{2,1,0:T(8,128)S(1)}, u32[]{:S(2)}, u32[]{:S(2)}) async-start(f32[32,18,128]{2,1,0:T(8,128)} %reshape.168), calls=%async_computation | async-start | bytes 786432 | tf_op jit(solution)/shard_map/all_to_all | solution.py:183
  49.3 0.7 copy-start.1
  51.4 16.4 %all-to-all-start.3 = ((f32[32,8,128]{2,1,0:T(8,128)}), f32[32,8,128]{2,1,0:T(8,128)S(1)}, u32[]{:S(2)}, u32[]{:S(2)}) async-start(f32[32,8,128]{2,1,0:T(8,128)} %bitcast.25), calls=%async_computation.3 | async-start | bytes 262144 | tf_op jit(solution)/shard_map/all_to_all | solution.py:196
  67.8 15.1 %all-to-all-start.1 = ((f32[32,8,128]{2,1,0:T(8,128)}), f32[32,8,128]{2,1,0:T(8,128)S(1)}, u32[]{:S(2)}, u32[]{:S(2)}) async-start(f32[32,8,128]{2,1,0:T(8,128)} %bitcast.19), calls=%async_computation.1 | async-start | bytes 262144 | tf_op jit(solution)/shard_map/all_to_all | solution.py:196

commit v10 on v8

--- a/solution.py
+++ b/solution.py
@@ -32,9 +32,12 @@
     count = lax.axis_size("row")
     forward = [(i, i + 1) for i in range(count - 1)]
     backward = [(target, source) for source, target in forward]
+    bottom = jnp.stack([right_side[0, rows - width :], kappa[rows - width :]])
+    top = jnp.stack([right_side[0, :width], kappa[:width]])
+    bottom, top = lax.optimization_barrier((bottom, top))
+    low = lax.ppermute(bottom, "row", forward)
+    high = lax.ppermute(top, "row", backward)
     joined = jnp.concatenate([right_side, kappa[None]], axis=0)
-    low = lax.ppermute(joined[:, rows - width :], "row", forward)
-    high = lax.ppermute(joined[:, :width], "row", backward)
     joined = jnp.concatenate([low, joined, high], axis=1)
     place = lax.axis_index("row") * rows - width + jnp.arange(rows + 2 * width)
     inside = (place >= 0) & (place < rows * count)

time: 61.1 us -> 59.5 us (0.974)
  waiting for transfers between devices: 7.11 us -> 6.2 us
    unnamed x15 -> x17, local copies, waits for them, and re-layouts: 2.38 us -> 1.43 us
    ppermute x2, waiting for transfers between devices: 0.93 us -> 0.01 us  [the longest x1 0.01 us: with_halo(): high = lax.ppermute(top, 'row', backward)]
    another operation x0 -> x1, local copies, waits for them, and re-layouts: none -> 0.82 us  [with_halo(): top = jnp.stack([right_side[0, :width], kappa[:width]])]
  transfers between devices with their start and end apart: 3 -> 3, of which waited for: 2 -> 1; matrix products, arithmetic and copies ran while one was open for 10% -> 12% of each run, Pallas kernels for 0% -> 0%
where the time goes in v10:
time: 59.5 us; the launch traced here: 58.6 us
  local copies, waits for them, and re-layouts  15.5 us (26%)
  starting transfers between devices  14.9 us (25%)
  blocking collectives  12.4 us (21%)
  waiting for transfers between devices  6.2 us (10%)
  Pallas kernels  6 us (10%)
  other arithmetic  2.08 us (3%)
  matrix products  1.16 us (2%)
    all_to_all x1, blocking collectives, body(): returned = lax.all_to_all(signal, 'tm', 0, 0, tiled=True)  12.4 us
    all_to_all x1, starting transfers between devices, body(): lax.all_to_all(sent, 'tm', 0, 0, tiled=True)  8.26 us
    all_to_all x1, waiting for transfers between devices, body(): lax.all_to_all(sent, 'tm', 0, 0, tiled=True)  6.19 us
    pallas_call x1, Pallas kernels, solve_slots(): pl.pallas_call(solve_kernel, out_shape=jax.ShapeDtypeStruct(spectrum.shap...  6 us
    ppermute x1, starting transfers between devices, with_halo(): low = lax.ppermute(bottom, 'row', forward)  4.76 us
    another operation x8, local copies, waits for them, and re-layouts, body(): jnp.tile(f, (1, half))  1.97 us
    ppermute x1, starting transfers between devices, with_halo(): high = lax.ppermute(top, 'row', backward)  1.92 us
    unnamed x17, local copies, waits for them, and re-layouts  1.43 us
  transfers between devices with their start and end apart: 3, of which 1 were waited for; matrix products, arithmetic and copies ran while one was open for 12% of the time, Pallas kernels for 0%

profile of v10, /device:TPU:97, one launch (start us, length us, event | category | flops | bytes accessed | tf_op | source)
XLA Modules:
  0.0 58.6 jit_solution(11281174542435615757)
XLA Ops:
  0.0 0.0 copy-start
  0.0 0.8 %slice_bitcast_fusion.3 = (f32[1,8,1024]{2,1,0:T(8,128)S(1)}, f32[1,8,1024]{2,1,0:T(8,128)S(1)}) fusion(f32[64,1024]{1,0:T(8,128)} %param.11), kind=kLoop, calls=%fused_computation.24 | loop fusion | bytes 131072 | tf_op jit(solution)/shard_map/stack | solution.py:36
  0.8 0.8 %fusion.13 = (f32[1,8,1024]{2,1,0:T(8,128)S(1)}, f32[1,8,1024]{2,1,0:T(8,128)S(1)}) fusion(f32[1,64,1024]{2,1,0:T(8,128)} %param.10), kind=kLoop, calls=%fused_computation.40 | loop fusion | bytes 131072 | tf_op jit(solution)/shard_map/slice | solution.py:36
  1.6 1.9 %collective-permute-start.1 = (f32[2,8,1024]{2,1,0:T(8,128)S(1)}, f32[2,8,1024]{2,1,0:T(8,128)S(1)}, u32[]{:S(2)}, u32[]{:S(2)}) collective-permute-start(f32[2,8,1024]{2,1,0:T(8,128)S(1)} %get-tuple-element.8), channel_id=1, source_target_pairs={{1,0},{2,1},{3,2},{4,3},{5,4},{6,5},{7,6},{9,8},{10,9},{11,10},{12... | collective-permute-start | bytes 196616 | tf_op jit(solution)/shard_map/ppermute | solution.py:39
  3.5 4.8 %collective-permute-start = (f32[2,8,1024]{2,1,0:T(8,128)S(1)}, f32[2,8,1024]{2,1,0:T(8,128)S(1)}, u32[]{:S(2)}, u32[]{:S(2)}) collective-permute-start(f32[2,8,1024]{2,1,0:T(8,128)S(1)} %get-tuple-element.7), channel_id=1, source_target_pairs={{0,1},{1,2},{2,3},{3,4},{4,5},{5,6},{6,7},{8,9},{9,10},{10,11},{11... | collective-permute-start | bytes 196616 | tf_op jit(solution)/shard_map/ppermute | solution.py:38
  8.3 1.1 %copy.35 = f32[64,1024]{0,1:T(8,128)S(1)} copy(f32[64,1024]{1,0:T(8,128)} %param.11) | data formatting | bytes 524288 | tf_op args[1]
  9.5 0.0 copy-done
  9.5 0.2 copy.36
  9.7 0.0 collective-permute-done.1
  9.7 0.3 copy.38
  10.1 0.0 collective-permute-done
  10.1 0.3 copy.37
  10.4 0.6 %pad_maximum_fusion = f32[2,80,1024]{1,2,0:T(8,128)S(1)} fusion(f32[2,8,1024]{1,2,0:T(8,128)S(1)} %copy.38, f32[1,64,1024]{1,2,0:T(8,128)S(1)} %bitcast.44, f32[1,64,1024]{1,2,0:T(8,128)S(1)} %copy.36, f32[2,8,1024]{1,2,0:T(8,128)S(1)} %copy.37), kind=kLoop, calls=%fused_computation.1 | loop fusion | flops 491520 | bytes 1310720 | tf_op jit(solution)/shard_map/concatenate | solution.py:41
  11.0 0.1 slice_bitcast_fusion.1
  11.1 0.1 pad_slice_fusion.1
  11.2 0.1 maximum_bitcast_fusion
  11.3 0.4 copy.39
  11.7 1.3 %reshape.102 = f32[32,30,128]{2,1,0:T(8,128)} reshape(f32[32,80,48]{2,1,0:T(8,128)S(1)} %copy.39) | data formatting | bytes 983040 | tf_op jit(solution)/shard_map/reshape | solution.py:175
  12.9 8.3 %all-to-all-start = ((f32[32,30,128]{2,1,0:T(8,128)}), f32[32,30,128]{2,1,0:T(8,128)S(1)}, u32[]{:S(2)}, u32[]{:S(2)}) async-start(f32[32,30,128]{2,1,0:T(8,128)} %reshape.102), calls=%async_computation | async-start | bytes 1048576 | tf_op jit(solution)/shard_map/all_to_all | solution.py:176
  21.2 0.1 broadcast_and_fusion
  21.3 0.2 copy.43
  21.5 0.2 broadcast_add_fusion.2
  21.7 0.8 %copy.47.north_ref = f32[80,768]{1,0:T(8,128)} copy(f32[80,768]{0,1:T(8,128)S(1)} %bitcast.46) | data formatting | bytes 491520 | tf_op jit(solution)/shard_map/tile | solution.py:185
  22.6 0.9 %copy.48.south_ref = f32[80,768]{1,0:T(8,128)} copy(f32[80,768]{0,1:T(8,128)S(1)} %bitcast.47) | data formatting | bytes 491520 | tf_op jit(solution)/shard_map/add | solution.py:152
  23.5 0.0 copy-start.3
  23.5 0.0 copy-start.4
  23.5 0.0 copy-start.5
  23.5 0.0 copy-start.6
  23.6 0.8 %copy.49.east_ref = f32[80,768]{1,0:T(8,128)} copy(f32[80,768]{0,1:T(8,128)S(1)} %bitcast.48) | data formatting | bytes 491520 | tf_op jit(solution)/shard_map/tile | solution.py:185
  24.4 0.9 %copy.50.west_ref = f32[80,768]{1,0:T(8,128)} copy(f32[80,768]{0,1:T(8,128)S(1)} %bitcast.49) | data formatting | bytes 491520 | tf_op jit(solution)/shard_map/add | solution.py:152
  25.3 0.0 copy-start.1
  25.3 0.1 copy.41
  25.5 0.0 copy-done.3
  25.5 0.0 copy-done.4
  25.5 0.0 copy-done.5
  25.5 0.0 copy-done.6
  25.5 1.1 %divide_select_fusion = (f32[80,768]{1,0:T(8,128)}, f32[80,768]{1,0:T(8,128)}, f32[80,768]{1,0:T(8,128)}, f32[80,768]{1,0:T(8,128)}, f32[80,768]{1,0:T(8,128)}) fusion(pred[80,768]{1,0:T(8,128)(4,1)S(1)} %copy.43, f32[768]{0:T(1024)S(1)} %copy-done.3, f32[768]{0:T(1024)S(1)} %copy-done.4, f32[80,768]{1,0:T(8,128)S(1)} %copy.41, f32[768]{0:T(1024)S(1)} %copy-done.5, ...), kind=kLoop, calls=%fused_computation.16 | loop fusion | flops 737280 | bytes 1548288 | tf_op jit(solution)/shard_map/jit(_where)/select_n | solution.py:151
  26.6 6.2 %all-to-all-done = f32[32,30,128]{2,1,0:T(8,128)S(1)} async-done(((f32[32,30,128]{2,1,0:T(8,128)}), f32[32,30,128]{2,1,0:T(8,128)S(1)}, u32[]{:S(2)}, u32[]{:S(2)}) %all-to-all-start) | async-done | bytes 491552 | tf_op jit(solution)/shard_map/all_to_all | solution.py:176
  32.8 0.0 copy-done.1
  32.8 0.8 %fusion = f32[32,3840]{1,0:T(8,128)S(1)} fusion(f32[32,32]{1,0:T(8,128)S(1)} %copy-done.1, f32[4,8,30,128]{3,2,1,0:T(8,128)S(1)} %bitcast.45), kind=kOutput, calls=%fused_computation.8 | convolution fusion | flops 47185920 | bytes 987136 | tf_op jit(solution)/shard_map/dot_general | solution.py:177
  33.6 0.8 %reshape.104 = f32[2,16,80,48]{3,2,1,0:T(8,128)S(1)} reshape(f32[32,3840]{1,0:T(8,128)S(1)} %fusion) | data formatting | bytes 983040 | tf_op jit(solution)/shard_map/reshape | solution.py:178
  34.5 0.4 copy.40
  34.9 1.0 %copy.46.spec_ref = f32[2,80,768]{2,1,0:T(8,128)} copy(f32[2,80,768]{1,2,0:T(8,128)S(1)} %bitcast.40) | data formatting | bytes 983040 | tf_op jit(solution)/shard_map/reshape | solution.py:179
  35.9 6.0 %shard_map.100 = f32[2,80,768]{2,1,0:T(8,128)} custom-call(f32[2,80,768]{2,1,0:T(8,128)} %copy.46.spec_ref, f32[80,768]{1,0:T(8,128)} %copy.47.north_ref, f32[80,768]{1,0:T(8,128)} %copy.48.south_ref, f32[80,768]{1,0:T(8,128)} %copy.49.east_ref, f32[80,768]{1,0:T(8,128)} %copy.50.west_ref, f32[80,768]{1,0:T(8,128)} %get-tuple-element.29.diag_a_ref, ...), custom_call_target="tpu_custom_call" | custom-call | tf_op jit(solution)/shard_map/pallas_call | solution.py:154
  41.9 1.3 %copy.51 = f32[2,80,768]{1,2,0:T(8,128)S(1)} copy(f32[2,80,768]{2,1,0:T(8,128)} %shard_map.100) | data formatting | bytes 983040 | tf_op jit(solution)/shard_map/pallas_call | solution.py:154
  43.2 0.2 slice_bitcast_fusion
  43.4 0.0 copy-start.2
  43.4 0.4 copy.52
  43.8 0.5 reshape.107
  44.3 0.0 copy-done.2
  44.3 0.4 convolution_bitcast_fusion
  44.7 12.4 %all_to_all.10 = f32[32,16,128]{2,1,0:T(8,128)S(1)} all-to-all(f32[32,16,128]{2,1,0:T(8,128)S(1)} %bitcast.52), channel_id=1, replica_groups=mesh['tm'=32,'row'=8] {'tm'}, dimensions={0} | all-to-all | bytes 524288 | tf_op jit(solution)/shard_map/all_to_all | solution.py:193
  57.1 0.3 reshape.109
  57.4 0.3 copy.53
  57.7 0.9 %copy.54 = f32[1,64,1024]{2,1,0:T(8,128)} copy(f32[1,64,1024]{1,2,0:T(8,128)S(1)} %bitcast.43) | data formatting | bytes 524288 | tf_op jit(solution)/shard_map/reshape | solution.py:195
  (11 shorter events, 0.3 us)
Async XLA Ops:
  0.0 9.5 %copy-start = (f32[1,64,1024]{2,1,0:T(8,128)S(1)}, f32[1,64,1024]{2,1,0:T(8,128)}, u32[]{:S(2)}) copy-start(f32[1,64,1024]{2,1,0:T(8,128)} %param.10) | copy-start | bytes 786436
  1.6 8.1 %collective-permute-start.1 = (f32[2,8,1024]{2,1,0:T(8,128)S(1)}, f32[2,8,1024]{2,1,0:T(8,128)S(1)}, u32[]{:S(2)}, u32[]{:S(2)}) collective-permute-start(f32[2,8,1024]{2,1,0:T(8,128)S(1)} %get-tuple-element.8), channel_id=1, source_target_pairs={{1,0},{2,1},{3,2},{4,3},{5,4},{6,5},{7,6},{9,8},{10,9},{11,10},{12... | collective-permute-start | bytes 196616 | tf_op jit(solution)/shard_map/ppermute | solution.py:39
  3.5 6.5 %collective-permute-start = (f32[2,8,1024]{2,1,0:T(8,128)S(1)}, f32[2,8,1024]{2,1,0:T(8,128)S(1)}, u32[]{:S(2)}, u32[]{:S(2)}) collective-permute-start(f32[2,8,1024]{2,1,0:T(8,128)S(1)} %get-tuple-element.7), channel_id=1, source_target_pairs={{0,1},{1,2},{2,3},{3,4},{4,5},{5,6},{6,7},{8,9},{9,10},{10,11},{11... | collective-permute-start | bytes 196616 | tf_op jit(solution)/shard_map/ppermute | solution.py:38
  12.9 19.9 %all-to-all-start = ((f32[32,30,128]{2,1,0:T(8,128)}), f32[32,30,128]{2,1,0:T(8,128)S(1)}, u32[]{:S(2)}, u32[]{:S(2)}) async-start(f32[32,30,128]{2,1,0:T(8,128)} %reshape.102), calls=%async_computation | async-start | bytes 1048576 | tf_op jit(solution)/shard_map/all_to_all | solution.py:176
  23.5 2.0 %copy-start.3 = (f32[768]{0:T(1024)S(1)}, f32[768]{0:T(1024)}, u32[]{:S(2)}) copy-start(f32[768]{0:T(1024)} %constant.66) | copy-start | bytes 9220
  23.5 2.0 %copy-start.4 = (f32[768]{0:T(1024)S(1)}, f32[768]{0:T(1024)}, u32[]{:S(2)}) copy-start(f32[768]{0:T(1024)} %constant.65) | copy-start | bytes 9220
  23.5 2.0 %copy-start.5 = (f32[768]{0:T(1024)S(1)}, f32[768]{0:T(1024)}, u32[]{:S(2)}) copy-start(f32[768]{0:T(1024)} %constant.63) | copy-start | bytes 9220
  23.5 2.0 %copy-start.6 = (f32[768]{0:T(1024)S(1)}, f32[768]{0:T(1024)}, u32[]{:S(2)}) copy-start(f32[768]{0:T(1024)} %constant.64) | copy-start | bytes 9220
  25.3 7.6 %copy-start.1 = (f32[32,32]{1,0:T(8,128)S(1)}, f32[32,32]{1,0:T(8,128)}, u32[]{:S(2)}) copy-start(f32[32,32]{1,0:T(8,128)} %constant.51.clone) | copy-start | bytes 12292
  43.4 0.9 %copy-start.2 = (f32[32,32]{1,0:T(8,128)S(1)}, f32[32,32]{1,0:T(8,128)}, u32[]{:S(2)}) copy-start(f32[32,32]{1,0:T(8,128)} %constant.57.clone) | copy-start | bytes 12292

commit v11 on v10

--- a/solution.py
+++ b/solution.py
@@ -1,3 +1,4 @@
+import functools
 import math
 
 import jax
@@ -101,9 +102,13 @@
     return jnp.concatenate([main, extra], axis=2).transpose(1, 0, 2)
 
 
-def solve_kernel(spec_ref, north_ref, south_ref, east_ref, west_ref, diag_a_ref, diag_b_ref,
-                 inva_ref, invb_ref, invi_ref, imag_ref, out_ref):
+def solve_kernel(margin, slabs_ref, north_ref, south_ref, east_ref, west_ref, diag_a_ref,
+                 diag_b_ref, inva_ref, invb_ref, invi_ref, imag_ref, interior_ref, spec_ref, out_ref):
     rows, lanes = north_ref.shape
+    parts, half, inner, span = interior_ref.shape
+    width = lanes // half
+    for part in range(parts):
+        spec_ref[part] = jnp.concatenate([slabs_ref[part, slot] for slot in range(half)], axis=1)
 
     def coupled(x):
         above = pltpu.roll(x, rows - 1, 0)
@@ -137,9 +142,13 @@
             else:
                 out_ref[0] = out_ref[0] + weight * corr_real
                 out_ref[1] = out_ref[1] + weight * corr_imag
-
-
-def solve_slots(spectrum, faces, shifts, inside):
+    for part in range(parts):
+        for slot in range(half):
+            start = slot * width + margin
+            interior_ref[part, slot] = out_ref[part, margin : margin + inner, start : start + span]
+
+
+def solve_slots(slabs, faces, shifts, inside, rows, span, margin):
     north, south, east, west, diagonal = faces
     real_a, real_b, imag = shifts
     diag_a = real_a + diagonal
@@ -149,11 +158,14 @@
     inv_a = jnp.where(inside, diag_a / mag_a, 0.0)
     inv_b = jnp.where(inside, diag_b / mag_b, 0.0)
     inv_imag = jnp.where(inside, -imag / mag_a, 0.0)
-    operands = (spectrum, north, south + courant_rows, east, west + courant_cols,
+    operands = (slabs, north, south + courant_rows, east, west + courant_cols,
                 diag_a, diag_b, inv_a, inv_b, inv_imag, jnp.asarray(imag))
+    parts, half = slabs.shape[:2]
+    field = (parts,) + north.shape
     return pl.pallas_call(
-        solve_kernel,
-        out_shape=jax.ShapeDtypeStruct(spectrum.shape, spectrum.dtype),
+        functools.partial(solve_kernel, margin),
+        out_shape=jax.ShapeDtypeStruct((parts, half, rows, span), slabs.dtype),
+        scratch_shapes=[pltpu.VMEM(field, jnp.float32), pltpu.VMEM(field, jnp.float32)],
     )(*operands)
 
 
@@ -175,8 +187,7 @@
     sent = column_tiles(wide_side, tiles, width, margin).reshape(tiles, -1, lane)
     gathered = lax.all_to_all(sent, "tm", 0, 0, tiled=True).reshape(tiles, extended * width)
     spectrum = jnp.dot(forward, gathered, precision=highest)
-    spectrum = spectrum.reshape(2, half, extended, width).transpose(0, 2, 1, 3)
-    spectrum = spectrum.reshape(2, extended, half * width)
+    spectrum = spectrum.reshape(2, half, extended, width)
 
     place = tile * span - margin + jnp.arange(width)
     inside_cols = (place >= 0) & (place < cols)
@@ -184,10 +195,8 @@
     inside = jnp.tile(inside, (1, half))
     faces = tuple(jnp.tile(f, (1, half)) for f in tile_faces(kappa_rows, tile, tiles, width, margin))
     shifts = slot_shifts(half, total, width)
-    solved = solve_slots(spectrum, faces, shifts, inside)
-
-    solved = solved.reshape(2, extended, half, width)[:, margin : margin + rows, :, margin : margin + span]
-    solved = solved.transpose(0, 2, 1, 3).reshape(total, rows * span)
+    solved = solve_slots(spectrum, faces, shifts, inside, rows, span, margin)
+    solved = solved.reshape(total, rows * span)
     signal = jnp.dot(inverse, solved, precision=highest)
     signal = signal.reshape(total, -1, lane)
     returned = lax.all_to_all(signal, "tm", 0, 0, tiled=True)

time: 59.5 us -> 62.8 us (1.055)
  waiting for transfers between devices: 6.2 us -> 9.09 us
  Pallas kernels: 6 us -> 7.03 us
  local copies, waits for them, and re-layouts: 15.5 us -> 14.5 us
  starting transfers between devices: 14.9 us -> 15.9 us
    ppermute x1, waiting for transfers between devices: 0.01 us -> 2.89 us  [with_halo(): high = lax.ppermute(top, 'row', backward)]
    pallas_call x1 -> x0, local copies, waits for them, and re-layouts: 1.29 us -> none  [solve_slots(): pl.pallas_call(solve_kernel, out_shape=jax.ShapeDtypeStruct(spectrum.shap...]
    reshape x3 -> x2, local copies, waits for them, and re-layouts: 2.36 us -> 3.63 us  [the longest x1 1.9 us: body(): spectrum = spectrum.reshape(2, half, extended, width)]
    pallas_call x1, Pallas kernels: 6 us -> 7.03 us  [solve_slots(): pl.pallas_call(functools.partial(solve_kernel, margin), out_shape=jax.Sha...]
    transpose x3 -> x0, local copies, waits for them, and re-layouts: 0.93 us -> none  [the longest x2 0.56 us: body(): solved = solved.transpose(0, 2, 1, 3).reshape(total, rows * span)]
    all_to_all x1, starting transfers between devices: 8.26 us -> 9.19 us  [body(): lax.all_to_all(sent, 'tm', 0, 0, tiled=True)]
  transfers between devices with their start and end apart: 3 -> 3, of which waited for: 1 -> 2; matrix products, arithmetic and copies ran while one was open for 12% -> 11% of each run, Pallas kernels for 0% -> 0%
where the time goes in v11:
time: 62.8 us; the launch traced here: 62.4 us
  starting transfers between devices  15.9 us (25%)
  local copies, waits for them, and re-layouts  14.5 us (23%)
  blocking collectives  12.4 us (20%)
  waiting for transfers between devices  9.09 us (14%)
  Pallas kernels  7.03 us (11%)
  other arithmetic  2.08 us (3%)
  matrix products  1.16 us (2%)
    all_to_all x1, blocking collectives, body(): returned = lax.all_to_all(signal, 'tm', 0, 0, tiled=True)  12.4 us
    all_to_all x1, starting transfers between devices, body(): lax.all_to_all(sent, 'tm', 0, 0, tiled=True)  9.19 us
    pallas_call x1, Pallas kernels, solve_slots(): pl.pallas_call(functools.partial(solve_kernel, margin), out_shape=jax.Sha...  7.03 us
    all_to_all x1, waiting for transfers between devices, body(): lax.all_to_all(sent, 'tm', 0, 0, tiled=True)  6.2 us
    ppermute x1, starting transfers between devices, with_halo(): low = lax.ppermute(bottom, 'row', forward)  4.76 us
    ppermute x1, waiting for transfers between devices, with_halo(): high = lax.ppermute(top, 'row', backward)  2.89 us
    another operation x8, local copies, waits for them, and re-layouts, body(): jnp.tile(f, (1, half))  2 us
    ppermute x1, starting transfers between devices, with_halo(): high = lax.ppermute(top, 'row', backward)  1.92 us
  transfers between devices with their start and end apart: 3, of which 2 were waited for; matrix products, arithmetic and copies ran while one was open for 11% of the time, Pallas kernels for 0%

profile of v11, /device:TPU:97, one launch (start us, length us, event | category | flops | bytes accessed | tf_op | source)
XLA Modules:
  0.0 62.4 jit_solution(7307845799713412375)
XLA Ops:
  0.0 0.0 copy-start
  0.0 0.8 %fusion.13 = (f32[1,8,1024]{2,1,0:T(8,128)S(1)}, f32[1,8,1024]{2,1,0:T(8,128)S(1)}) fusion(f32[1,64,1024]{2,1,0:T(8,128)} %param.10), kind=kLoop, calls=%fused_computation.39 | loop fusion | bytes 131072 | tf_op jit(solution)/shard_map/slice | solution.py:37
  0.8 0.8 %slice_bitcast_fusion.2 = (f32[1,8,1024]{2,1,0:T(8,128)S(1)}, f32[1,8,1024]{2,1,0:T(8,128)S(1)}) fusion(f32[64,1024]{1,0:T(8,128)} %param.11), kind=kLoop, calls=%fused_computation.23 | loop fusion | bytes 131072 | tf_op jit(solution)/shard_map/stack | solution.py:37
  1.6 4.8 %collective-permute-start = (f32[2,8,1024]{2,1,0:T(8,128)S(1)}, f32[2,8,1024]{2,1,0:T(8,128)S(1)}, u32[]{:S(2)}, u32[]{:S(2)}) collective-permute-start(f32[2,8,1024]{2,1,0:T(8,128)S(1)} %get-tuple-element.7), channel_id=1, source_target_pairs={{0,1},{1,2},{2,3},{3,4},{4,5},{5,6},{6,7},{8,9},{9,10},{10,11},{11... | collective-permute-start | bytes 196616 | tf_op jit(solution)/shard_map/ppermute | solution.py:39
  6.4 1.9 %collective-permute-start.1 = (f32[2,8,1024]{2,1,0:T(8,128)S(1)}, f32[2,8,1024]{2,1,0:T(8,128)S(1)}, u32[]{:S(2)}, u32[]{:S(2)}) collective-permute-start(f32[2,8,1024]{2,1,0:T(8,128)S(1)} %get-tuple-element.8), channel_id=1, source_target_pairs={{1,0},{2,1},{3,2},{4,3},{5,4},{6,5},{7,6},{9,8},{10,9},{11,10},{12... | collective-permute-start | bytes 196616 | tf_op jit(solution)/shard_map/ppermute | solution.py:40
  8.3 1.1 %copy.31 = f32[1,64,1024]{1,2,0:T(8,128)S(1)} copy(f32[1,64,1024]{2,1,0:T(8,128)} %param.10) | data formatting | bytes 524288 | tf_op args[0]
  9.5 0.0 copy-done
  9.5 0.2 copy.30
  9.7 2.9 %collective-permute-done.1 = f32[2,8,1024]{2,1,0:T(8,128)S(1)} collective-permute-done((f32[2,8,1024]{2,1,0:T(8,128)S(1)}, f32[2,8,1024]{2,1,0:T(8,128)S(1)}, u32[]{:S(2)}, u32[]{:S(2)}) %collective-permute-start.1) | collective-permute-done | bytes 65568 | tf_op jit(solution)/shard_map/ppermute | solution.py:40
  12.6 0.3 copy.33
  12.9 0.0 collective-permute-done
  12.9 0.3 copy.32
  13.3 0.6 pad_maximum_fusion
  13.9 0.1 slice_bitcast_fusion
  14.0 0.1 pad_slice_fusion.1
  14.1 0.1 maximum_bitcast_fusion
  14.2 0.4 copy.34
  14.6 1.3 %reshape.96 = f32[32,30,128]{2,1,0:T(8,128)} reshape(f32[32,80,48]{2,1,0:T(8,128)S(1)} %copy.34) | data formatting | bytes 983040 | tf_op jit(solution)/shard_map/reshape | solution.py:187
  15.8 9.2 %all-to-all-start = ((f32[32,30,128]{2,1,0:T(8,128)}), f32[32,30,128]{2,1,0:T(8,128)S(1)}, u32[]{:S(2)}, u32[]{:S(2)}) async-start(f32[32,30,128]{2,1,0:T(8,128)} %reshape.96), calls=%async_computation | async-start | bytes 1048576 | tf_op jit(solution)/shard_map/all_to_all | solution.py:188
  25.0 0.1 broadcast_and_fusion
  25.1 0.2 copy.37
  25.3 0.2 broadcast_add_fusion.2
  25.5 0.9 %copy.43.west_ref = f32[80,768]{1,0:T(8,128)} copy(f32[80,768]{0,1:T(8,128)S(1)} %bitcast.38) | data formatting | bytes 491520 | tf_op jit(solution)/shard_map/add | solution.py:161
  26.4 0.9 %copy.41.south_ref = f32[80,768]{1,0:T(8,128)} copy(f32[80,768]{0,1:T(8,128)S(1)} %bitcast.39) | data formatting | bytes 491520 | tf_op jit(solution)/shard_map/add | solution.py:161
  27.3 0.0 copy-start.3
  27.3 0.0 copy-start.4
  27.3 0.0 copy-start.5
  27.3 0.0 copy-start.6
  27.4 0.1 copy.35
  27.6 0.9 %copy.42.east_ref = f32[80,768]{1,0:T(8,128)} copy(f32[80,768]{0,1:T(8,128)S(1)} %bitcast.41) | data formatting | bytes 491520 | tf_op jit(solution)/shard_map/tile | solution.py:196
  28.4 0.0 copy-start.1
  28.5 0.8 %copy.40.north_ref = f32[80,768]{1,0:T(8,128)} copy(f32[80,768]{0,1:T(8,128)S(1)} %bitcast.42) | data formatting | bytes 491520 | tf_op jit(solution)/shard_map/tile | solution.py:196
  29.3 0.0 copy-done.3
  29.3 0.0 copy-done.4
  29.3 0.0 copy-done.5
  29.3 0.0 copy-done.6
  29.3 1.1 %divide_select_fusion = (f32[80,768]{1,0:T(8,128)}, f32[80,768]{1,0:T(8,128)}, f32[80,768]{1,0:T(8,128)}, f32[80,768]{1,0:T(8,128)}, f32[80,768]{1,0:T(8,128)}) fusion(pred[80,768]{1,0:T(8,128)(4,1)S(1)} %copy.37, f32[768]{0:T(1024)S(1)} %copy-done.3, f32[768]{0:T(1024)S(1)} %copy-done.4, f32[80,768]{1,0:T(8,128)S(1)} %copy.35, f32[768]{0:T(1024)S(1)} %copy-done.6, ...), kind=kLoop, calls=%fused_computation.15 | loop fusion | flops 737280 | bytes 1548288 | tf_op jit(solution)/shard_map/jit(_where)/select_n | solution.py:160
  30.4 6.2 %all-to-all-done = f32[32,30,128]{2,1,0:T(8,128)S(1)} async-done(((f32[32,30,128]{2,1,0:T(8,128)}), f32[32,30,128]{2,1,0:T(8,128)S(1)}, u32[]{:S(2)}, u32[]{:S(2)}) %all-to-all-start) | async-done | bytes 491552 | tf_op jit(solution)/shard_map/all_to_all | solution.py:188
  36.6 0.0 copy-done.1
  36.6 0.8 %fusion = f32[32,3840]{1,0:T(8,128)S(1)} fusion(f32[32,32]{1,0:T(8,128)S(1)} %copy-done.1, f32[4,8,30,128]{3,2,1,0:T(8,128)S(1)} %bitcast.37), kind=kOutput, calls=%fused_computation.7 | convolution fusion | flops 47185920 | bytes 987136 | tf_op jit(solution)/shard_map/dot_general | solution.py:189
  37.5 1.9 %reshape.98.slabs_ref = f32[2,16,80,48]{3,2,1,0:T(8,128)} reshape(f32[32,3840]{1,0:T(8,128)S(1)} %fusion) | data formatting | bytes 983040 | tf_op jit(solution)/shard_map/reshape | solution.py:190
  39.4 7.0 %shard_map.100 = f32[2,16,64,32]{3,2,1,0:T(8,128)} custom-call(f32[2,16,80,48]{3,2,1,0:T(8,128)} %reshape.98.slabs_ref, f32[80,768]{1,0:T(8,128)} %copy.40.north_ref, f32[80,768]{1,0:T(8,128)} %copy.41.south_ref, f32[80,768]{1,0:T(8,128)} %copy.42.east_ref, f32[80,768]{1,0:T(8,128)} %copy.43.west_ref, f32[80,768]{1,0:T(8,128)} %get-tuple-element.29.diag_a_ref, ...), custom_call_target="tpu_custom_call" | custom-call | tf_op jit(solution)/shard_map/pallas_call | solution.py:165
  46.4 0.0 copy-start.2
  46.4 1.7 %reshape.99 = f32[32,2048]{1,0:T(8,128)S(1)} reshape(f32[2,16,64,32]{3,2,1,0:T(8,128)} %shard_map.100) | data formatting | bytes 524288 | tf_op jit(solution)/shard_map/reshape | solution.py:199
  48.1 0.0 copy-done.2
  48.1 0.4 convolution_bitcast_fusion
  48.5 12.4 %all_to_all.10 = f32[32,16,128]{2,1,0:T(8,128)S(1)} all-to-all(f32[32,16,128]{2,1,0:T(8,128)S(1)} %bitcast.44), channel_id=1, replica_groups=mesh['tm'=32,'row'=8] {'tm'}, dimensions={0} | all-to-all | bytes 524288 | tf_op jit(solution)/shard_map/all_to_all | solution.py:202
  61.0 0.3 reshape.101
  61.2 0.3 copy.44
  61.5 0.9 %copy.45 = f32[1,64,1024]{2,1,0:T(8,128)} copy(f32[1,64,1024]{1,2,0:T(8,128)S(1)} %bitcast.35) | data formatting | bytes 524288 | tf_op jit(solution)/shard_map/reshape | solution.py:204
  (11 shorter events, 0.3 us)
Async XLA Ops:
  0.0 9.5 %copy-start = (f32[64,1024]{1,0:T(8,128)S(1)}, f32[64,1024]{1,0:T(8,128)}, u32[]{:S(2)}) copy-start(f32[64,1024]{1,0:T(8,128)} %param.11) | copy-start | bytes 786436
  1.6 11.3 %collective-permute-start = (f32[2,8,1024]{2,1,0:T(8,128)S(1)}, f32[2,8,1024]{2,1,0:T(8,128)S(1)}, u32[]{:S(2)}, u32[]{:S(2)}) collective-permute-start(f32[2,8,1024]{2,1,0:T(8,128)S(1)} %get-tuple-element.7), channel_id=1, source_target_pairs={{0,1},{1,2},{2,3},{3,4},{4,5},{5,6},{6,7},{8,9},{9,10},{10,11},{11... | collective-permute-start | bytes 196616 | tf_op jit(solution)/shard_map/ppermute | solution.py:39
  6.4 6.2 %collective-permute-start.1 = (f32[2,8,1024]{2,1,0:T(8,128)S(1)}, f32[2,8,1024]{2,1,0:T(8,128)S(1)}, u32[]{:S(2)}, u32[]{:S(2)}) collective-permute-start(f32[2,8,1024]{2,1,0:T(8,128)S(1)} %get-tuple-element.8), channel_id=1, source_target_pairs={{1,0},{2,1},{3,2},{4,3},{5,4},{6,5},{7,6},{9,8},{10,9},{11,10},{12... | collective-permute-start | bytes 196616 | tf_op jit(solution)/shard_map/ppermute | solution.py:40
  15.8 20.8 %all-to-all-start = ((f32[32,30,128]{2,1,0:T(8,128)}), f32[32,30,128]{2,1,0:T(8,128)S(1)}, u32[]{:S(2)}, u32[]{:S(2)}) async-start(f32[32,30,128]{2,1,0:T(8,128)} %reshape.96), calls=%async_computation | async-start | bytes 1048576 | tf_op jit(solution)/shard_map/all_to_all | solution.py:188
  27.3 2.0 %copy-start.3 = (f32[768]{0:T(1024)S(1)}, f32[768]{0:T(1024)}, u32[]{:S(2)}) copy-start(f32[768]{0:T(1024)} %constant.66) | copy-start | bytes 9220
  27.3 2.0 %copy-start.4 = (f32[768]{0:T(1024)S(1)}, f32[768]{0:T(1024)}, u32[]{:S(2)}) copy-start(f32[768]{0:T(1024)} %constant.65) | copy-start | bytes 9220
  27.3 2.0 %copy-start.5 = (f32[768]{0:T(1024)S(1)}, f32[768]{0:T(1024)}, u32[]{:S(2)}) copy-start(f32[768]{0:T(1024)} %constant.64) | copy-start | bytes 9220
  27.3 2.0 %copy-start.6 = (f32[768]{0:T(1024)S(1)}, f32[768]{0:T(1024)}, u32[]{:S(2)}) copy-start(f32[768]{0:T(1024)} %constant.63) | copy-start | bytes 9220
  28.4 8.2 %copy-start.1 = (f32[32,32]{1,0:T(8,128)S(1)}, f32[32,32]{1,0:T(8,128)}, u32[]{:S(2)}) copy-start(f32[32,32]{1,0:T(8,128)} %constant.51.clone) | copy-start | bytes 12292
  46.4 1.7 %copy-start.2 = (f32[32,32]{1,0:T(8,128)S(1)}, f32[32,32]{1,0:T(8,128)}, u32[]{:S(2)}) copy-start(f32[32,32]{1,0:T(8,128)} %constant.57.clone) | copy-start | bytes 12292

commit v12 on v10

--- a/solution.py
+++ b/solution.py
@@ -42,6 +42,38 @@
     place = lax.axis_index("row") * rows - width + jnp.arange(rows + 2 * width)
     inside = (place >= 0) & (place < rows * count)
     return joined[0], joined[1], inside
+
+
+def core_pairs(count):
+    return [(source, source ^ 1) for source in range(count)]
+
+
+def chip_groups(count):
+    return [[2 * chip + core for chip in range(count // 2)] for core in range(2)]
+
+
+def gather_steps(sent):
+    count = sent.shape[0]
+    core = lax.axis_index("tm") % 2
+    pairs = sent.reshape((count // 2, 2) + sent.shape[1:])
+    keep = jnp.where(core == 0, pairs[:, 0], pairs[:, 1])
+    give = jnp.where(core == 0, pairs[:, 1], pairs[:, 0])
+    got = lax.ppermute(give, "tm", core_pairs(count))
+    both = jnp.where(core == 0, jnp.stack([keep, got], 1), jnp.stack([got, keep], 1))
+    received = lax.all_to_all(both, "tm", 0, 0, axis_index_groups=chip_groups(count), tiled=True)
+    return received.reshape(sent.shape)
+
+
+def scatter_steps(signal):
+    count = signal.shape[0]
+    core = lax.axis_index("tm") % 2
+    pairs = signal.reshape((count // 2, 2) + signal.shape[1:])
+    received = lax.all_to_all(pairs, "tm", 0, 0, axis_index_groups=chip_groups(count), tiled=True)
+    mine = jnp.where(core == 0, received[:, 0], received[:, 1])
+    other = jnp.where(core == 0, received[:, 1], received[:, 0])
+    got = lax.ppermute(other, "tm", core_pairs(count))
+    both = jnp.where(core == 0, jnp.stack([mine, got], 1), jnp.stack([got, mine], 1))
+    return both.reshape(signal.shape)
 
 
 def transform_matrices(total):
@@ -173,7 +205,7 @@
     extended = rows + 2 * margin
     lane = 128
     sent = column_tiles(wide_side, tiles, width, margin).reshape(tiles, -1, lane)
-    gathered = lax.all_to_all(sent, "tm", 0, 0, tiled=True).reshape(tiles, extended * width)
+    gathered = gather_steps(sent).reshape(tiles, extended * width)
     spectrum = jnp.dot(forward, gathered, precision=highest)
     spectrum = spectrum.reshape(2, half, extended, width).transpose(0, 2, 1, 3)
     spectrum = spectrum.reshape(2, extended, half * width)
@@ -190,7 +222,7 @@
     solved = solved.transpose(0, 2, 1, 3).reshape(total, rows * span)
     signal = jnp.dot(inverse, solved, precision=highest)
     signal = signal.reshape(total, -1, lane)
-    returned = lax.all_to_all(signal, "tm", 0, 0, tiled=True)
+    returned = scatter_steps(signal)
     returned = returned.reshape(tiles, rows, span).transpose(1, 0, 2)
     return returned.reshape(steps_dev, rows, cols)
 

time: 59.5 us -> 61.9 us (1.040)
  starting transfers between devices: 14.9 us -> 17.7 us
  blocking collectives: 12.4 us -> 10.8 us
    ppermute x0 -> x2, starting transfers between devices: none -> 4.31 us  [the longest x1 3.04 us: scatter_steps(): got = lax.ppermute(other, 'tm', core_pairs(count))]
    ppermute x0 -> x2, waiting for transfers between devices: none -> 2.08 us  [the longest x1 1.12 us: gather_steps(): got = lax.ppermute(give, 'tm', core_pairs(count))]
    all_to_all x1, blocking collectives: 12.4 us -> 10.8 us  [scatter_steps(): lax.all_to_all(pairs, 'tm', 0, 0, axis_index_groups=chip_groups(count), t...]
    all_to_all x1, waiting for transfers between devices: 6.19 us -> 4.64 us  [gather_steps(): lax.all_to_all(both, 'tm', 0, 0, axis_index_groups=chip_groups(count), ti...]
    reshape x2 -> x0, local copies, waits for them, and re-layouts: 1.52 us -> none  [the longest x1 1.26 us: body(): column_tiles(wide_side, tiles, width, margin).reshape(tiles, -1, lane)]
    all_to_all x1, starting transfers between devices: 8.26 us -> 6.75 us  [gather_steps(): lax.all_to_all(both, 'tm', 0, 0, axis_index_groups=chip_groups(count), ti...]
    select_n x0 -> x3, local copies, waits for them, and re-layouts: none -> 1.45 us  [the longest x1 1.16 us: gather_steps(): jnp.where(core == 0, jnp.stack([keep, got], 1), jnp.stack([got, keep], 1))]
  transfers between devices with their start and end apart: 3 -> 5, of which waited for: 1 -> 3; matrix products, arithmetic and copies ran while one was open for 12% -> 12% of each run, Pallas kernels for 0% -> 0%
where the time goes in v12:
time: 61.9 us; the launch traced here: 61 us
  starting transfers between devices  17.7 us (29%)
  local copies, waits for them, and re-layouts  15.9 us (26%)
  blocking collectives  10.8 us (17%)
  waiting for transfers between devices  6.73 us (11%)
  Pallas kernels  6.01 us (10%)
  other arithmetic  2.26 us (4%)
  matrix products  1.16 us (2%)
    all_to_all x1, blocking collectives, scatter_steps(): lax.all_to_all(pairs, 'tm', 0, 0, axis_index_groups=chip_groups(count), t...  10.8 us
    all_to_all x1, starting transfers between devices, gather_steps(): lax.all_to_all(both, 'tm', 0, 0, axis_index_groups=chip_groups(count), ti...  6.75 us
    pallas_call x1, Pallas kernels, solve_slots(): pl.pallas_call(solve_kernel, out_shape=jax.ShapeDtypeStruct(spectrum.shap...  6.01 us
    ppermute x1, starting transfers between devices, with_halo(): low = lax.ppermute(bottom, 'row', forward)  4.76 us
    all_to_all x1, waiting for transfers between devices, gather_steps(): lax.all_to_all(both, 'tm', 0, 0, axis_index_groups=chip_groups(count), ti...  4.64 us
    ppermute x1, starting transfers between devices, scatter_steps(): got = lax.ppermute(other, 'tm', core_pairs(count))  3.04 us
    another operation x8, local copies, waits for them, and re-layouts, body(): jnp.tile(f, (1, half))  1.98 us
    ppermute x1, starting transfers between devices, with_halo(): high = lax.ppermute(top, 'row', backward)  1.92 us
  transfers between devices with their start and end apart: 5, of which 3 were waited for; matrix products, arithmetic and copies ran while one was open for 12% of the time, Pallas kernels for 0%

profile of v12, /device:TPU:97, one launch (start us, length us, event | category | flops | bytes accessed | tf_op | source)
XLA Modules:
  0.0 61.0 jit_solution(1751469061618561760)
XLA Ops:
  0.0 0.0 copy-start
  0.0 0.8 %slice_bitcast_fusion.3 = (f32[1,8,1024]{2,1,0:T(8,128)S(1)}, f32[1,8,1024]{2,1,0:T(8,128)S(1)}) fusion(f32[64,1024]{1,0:T(8,128)} %param.11), kind=kLoop, calls=%fused_computation.30 | loop fusion | bytes 131072 | tf_op jit(solution)/shard_map/stack | solution.py:36
  0.8 0.8 %fusion.13 = (f32[1,8,1024]{2,1,0:T(8,128)S(1)}, f32[1,8,1024]{2,1,0:T(8,128)S(1)}) fusion(f32[1,64,1024]{2,1,0:T(8,128)} %param.10), kind=kLoop, calls=%fused_computation.46 | loop fusion | bytes 131072 | tf_op jit(solution)/shard_map/slice | solution.py:36
  1.6 1.9 %collective-permute-start.1 = (f32[2,8,1024]{2,1,0:T(8,128)S(1)}, f32[2,8,1024]{2,1,0:T(8,128)S(1)}, u32[]{:S(2)}, u32[]{:S(2)}) collective-permute-start(f32[2,8,1024]{2,1,0:T(8,128)S(1)} %get-tuple-element.8), channel_id=1, source_target_pairs={{1,0},{2,1},{3,2},{4,3},{5,4},{6,5},{7,6},{9,8},{10,9},{11,10},{12... | collective-permute-start | bytes 196616 | tf_op jit(solution)/shard_map/ppermute | solution.py:39
  3.5 4.8 %collective-permute-start = (f32[2,8,1024]{2,1,0:T(8,128)S(1)}, f32[2,8,1024]{2,1,0:T(8,128)S(1)}, u32[]{:S(2)}, u32[]{:S(2)}) collective-permute-start(f32[2,8,1024]{2,1,0:T(8,128)S(1)} %get-tuple-element.7), channel_id=1, source_target_pairs={{0,1},{1,2},{2,3},{3,4},{4,5},{5,6},{6,7},{8,9},{9,10},{10,11},{11... | collective-permute-start | bytes 196616 | tf_op jit(solution)/shard_map/ppermute | solution.py:38
  8.3 1.1 %copy.50 = f32[64,1024]{0,1:T(8,128)S(1)} copy(f32[64,1024]{1,0:T(8,128)} %param.11) | data formatting | bytes 524288 | tf_op args[1]
  9.5 0.0 copy-done
  9.5 0.2 copy.51
  9.7 0.0 collective-permute-done.1
  9.7 0.3 copy.53
  10.1 0.0 collective-permute-done
  10.1 0.3 copy.52
  10.4 0.6 %pad_maximum_fusion = f32[2,80,1024]{1,2,0:T(8,128)S(1)} fusion(f32[2,8,1024]{1,2,0:T(8,128)S(1)} %copy.53, f32[1,64,1024]{1,2,0:T(8,128)S(1)} %bitcast.70, f32[1,64,1024]{1,2,0:T(8,128)S(1)} %copy.51, f32[2,8,1024]{1,2,0:T(8,128)S(1)} %copy.52), kind=kLoop, calls=%fused_computation.1 | loop fusion | flops 491520 | bytes 1310720 | tf_op jit(solution)/shard_map/concatenate | solution.py:41
  11.0 0.1 slice_bitcast_fusion.1
  11.1 0.1 pad_slice_fusion.1
  11.2 0.1 maximum_bitcast_fusion
  11.3 0.4 copy.54
  11.7 0.5 reshape_reshape.10
  12.2 1.3 %collective-permute-start.2 = (f32[16,30,128]{2,1,0:T(8,128)S(1)}, f32[16,30,128]{2,1,0:T(8,128)S(1)}, u32[]{:S(2)}, u32[]{:S(2)}) collective-permute-start(f32[16,30,128]{2,1,0:T(8,128)S(1)} %select_bitcast_fusion), channel_id=1, source_target_pairs={{0,8},{8,0},{16,24},{24,16},{32,40},{40,32},{48,56},{56,48},{64,72... | collective-permute-start | bytes 737288 | tf_op jit(solution)/shard_map/ppermute | solution.py:61
  13.5 1.1 %collective-permute-done.2 = f32[16,30,128]{2,1,0:T(8,128)S(1)} collective-permute-done((f32[16,30,128]{2,1,0:T(8,128)S(1)}, f32[16,30,128]{2,1,0:T(8,128)S(1)}, u32[]{:S(2)}, u32[]{:S(2)}) %collective-permute-start.2) | collective-permute-done | bytes 245792 | tf_op jit(solution)/shard_map/ppermute | solution.py:61
  14.7 1.2 %copy.59 = f32[16,2,30,128]{3,1,2,0:T(2,128)} copy(f32[16,2,30,128]{3,2,0,1:T(8,128)S(1)} %maximum_select_fusion) | data formatting | bytes 983040 | tf_op jit(solution)/shard_map/jit(_where)/select_n | solution.py:62
  15.8 6.8 %all-to-all-start = ((f32[16,2,30,128]{3,1,2,0:T(2,128)}), f32[16,2,30,128]{3,1,2,0:T(2,128)S(1)}, u32[]{:S(2)}, u32[]{:S(2)}) async-start(f32[16,2,30,128]{3,1,2,0:T(2,128)} %copy.59), calls=%async_computation | async-start | bytes 983040 | tf_op jit(solution)/shard_map/all_to_all | solution.py:63
  22.6 0.1 broadcast_and_fusion
  22.7 0.2 copy.64
  22.9 0.2 broadcast_add_fusion.2
  23.1 0.8 %copy.68.north_ref = f32[80,768]{1,0:T(8,128)} copy(f32[80,768]{0,1:T(8,128)S(1)} %bitcast.72) | data formatting | bytes 491520 | tf_op jit(solution)/shard_map/tile | solution.py:217
  24.0 0.9 %copy.69.south_ref = f32[80,768]{1,0:T(8,128)} copy(f32[80,768]{0,1:T(8,128)S(1)} %bitcast.73) | data formatting | bytes 491520 | tf_op jit(solution)/shard_map/add | solution.py:184
  24.9 0.0 copy-start.3
  24.9 0.0 copy-start.4
  24.9 0.0 copy-start.5
  24.9 0.0 copy-start.6
  24.9 0.8 %copy.70.east_ref = f32[80,768]{1,0:T(8,128)} copy(f32[80,768]{0,1:T(8,128)S(1)} %bitcast.74) | data formatting | bytes 491520 | tf_op jit(solution)/shard_map/tile | solution.py:217
  25.8 0.9 %copy.71.west_ref = f32[80,768]{1,0:T(8,128)} copy(f32[80,768]{0,1:T(8,128)S(1)} %bitcast.75) | data formatting | bytes 491520 | tf_op jit(solution)/shard_map/add | solution.py:184
  26.7 0.1 copy.62
  26.9 0.0 copy-done.3
  26.9 0.0 copy-done.4
  26.9 0.0 copy-done.5
  26.9 0.0 copy-done.6
  26.9 0.0 copy-start.1
  26.9 1.1 %divide_select_fusion = (f32[80,768]{1,0:T(8,128)}, f32[80,768]{1,0:T(8,128)}, f32[80,768]{1,0:T(8,128)}, f32[80,768]{1,0:T(8,128)}, f32[80,768]{1,0:T(8,128)}) fusion(pred[80,768]{1,0:T(8,128)(4,1)S(1)} %copy.64, f32[768]{0:T(1024)S(1)} %copy-done.3, f32[768]{0:T(1024)S(1)} %copy-done.4, f32[80,768]{1,0:T(8,128)S(1)} %copy.62, f32[768]{0:T(1024)S(1)} %copy-done.5, ...), kind=kLoop, calls=%fused_computation.20 | loop fusion | flops 737280 | bytes 1548288 | tf_op jit(solution)/shard_map/jit(_where)/select_n | solution.py:183
  28.1 4.6 %all-to-all-done = f32[16,2,30,128]{3,1,2,0:T(2,128)S(1)} async-done(((f32[16,2,30,128]{3,1,2,0:T(2,128)}), f32[16,2,30,128]{3,1,2,0:T(2,128)S(1)}, u32[]{:S(2)}, u32[]{:S(2)}) %all-to-all-start) | async-done | bytes 491552 | tf_op jit(solution)/shard_map/all_to_all | solution.py:63
  32.7 0.1 copy.60
  32.8 0.0 copy-done.1
  32.8 0.8 %fusion = f32[32,3840]{1,0:T(8,128)S(1)} fusion(f32[32,32]{1,0:T(8,128)S(1)} %copy-done.1, f32[4,8,30,128]{3,2,1,0:T(8,128)S(1)} %bitcast.71), kind=kOutput, calls=%fused_computation.9 | convolution fusion | flops 47185920 | bytes 987136 | tf_op jit(solution)/shard_map/dot_general | solution.py:209
  33.6 0.8 %reshape.98 = f32[2,16,80,48]{3,2,1,0:T(8,128)S(1)} reshape(f32[32,3840]{1,0:T(8,128)S(1)} %fusion) | data formatting | bytes 983040 | tf_op jit(solution)/shard_map/reshape | solution.py:210
  34.4 0.4 copy.61
  34.8 1.1 %copy.67.spec_ref = f32[2,80,768]{2,1,0:T(8,128)} copy(f32[2,80,768]{1,2,0:T(8,128)S(1)} %bitcast.66) | data formatting | bytes 983040 | tf_op jit(solution)/shard_map/reshape | solution.py:211
  35.9 6.0 %shard_map.100 = f32[2,80,768]{2,1,0:T(8,128)} custom-call(f32[2,80,768]{2,1,0:T(8,128)} %copy.67.spec_ref, f32[80,768]{1,0:T(8,128)} %copy.68.north_ref, f32[80,768]{1,0:T(8,128)} %copy.69.south_ref, f32[80,768]{1,0:T(8,128)} %copy.70.east_ref, f32[80,768]{1,0:T(8,128)} %copy.71.west_ref, f32[80,768]{1,0:T(8,128)} %get-tuple-element.29.diag_a_ref, ...), custom_call_target="tpu_custom_call" | custom-call | tf_op jit(solution)/shard_map/pallas_call | solution.py:186
  41.9 1.3 %copy.72 = f32[2,80,768]{1,2,0:T(8,128)S(1)} copy(f32[2,80,768]{2,1,0:T(8,128)} %shard_map.100) | data formatting | bytes 983040 | tf_op jit(solution)/shard_map/pallas_call | solution.py:186
  43.2 0.2 slice_bitcast_fusion
  43.4 0.0 copy-start.2
  43.4 0.4 copy.73
  43.7 0.5 reshape.101
  44.2 0.0 copy-done.2
  44.2 0.3 convolution_bitcast_fusion
  44.6 10.8 %all_to_all.10 = f32[16,2,16,128]{3,2,1,0:T(8,128)S(1)} all-to-all(f32[16,2,16,128]{3,2,1,0:T(8,128)S(1)} %bitcast.78), channel_id=1, replica_groups={{0,16,32,48,64,80,96,112,128,144,160,176,192,208,224,240},{8,24,40,56,7..., dimensions={0} | all-to-all | bytes 524288 | tf_op jit(solution)/shard_map/all_to_all | solution.py:71
  55.4 3.0 %collective-permute-start.3 = (f32[16,16,128]{2,1,0:T(8,128)S(1)}, f32[16,16,128]{2,1,0:T(8,128)S(1)}, u32[]{:S(2)}, u32[]{:S(2)}) collective-permute-start(f32[16,16,128]{2,1,0:T(8,128)S(1)} %select_bitcast_fusion.1), channel_id=1, source_target_pairs={{0,8},{8,0},{16,24},{24,16},{32,40},{40,32},{48,56},{56,48},{64,72... | collective-permute-start | bytes 393224 | tf_op jit(solution)/shard_map/ppermute | solution.py:74
  58.5 1.0 %collective-permute-done.3 = f32[16,16,128]{2,1,0:T(8,128)S(1)} collective-permute-done((f32[16,16,128]{2,1,0:T(8,128)S(1)}, f32[16,16,128]{2,1,0:T(8,128)S(1)}, u32[]{:S(2)}, u32[]{:S(2)}) %collective-permute-start.3) | collective-permute-done | bytes 131104 | tf_op jit(solution)/shard_map/ppermute | solution.py:74
  59.5 0.3 select_n.91
  59.8 0.3 copy.79
  60.1 0.9 %copy.80 = f32[1,64,1024]{2,1,0:T(8,128)} copy(f32[1,64,1024]{1,2,0:T(8,128)S(1)} %bitcast.69) | data formatting | bytes 524288 | tf_op jit(solution)/shard_map/reshape | solution.py:227
  (18 shorter events, 0.4 us)
Async XLA Ops:
  0.0 9.5 %copy-start = (f32[1,64,1024]{2,1,0:T(8,128)S(1)}, f32[1,64,1024]{2,1,0:T(8,128)}, u32[]{:S(2)}) copy-start(f32[1,64,1024]{2,1,0:T(8,128)} %param.10) | copy-start | bytes 786436
  1.6 8.1 %collective-permute-start.1 = (f32[2,8,1024]{2,1,0:T(8,128)S(1)}, f32[2,8,1024]{2,1,0:T(8,128)S(1)}, u32[]{:S(2)}, u32[]{:S(2)}) collective-permute-start(f32[2,8,1024]{2,1,0:T(8,128)S(1)} %get-tuple-element.8), channel_id=1, source_target_pairs={{1,0},{2,1},{3,2},{4,3},{5,4},{6,5},{7,6},{9,8},{10,9},{11,10},{12... | collective-permute-start | bytes 196616 | tf_op jit(solution)/shard_map/ppermute | solution.py:39
  3.5 6.5 %collective-permute-start = (f32[2,8,1024]{2,1,0:T(8,128)S(1)}, f32[2,8,1024]{2,1,0:T(8,128)S(1)}, u32[]{:S(2)}, u32[]{:S(2)}) collective-permute-start(f32[2,8,1024]{2,1,0:T(8,128)S(1)} %get-tuple-element.7), channel_id=1, source_target_pairs={{0,1},{1,2},{2,3},{3,4},{4,5},{5,6},{6,7},{8,9},{9,10},{10,11},{11... | collective-permute-start | bytes 196616 | tf_op jit(solution)/shard_map/ppermute | solution.py:38
  12.2 2.4 %collective-permute-start.2 = (f32[16,30,128]{2,1,0:T(8,128)S(1)}, f32[16,30,128]{2,1,0:T(8,128)S(1)}, u32[]{:S(2)}, u32[]{:S(2)}) collective-permute-start(f32[16,30,128]{2,1,0:T(8,128)S(1)} %select_bitcast_fusion), channel_id=1, source_target_pairs={{0,8},{8,0},{16,24},{24,16},{32,40},{40,32},{48,56},{56,48},{64,72... | collective-permute-start | bytes 737288 | tf_op jit(solution)/shard_map/ppermute | solution.py:61
  15.8 16.9 %all-to-all-start = ((f32[16,2,30,128]{3,1,2,0:T(2,128)}), f32[16,2,30,128]{3,1,2,0:T(2,128)S(1)}, u32[]{:S(2)}, u32[]{:S(2)}) async-start(f32[16,2,30,128]{3,1,2,0:T(2,128)} %copy.59), calls=%async_computation | async-start | bytes 983040 | tf_op jit(solution)/shard_map/all_to_all | solution.py:63
  24.9 2.0 %copy-start.3 = (f32[768]{0:T(1024)S(1)}, f32[768]{0:T(1024)}, u32[]{:S(2)}) copy-start(f32[768]{0:T(1024)} %constant.80) | copy-start | bytes 9220
  24.9 2.0 %copy-start.4 = (f32[768]{0:T(1024)S(1)}, f32[768]{0:T(1024)}, u32[]{:S(2)}) copy-start(f32[768]{0:T(1024)} %constant.79) | copy-start | bytes 9220
  24.9 2.0 %copy-start.5 = (f32[768]{0:T(1024)S(1)}, f32[768]{0:T(1024)}, u32[]{:S(2)}) copy-start(f32[768]{0:T(1024)} %constant.77) | copy-start | bytes 9220
  24.9 2.0 %copy-start.6 = (f32[768]{0:T(1024)S(1)}, f32[768]{0:T(1024)}, u32[]{:S(2)}) copy-start(f32[768]{0:T(1024)} %constant.78) | copy-start | bytes 9220
  26.9 5.9 %copy-start.1 = (f32[32,32]{1,0:T(8,128)S(1)}, f32[32,32]{1,0:T(8,128)}, u32[]{:S(2)}) copy-start(f32[32,32]{1,0:T(8,128)} %constant.65.clone) | copy-start | bytes 12292
  43.4 0.9 %copy-start.2 = (f32[32,32]{1,0:T(8,128)S(1)}, f32[32,32]{1,0:T(8,128)}, u32[]{:S(2)}) copy-start(f32[32,32]{1,0:T(8,128)} %constant.71.clone) | copy-start | bytes 12292
  55.4 4.0 %collective-permute-start.3 = (f32[16,16,128]{2,1,0:T(8,128)S(1)}, f32[16,16,128]{2,1,0:T(8,128)S(1)}, u32[]{:S(2)}, u32[]{:S(2)}) collective-permute-start(f32[16,16,128]{2,1,0:T(8,128)S(1)} %select_bitcast_fusion.1), channel_id=1, source_target_pairs={{0,8},{8,0},{16,24},{24,16},{32,40},{40,32},{48,56},{56,48},{64,72... | collective-permute-start | bytes 393224 | tf_op jit(solution)/shard_map/ppermute | solution.py:74

commit v13 on v10

--- a/solution.py
+++ b/solution.py
@@ -1,3 +1,4 @@
+import functools
 import math
 
 import jax
@@ -101,8 +102,8 @@
     return jnp.concatenate([main, extra], axis=2).transpose(1, 0, 2)
 
 
-def solve_kernel(spec_ref, north_ref, south_ref, east_ref, west_ref, diag_a_ref, diag_b_ref,
-                 inva_ref, invb_ref, invi_ref, imag_ref, out_ref):
+def solve_kernel(margin, spec_ref, north_ref, south_ref, east_ref, west_ref, diag_a_ref, diag_b_ref,
+                 inva_ref, invb_ref, invi_ref, imag_ref, interior_ref, out_ref):
     rows, lanes = north_ref.shape
 
     def coupled(x):
@@ -137,9 +138,11 @@
             else:
                 out_ref[0] = out_ref[0] + weight * corr_real
                 out_ref[1] = out_ref[1] + weight * corr_imag
-
-
-def solve_slots(spectrum, faces, shifts, inside):
+    inner = interior_ref.shape[1]
+    interior_ref[...] = out_ref[:, margin : margin + inner]
+
+
+def solve_slots(spectrum, faces, shifts, inside, margin):
     north, south, east, west, diagonal = faces
     real_a, real_b, imag = shifts
     diag_a = real_a + diagonal
@@ -151,9 +154,11 @@
     inv_imag = jnp.where(inside, -imag / mag_a, 0.0)
     operands = (spectrum, north, south + courant_rows, east, west + courant_cols,
                 diag_a, diag_b, inv_a, inv_b, inv_imag, jnp.asarray(imag))
+    parts, extended, lanes = spectrum.shape
     return pl.pallas_call(
-        solve_kernel,
-        out_shape=jax.ShapeDtypeStruct(spectrum.shape, spectrum.dtype),
+        functools.partial(solve_kernel, margin),
+        out_shape=jax.ShapeDtypeStruct((parts, extended - 2 * margin, lanes), spectrum.dtype),
+        scratch_shapes=[pltpu.VMEM(spectrum.shape, jnp.float32)],
     )(*operands)
 
 
@@ -184,9 +189,9 @@
     inside = jnp.tile(inside, (1, half))
     faces = tuple(jnp.tile(f, (1, half)) for f in tile_faces(kappa_rows, tile, tiles, width, margin))
     shifts = slot_shifts(half, total, width)
-    solved = solve_slots(spectrum, faces, shifts, inside)
-
-    solved = solved.reshape(2, extended, half, width)[:, margin : margin + rows, :, margin : margin + span]
+    solved = solve_slots(spectrum, faces, shifts, inside, margin)
+
+    solved = solved.reshape(2, rows, half, width)[..., margin : margin + span]
     solved = solved.transpose(0, 2, 1, 3).reshape(total, rows * span)
     signal = jnp.dot(inverse, solved, precision=highest)
     signal = signal.reshape(total, -1, lane)

time: 59.5 us -> 59.8 us (level)
    reshape x0 -> x1, local copies, waits for them, and re-layouts: none -> 1.54 us  [body(): solved = solved.reshape(2, rows, half, width)[..., margin:margin + span]]
    pallas_call x1 -> x0, local copies, waits for them, and re-layouts: 1.29 us -> none  [solve_slots(): pl.pallas_call(solve_kernel, out_shape=jax.ShapeDtypeStruct(spectrum.shap...]
where the time goes in v13:
time: 59.8 us; the launch traced here: 58.9 us
  local copies, waits for them, and re-layouts  15.8 us (26%)
  starting transfers between devices  14.9 us (25%)
  blocking collectives  12.4 us (21%)
  waiting for transfers between devices  6.19 us (10%)
  Pallas kernels  5.96 us (10%)
  other arithmetic  2.09 us (3%)
  matrix products  1.16 us (2%)
    all_to_all x1, blocking collectives, body(): returned = lax.all_to_all(signal, 'tm', 0, 0, tiled=True)  12.4 us
    all_to_all x1, starting transfers between devices, body(): lax.all_to_all(sent, 'tm', 0, 0, tiled=True)  8.26 us
    all_to_all x1, waiting for transfers between devices, body(): lax.all_to_all(sent, 'tm', 0, 0, tiled=True)  6.19 us
    pallas_call x1, Pallas kernels, solve_slots(): pl.pallas_call(functools.partial(solve_kernel, margin), out_shape=jax.Sha...  5.96 us
    ppermute x1, starting transfers between devices, with_halo(): low = lax.ppermute(bottom, 'row', forward)  4.76 us
    another operation x8, local copies, waits for them, and re-layouts, body(): jnp.tile(f, (1, half))  1.98 us
    ppermute x1, starting transfers between devices, with_halo(): high = lax.ppermute(top, 'row', backward)  1.92 us
    reshape x1, local copies, waits for them, and re-layouts, body(): solved = solved.reshape(2, rows, half, width)[..., margin:margin + span]  1.54 us
  transfers between devices with their start and end apart: 3, of which 1 were waited for; matrix products, arithmetic and copies ran while one was open for 12% of the time, Pallas kernels for 0%

profile of v13, /device:TPU:97, one launch (start us, length us, event | category | flops | bytes accessed | tf_op | source)
XLA Modules:
  0.0 58.9 jit_solution(7306686586386098987)
XLA Ops:
  0.0 0.0 copy-start
  0.0 0.8 %slice_bitcast_fusion.3 = (f32[1,8,1024]{2,1,0:T(8,128)S(1)}, f32[1,8,1024]{2,1,0:T(8,128)S(1)}) fusion(f32[64,1024]{1,0:T(8,128)} %param.11), kind=kLoop, calls=%fused_computation.24 | loop fusion | bytes 131072 | tf_op jit(solution)/shard_map/stack | solution.py:37
  0.8 0.8 %fusion.13 = (f32[1,8,1024]{2,1,0:T(8,128)S(1)}, f32[1,8,1024]{2,1,0:T(8,128)S(1)}) fusion(f32[1,64,1024]{2,1,0:T(8,128)} %param.10), kind=kLoop, calls=%fused_computation.40 | loop fusion | bytes 131072 | tf_op jit(solution)/shard_map/slice | solution.py:37
  1.6 1.9 %collective-permute-start.1 = (f32[2,8,1024]{2,1,0:T(8,128)S(1)}, f32[2,8,1024]{2,1,0:T(8,128)S(1)}, u32[]{:S(2)}, u32[]{:S(2)}) collective-permute-start(f32[2,8,1024]{2,1,0:T(8,128)S(1)} %get-tuple-element.8), channel_id=1, source_target_pairs={{1,0},{2,1},{3,2},{4,3},{5,4},{6,5},{7,6},{9,8},{10,9},{11,10},{12... | collective-permute-start | bytes 196616 | tf_op jit(solution)/shard_map/ppermute | solution.py:40
  3.5 4.8 %collective-permute-start = (f32[2,8,1024]{2,1,0:T(8,128)S(1)}, f32[2,8,1024]{2,1,0:T(8,128)S(1)}, u32[]{:S(2)}, u32[]{:S(2)}) collective-permute-start(f32[2,8,1024]{2,1,0:T(8,128)S(1)} %get-tuple-element.7), channel_id=1, source_target_pairs={{0,1},{1,2},{2,3},{3,4},{4,5},{5,6},{6,7},{8,9},{9,10},{10,11},{11... | collective-permute-start | bytes 196616 | tf_op jit(solution)/shard_map/ppermute | solution.py:39
  8.3 1.1 %copy.34 = f32[64,1024]{0,1:T(8,128)S(1)} copy(f32[64,1024]{1,0:T(8,128)} %param.11) | data formatting | bytes 524288 | tf_op args[1]
  9.5 0.0 copy-done
  9.5 0.2 copy.35
  9.7 0.0 collective-permute-done.1
  9.7 0.3 copy.37
  10.1 0.0 collective-permute-done
  10.1 0.3 copy.36
  10.4 0.6 %pad_maximum_fusion = f32[2,80,1024]{1,2,0:T(8,128)S(1)} fusion(f32[2,8,1024]{1,2,0:T(8,128)S(1)} %copy.37, f32[1,64,1024]{1,2,0:T(8,128)S(1)} %bitcast.42, f32[1,64,1024]{1,2,0:T(8,128)S(1)} %copy.35, f32[2,8,1024]{1,2,0:T(8,128)S(1)} %copy.36), kind=kLoop, calls=%fused_computation.2 | loop fusion | flops 491520 | bytes 1310720 | tf_op jit(solution)/shard_map/concatenate | solution.py:42
  11.0 0.1 slice_bitcast_fusion.1
  11.1 0.1 pad_slice_fusion.1
  11.2 0.1 maximum_bitcast_fusion
  11.3 0.4 copy.38
  11.7 1.3 %reshape.102 = f32[32,30,128]{2,1,0:T(8,128)} reshape(f32[32,80,48]{2,1,0:T(8,128)S(1)} %copy.38) | data formatting | bytes 983040 | tf_op jit(solution)/shard_map/reshape | solution.py:180
  12.9 8.3 %all-to-all-start = ((f32[32,30,128]{2,1,0:T(8,128)}), f32[32,30,128]{2,1,0:T(8,128)S(1)}, u32[]{:S(2)}, u32[]{:S(2)}) async-start(f32[32,30,128]{2,1,0:T(8,128)} %reshape.102), calls=%async_computation | async-start | bytes 1048576 | tf_op jit(solution)/shard_map/all_to_all | solution.py:181
  21.2 0.1 broadcast_and_fusion
  21.3 0.2 copy.42
  21.5 0.2 broadcast_add_fusion.2
  21.7 0.8 %copy.46.north_ref = f32[80,768]{1,0:T(8,128)} copy(f32[80,768]{0,1:T(8,128)S(1)} %bitcast.44) | data formatting | bytes 491520 | tf_op jit(solution)/shard_map/tile | solution.py:190
  22.6 0.9 %copy.47.south_ref = f32[80,768]{1,0:T(8,128)} copy(f32[80,768]{0,1:T(8,128)S(1)} %bitcast.45) | data formatting | bytes 491520 | tf_op jit(solution)/shard_map/add | solution.py:155
  23.5 0.0 copy-start.3
  23.5 0.0 copy-start.4
  23.5 0.0 copy-start.5
  23.5 0.0 copy-start.6
  23.5 0.9 %copy.48.east_ref = f32[80,768]{1,0:T(8,128)} copy(f32[80,768]{0,1:T(8,128)S(1)} %bitcast.46) | data formatting | bytes 491520 | tf_op jit(solution)/shard_map/tile | solution.py:190
  24.4 0.9 %copy.49.west_ref = f32[80,768]{1,0:T(8,128)} copy(f32[80,768]{0,1:T(8,128)S(1)} %bitcast.47) | data formatting | bytes 491520 | tf_op jit(solution)/shard_map/add | solution.py:155
  25.3 0.0 copy-start.1
  25.3 0.1 copy.40
  25.5 0.0 copy-done.3
  25.5 0.0 copy-done.4
  25.5 0.0 copy-done.5
  25.5 0.0 copy-done.6
  25.5 1.1 %divide_select_fusion = (f32[80,768]{1,0:T(8,128)}, f32[80,768]{1,0:T(8,128)}, f32[80,768]{1,0:T(8,128)}, f32[80,768]{1,0:T(8,128)}, f32[80,768]{1,0:T(8,128)}) fusion(pred[80,768]{1,0:T(8,128)(4,1)S(1)} %copy.42, f32[768]{0:T(1024)S(1)} %copy-done.3, f32[768]{0:T(1024)S(1)} %copy-done.4, f32[80,768]{1,0:T(8,128)S(1)} %copy.40, f32[768]{0:T(1024)S(1)} %copy-done.5, ...), kind=kLoop, calls=%fused_computation.16 | loop fusion | flops 737280 | bytes 1548288 | tf_op jit(solution)/shard_map/jit(_where)/select_n | solution.py:154
  26.6 6.2 %all-to-all-done = f32[32,30,128]{2,1,0:T(8,128)S(1)} async-done(((f32[32,30,128]{2,1,0:T(8,128)}), f32[32,30,128]{2,1,0:T(8,128)S(1)}, u32[]{:S(2)}, u32[]{:S(2)}) %all-to-all-start) | async-done | bytes 491552 | tf_op jit(solution)/shard_map/all_to_all | solution.py:181
  32.8 0.0 copy-done.1
  32.8 0.8 %fusion = f32[32,3840]{1,0:T(8,128)S(1)} fusion(f32[32,32]{1,0:T(8,128)S(1)} %copy-done.1, f32[4,8,30,128]{3,2,1,0:T(8,128)S(1)} %bitcast.43), kind=kOutput, calls=%fused_computation.8 | convolution fusion | flops 47185920 | bytes 987136 | tf_op jit(solution)/shard_map/dot_general | solution.py:182
  33.6 0.8 %reshape.104 = f32[2,16,80,48]{3,2,1,0:T(8,128)S(1)} reshape(f32[32,3840]{1,0:T(8,128)S(1)} %fusion) | data formatting | bytes 983040 | tf_op jit(solution)/shard_map/reshape | solution.py:183
  34.5 0.4 copy.39
  34.9 1.0 %copy.45.spec_ref = f32[2,80,768]{2,1,0:T(8,128)} copy(f32[2,80,768]{1,2,0:T(8,128)S(1)} %bitcast.39) | data formatting | bytes 983040 | tf_op jit(solution)/shard_map/reshape | solution.py:184
  35.9 6.0 %shard_map.100 = f32[2,64,768]{2,1,0:T(8,128)} custom-call(f32[2,80,768]{2,1,0:T(8,128)} %copy.45.spec_ref, f32[80,768]{1,0:T(8,128)} %copy.46.north_ref, f32[80,768]{1,0:T(8,128)} %copy.47.south_ref, f32[80,768]{1,0:T(8,128)} %copy.48.east_ref, f32[80,768]{1,0:T(8,128)} %copy.49.west_ref, f32[80,768]{1,0:T(8,128)} %get-tuple-element.29.diag_a_ref, ...), custom_call_target="tpu_custom_call" | custom-call | tf_op jit(solution)/shard_map/pallas_call | solution.py:158
  41.9 1.5 %reshape.106 = f32[2,64,16,48]{3,2,1,0:T(8,128)S(1)} reshape(f32[2,64,768]{2,1,0:T(8,128)} %shard_map.100) | data formatting | bytes 786432 | tf_op jit(solution)/shard_map/reshape | solution.py:194
  43.4 0.3 slice_bitcast_fusion
  43.8 0.0 copy-start.2
  43.8 0.3 copy.50
  44.1 0.5 reshape.107
  44.6 0.0 copy-done.2
  44.6 0.4 convolution_bitcast_fusion
  45.0 12.4 %all_to_all.10 = f32[32,16,128]{2,1,0:T(8,128)S(1)} all-to-all(f32[32,16,128]{2,1,0:T(8,128)S(1)} %bitcast.50), channel_id=1, replica_groups=mesh['tm'=32,'row'=8] {'tm'}, dimensions={0} | all-to-all | bytes 524288 | tf_op jit(solution)/shard_map/all_to_all | solution.py:198
  57.4 0.3 reshape.109
  57.7 0.3 copy.51
  58.0 0.9 %copy.52 = f32[1,64,1024]{2,1,0:T(8,128)} copy(f32[1,64,1024]{1,2,0:T(8,128)S(1)} %bitcast.41) | data formatting | bytes 524288 | tf_op jit(solution)/shard_map/reshape | solution.py:200
  (11 shorter events, 0.3 us)
Async XLA Ops:
  0.0 9.5 %copy-start = (f32[1,64,1024]{2,1,0:T(8,128)S(1)}, f32[1,64,1024]{2,1,0:T(8,128)}, u32[]{:S(2)}) copy-start(f32[1,64,1024]{2,1,0:T(8,128)} %param.10) | copy-start | bytes 786436
  1.6 8.1 %collective-permute-start.1 = (f32[2,8,1024]{2,1,0:T(8,128)S(1)}, f32[2,8,1024]{2,1,0:T(8,128)S(1)}, u32[]{:S(2)}, u32[]{:S(2)}) collective-permute-start(f32[2,8,1024]{2,1,0:T(8,128)S(1)} %get-tuple-element.8), channel_id=1, source_target_pairs={{1,0},{2,1},{3,2},{4,3},{5,4},{6,5},{7,6},{9,8},{10,9},{11,10},{12... | collective-permute-start | bytes 196616 | tf_op jit(solution)/shard_map/ppermute | solution.py:40
  3.5 6.5 %collective-permute-start = (f32[2,8,1024]{2,1,0:T(8,128)S(1)}, f32[2,8,1024]{2,1,0:T(8,128)S(1)}, u32[]{:S(2)}, u32[]{:S(2)}) collective-permute-start(f32[2,8,1024]{2,1,0:T(8,128)S(1)} %get-tuple-element.7), channel_id=1, source_target_pairs={{0,1},{1,2},{2,3},{3,4},{4,5},{5,6},{6,7},{8,9},{9,10},{10,11},{11... | collective-permute-start | bytes 196616 | tf_op jit(solution)/shard_map/ppermute | solution.py:39
  12.9 19.9 %all-to-all-start = ((f32[32,30,128]{2,1,0:T(8,128)}), f32[32,30,128]{2,1,0:T(8,128)S(1)}, u32[]{:S(2)}, u32[]{:S(2)}) async-start(f32[32,30,128]{2,1,0:T(8,128)} %reshape.102), calls=%async_computation | async-start | bytes 1048576 | tf_op jit(solution)/shard_map/all_to_all | solution.py:181
  23.5 2.0 %copy-start.3 = (f32[768]{0:T(1024)S(1)}, f32[768]{0:T(1024)}, u32[]{:S(2)}) copy-start(f32[768]{0:T(1024)} %constant.66) | copy-start | bytes 9220
  23.5 2.0 %copy-start.4 = (f32[768]{0:T(1024)S(1)}, f32[768]{0:T(1024)}, u32[]{:S(2)}) copy-start(f32[768]{0:T(1024)} %constant.65) | copy-start | bytes 9220
  23.5 2.0 %copy-start.5 = (f32[768]{0:T(1024)S(1)}, f32[768]{0:T(1024)}, u32[]{:S(2)}) copy-start(f32[768]{0:T(1024)} %constant.63) | copy-start | bytes 9220
  23.5 2.0 %copy-start.6 = (f32[768]{0:T(1024)S(1)}, f32[768]{0:T(1024)}, u32[]{:S(2)}) copy-start(f32[768]{0:T(1024)} %constant.64) | copy-start | bytes 9220
  25.3 7.6 %copy-start.1 = (f32[32,32]{1,0:T(8,128)S(1)}, f32[32,32]{1,0:T(8,128)}, u32[]{:S(2)}) copy-start(f32[32,32]{1,0:T(8,128)} %constant.51.clone) | copy-start | bytes 12292
  43.8 0.8 %copy-start.2 = (f32[32,32]{1,0:T(8,128)S(1)}, f32[32,32]{1,0:T(8,128)}, u32[]{:S(2)}) copy-start(f32[32,32]{1,0:T(8,128)} %constant.57.clone) | copy-start | bytes 12292

commit v14 on v10

--- a/solution.py
+++ b/solution.py
@@ -37,11 +37,11 @@
     bottom, top = lax.optimization_barrier((bottom, top))
     low = lax.ppermute(bottom, "row", forward)
     high = lax.ppermute(top, "row", backward)
-    joined = jnp.concatenate([right_side, kappa[None]], axis=0)
-    joined = jnp.concatenate([low, joined, high], axis=1)
+    wide_side = jnp.concatenate([low[0], right_side[0], high[0]], axis=0)
+    kappa_rows = jnp.concatenate([low[1], kappa, high[1]], axis=0)
     place = lax.axis_index("row") * rows - width + jnp.arange(rows + 2 * width)
     inside = (place >= 0) & (place < rows * count)
-    return joined[0], joined[1], inside
+    return wide_side, kappa_rows, inside
 
 
 def transform_matrices(total):

time: 59.5 us -> 59 us (level)
    unnamed x17 -> x21, local copies, waits for them, and re-layouts: 1.43 us -> 2.21 us
    ppermute x2 -> x0, local copies, waits for them, and re-layouts: 0.66 us -> none  [the longest x1 0.33 us: with_halo(): high = lax.ppermute(top, 'row', backward)]
  transfers between devices with their start and end apart: 3 -> 3, of which waited for: 1 -> 1; matrix products, arithmetic and copies ran while one was open for 12% -> 13% of each run, Pallas kernels for 0% -> 0%
where the time goes in v14:
time: 59 us; the launch traced here: 58.3 us
  local copies, waits for them, and re-layouts  15.6 us (26%)
  starting transfers between devices  14.8 us (25%)
  blocking collectives  12.4 us (21%)
  waiting for transfers between devices  6.03 us (10%)
  Pallas kernels  6.01 us (10%)
  other arithmetic  1.92 us (3%)
  matrix products  1.16 us (2%)
    all_to_all x1, blocking collectives, body(): returned = lax.all_to_all(signal, 'tm', 0, 0, tiled=True)  12.4 us
    all_to_all x1, starting transfers between devices, body(): lax.all_to_all(sent, 'tm', 0, 0, tiled=True)  8.13 us
    all_to_all x1, waiting for transfers between devices, body(): lax.all_to_all(sent, 'tm', 0, 0, tiled=True)  6.03 us
    pallas_call x1, Pallas kernels, solve_slots(): pl.pallas_call(solve_kernel, out_shape=jax.ShapeDtypeStruct(spectrum.shap...  6.01 us
    ppermute x1, starting transfers between devices, with_halo(): low = lax.ppermute(bottom, 'row', forward)  4.76 us
    unnamed x21, local copies, waits for them, and re-layouts  2.21 us
    another operation x8, local copies, waits for them, and re-layouts, body(): jnp.tile(f, (1, half))  1.98 us
    ppermute x1, starting transfers between devices, with_halo(): high = lax.ppermute(top, 'row', backward)  1.92 us
  transfers between devices with their start and end apart: 3, of which 1 were waited for; matrix products, arithmetic and copies ran while one was open for 13% of the time, Pallas kernels for 0%

profile of v14, /device:TPU:97, one launch (start us, length us, event | category | flops | bytes accessed | tf_op | source)
XLA Modules:
  0.0 58.3 jit_solution(3729439683983251988)
XLA Ops:
  0.0 0.0 copy-start
  0.0 0.8 %slice_bitcast_fusion.1 = (f32[1,8,1024]{2,1,0:T(8,128)S(1)}, f32[1,8,1024]{2,1,0:T(8,128)S(1)}) fusion(f32[64,1024]{1,0:T(8,128)} %param.11), kind=kLoop, calls=%fused_computation.26 | loop fusion | bytes 131072 | tf_op jit(solution)/shard_map/stack | solution.py:36
  0.8 0.8 %fusion.21 = (f32[1,8,1024]{2,1,0:T(8,128)S(1)}, f32[1,8,1024]{2,1,0:T(8,128)S(1)}) fusion(f32[1,64,1024]{2,1,0:T(8,128)} %param.10), kind=kLoop, calls=%fused_computation.57 | loop fusion | bytes 131072 | tf_op jit(solution)/shard_map/slice | solution.py:36
  1.6 1.9 %collective-permute-start.1 = (f32[2,8,1024]{2,1,0:T(8,128)S(1)}, f32[2,8,1024]{2,1,0:T(8,128)S(1)}, u32[]{:S(2)}, u32[]{:S(2)}) collective-permute-start(f32[2,8,1024]{2,1,0:T(8,128)S(1)} %get-tuple-element.8), channel_id=1, source_target_pairs={{1,0},{2,1},{3,2},{4,3},{5,4},{6,5},{7,6},{9,8},{10,9},{11,10},{12... | collective-permute-start | bytes 196616 | tf_op jit(solution)/shard_map/ppermute | solution.py:39
  3.6 4.8 %collective-permute-start = (f32[2,8,1024]{2,1,0:T(8,128)S(1)}, f32[2,8,1024]{2,1,0:T(8,128)S(1)}, u32[]{:S(2)}, u32[]{:S(2)}) collective-permute-start(f32[2,8,1024]{2,1,0:T(8,128)S(1)} %get-tuple-element.7), channel_id=1, source_target_pairs={{0,1},{1,2},{2,3},{3,4},{4,5},{5,6},{6,7},{8,9},{9,10},{10,11},{11... | collective-permute-start | bytes 196616 | tf_op jit(solution)/shard_map/ppermute | solution.py:38
  8.3 0.1 iota_compare_fusion.2
  8.4 0.1 broadcast_and_fusion
  8.5 1.1 %copy.66 = f32[1,64,1024]{1,2,0:T(8,128)S(1)} copy(f32[1,64,1024]{2,1,0:T(8,128)} %param.10) | data formatting | bytes 524288 | tf_op args[0]
  9.7 0.0 copy-done
  9.7 0.2 copy.72
  9.9 0.2 copy.75
  10.1 0.0 collective-permute-done.1
  10.1 0.2 copy.88
  10.3 0.0 collective-permute-done
  10.4 0.2 copy.87
  10.6 0.3 select_maximum_fusion
  10.9 0.1 fusion.20
  11.0 0.1 maximum_bitcast_fusion
  11.1 0.4 copy.68
  11.5 1.3 %reshape.102 = f32[32,30,128]{2,1,0:T(8,128)} reshape(f32[32,80,48]{2,1,0:T(8,128)S(1)} %copy.68) | data formatting | bytes 983040 | tf_op jit(solution)/shard_map/reshape | solution.py:175
  12.8 8.1 %all-to-all-start = ((f32[32,30,128]{2,1,0:T(8,128)}), f32[32,30,128]{2,1,0:T(8,128)S(1)}, u32[]{:S(2)}, u32[]{:S(2)}) async-start(f32[32,30,128]{2,1,0:T(8,128)} %reshape.102), calls=%async_computation | async-start | bytes 1048576 | tf_op jit(solution)/shard_map/all_to_all | solution.py:176
  20.9 0.2 copy.90
  21.1 0.2 copy.89
  21.3 0.1 select_maximum_fusion.2
  21.4 0.1 broadcast_add_fusion.2
  21.6 0.8 %copy.79.north_ref = f32[80,768]{1,0:T(8,128)} copy(f32[80,768]{0,1:T(8,128)S(1)} %bitcast.50) | data formatting | bytes 491520 | tf_op jit(solution)/shard_map/tile | solution.py:185
  22.4 0.9 %copy.80.south_ref = f32[80,768]{1,0:T(8,128)} copy(f32[80,768]{0,1:T(8,128)S(1)} %bitcast.51) | data formatting | bytes 491520 | tf_op jit(solution)/shard_map/add | solution.py:152
  23.3 0.0 copy-start.3
  23.3 0.0 copy-start.4
  23.4 0.0 copy-start.5
  23.4 0.0 copy-start.6
  23.4 0.8 %copy.81.east_ref = f32[80,768]{1,0:T(8,128)} copy(f32[80,768]{0,1:T(8,128)S(1)} %bitcast.52) | data formatting | bytes 491520 | tf_op jit(solution)/shard_map/tile | solution.py:185
  24.3 0.9 %copy.82.west_ref = f32[80,768]{1,0:T(8,128)} copy(f32[80,768]{0,1:T(8,128)S(1)} %bitcast.53) | data formatting | bytes 491520 | tf_op jit(solution)/shard_map/add | solution.py:152
  25.1 0.0 copy-start.1
  25.2 0.1 copy.73
  25.3 0.0 copy-done.3
  25.3 0.0 copy-done.4
  25.3 0.0 copy-done.5
  25.3 0.0 copy-done.6
  25.3 1.1 %divide_select_fusion = (f32[80,768]{1,0:T(8,128)}, f32[80,768]{1,0:T(8,128)}, f32[80,768]{1,0:T(8,128)}, f32[80,768]{1,0:T(8,128)}, f32[80,768]{1,0:T(8,128)}) fusion(pred[80,768]{1,0:T(8,128)(4,1)S(1)} %copy.75, f32[768]{0:T(1024)S(1)} %copy-done.3, f32[768]{0:T(1024)S(1)} %copy-done.4, f32[80,768]{1,0:T(8,128)S(1)} %copy.73, f32[768]{0:T(1024)S(1)} %copy-done.5, ...), kind=kLoop, calls=%fused_computation.16 | loop fusion | flops 737280 | bytes 1548288 | tf_op jit(solution)/shard_map/jit(_where)/select_n | solution.py:151
  26.5 6.0 %all-to-all-done = f32[32,30,128]{2,1,0:T(8,128)S(1)} async-done(((f32[32,30,128]{2,1,0:T(8,128)}), f32[32,30,128]{2,1,0:T(8,128)S(1)}, u32[]{:S(2)}, u32[]{:S(2)}) %all-to-all-start) | async-done | bytes 491552 | tf_op jit(solution)/shard_map/all_to_all | solution.py:176
  32.5 0.0 copy-done.1
  32.5 0.8 %fusion.1 = f32[32,3840]{1,0:T(8,128)S(1)} fusion(f32[32,32]{1,0:T(8,128)S(1)} %copy-done.1, f32[4,8,30,128]{3,2,1,0:T(8,128)S(1)} %bitcast.49), kind=kOutput, calls=%fused_computation.13 | convolution fusion | flops 47185920 | bytes 987136 | tf_op jit(solution)/shard_map/dot_general | solution.py:177
  33.3 0.8 %reshape.104 = f32[2,16,80,48]{3,2,1,0:T(8,128)S(1)} reshape(f32[32,3840]{1,0:T(8,128)S(1)} %fusion.1) | data formatting | bytes 983040 | tf_op jit(solution)/shard_map/reshape | solution.py:178
  34.2 0.4 copy.69
  34.5 1.1 %copy.78.spec_ref = f32[2,80,768]{2,1,0:T(8,128)} copy(f32[2,80,768]{1,2,0:T(8,128)S(1)} %bitcast.40) | data formatting | bytes 983040 | tf_op jit(solution)/shard_map/reshape | solution.py:179
  35.6 6.0 %shard_map.100 = f32[2,80,768]{2,1,0:T(8,128)} custom-call(f32[2,80,768]{2,1,0:T(8,128)} %copy.78.spec_ref, f32[80,768]{1,0:T(8,128)} %copy.79.north_ref, f32[80,768]{1,0:T(8,128)} %copy.80.south_ref, f32[80,768]{1,0:T(8,128)} %copy.81.east_ref, f32[80,768]{1,0:T(8,128)} %copy.82.west_ref, f32[80,768]{1,0:T(8,128)} %get-tuple-element.22.diag_a_ref, ...), custom_call_target="tpu_custom_call" | custom-call | tf_op jit(solution)/shard_map/pallas_call | solution.py:154
  41.6 1.3 %copy.83 = f32[2,80,768]{1,2,0:T(8,128)S(1)} copy(f32[2,80,768]{2,1,0:T(8,128)} %shard_map.100) | data formatting | bytes 983040 | tf_op jit(solution)/shard_map/pallas_call | solution.py:154
  42.9 0.2 slice_bitcast_fusion
  43.1 0.0 copy-start.2
  43.1 0.4 copy.84
  43.5 0.5 reshape.107
  44.0 0.0 copy-done.2
  44.0 0.4 convolution_bitcast_fusion
  44.4 12.4 %all_to_all.10 = f32[32,16,128]{2,1,0:T(8,128)S(1)} all-to-all(f32[32,16,128]{2,1,0:T(8,128)S(1)} %bitcast.56), channel_id=1, replica_groups=mesh['tm'=32,'row'=8] {'tm'}, dimensions={0} | all-to-all | bytes 524288 | tf_op jit(solution)/shard_map/all_to_all | solution.py:193
  56.8 0.3 reshape.109
  57.1 0.3 copy.85
  57.4 0.9 %copy.86 = f32[1,64,1024]{2,1,0:T(8,128)} copy(f32[1,64,1024]{1,2,0:T(8,128)S(1)} %bitcast.42) | data formatting | bytes 524288 | tf_op jit(solution)/shard_map/reshape | solution.py:195
  (13 shorter events, 0.3 us)
Async XLA Ops:
  0.0 9.7 %copy-start = (f32[64,1024]{1,0:T(8,128)S(1)}, f32[64,1024]{1,0:T(8,128)}, u32[]{:S(2)}) copy-start(f32[64,1024]{1,0:T(8,128)} %param.11) | copy-start | bytes 786436
  1.6 8.5 %collective-permute-start.1 = (f32[2,8,1024]{2,1,0:T(8,128)S(1)}, f32[2,8,1024]{2,1,0:T(8,128)S(1)}, u32[]{:S(2)}, u32[]{:S(2)}) collective-permute-start(f32[2,8,1024]{2,1,0:T(8,128)S(1)} %get-tuple-element.8), channel_id=1, source_target_pairs={{1,0},{2,1},{3,2},{4,3},{5,4},{6,5},{7,6},{9,8},{10,9},{11,10},{12... | collective-permute-start | bytes 196616 | tf_op jit(solution)/shard_map/ppermute | solution.py:39
  3.6 6.8 %collective-permute-start = (f32[2,8,1024]{2,1,0:T(8,128)S(1)}, f32[2,8,1024]{2,1,0:T(8,128)S(1)}, u32[]{:S(2)}, u32[]{:S(2)}) collective-permute-start(f32[2,8,1024]{2,1,0:T(8,128)S(1)} %get-tuple-element.7), channel_id=1, source_target_pairs={{0,1},{1,2},{2,3},{3,4},{4,5},{5,6},{6,7},{8,9},{9,10},{10,11},{11... | collective-permute-start | bytes 196616 | tf_op jit(solution)/shard_map/ppermute | solution.py:38
  12.8 19.8 %all-to-all-start = ((f32[32,30,128]{2,1,0:T(8,128)}), f32[32,30,128]{2,1,0:T(8,128)S(1)}, u32[]{:S(2)}, u32[]{:S(2)}) async-start(f32[32,30,128]{2,1,0:T(8,128)} %reshape.102), calls=%async_computation | async-start | bytes 1048576 | tf_op jit(solution)/shard_map/all_to_all | solution.py:176
  23.3 2.0 %copy-start.3 = (f32[768]{0:T(1024)S(1)}, f32[768]{0:T(1024)}, u32[]{:S(2)}) copy-start(f32[768]{0:T(1024)} %constant.66) | copy-start | bytes 9220
  23.3 2.0 %copy-start.4 = (f32[768]{0:T(1024)S(1)}, f32[768]{0:T(1024)}, u32[]{:S(2)}) copy-start(f32[768]{0:T(1024)} %constant.65) | copy-start | bytes 9220
  23.4 2.0 %copy-start.5 = (f32[768]{0:T(1024)S(1)}, f32[768]{0:T(1024)}, u32[]{:S(2)}) copy-start(f32[768]{0:T(1024)} %constant.63) | copy-start | bytes 9220
  23.4 2.0 %copy-start.6 = (f32[768]{0:T(1024)S(1)}, f32[768]{0:T(1024)}, u32[]{:S(2)}) copy-start(f32[768]{0:T(1024)} %constant.64) | copy-start | bytes 9220
  25.1 7.4 %copy-start.1 = (f32[32,32]{1,0:T(8,128)S(1)}, f32[32,32]{1,0:T(8,128)}, u32[]{:S(2)}) copy-start(f32[32,32]{1,0:T(8,128)} %constant.51.clone) | copy-start | bytes 12292
  43.1 0.9 %copy-start.2 = (f32[32,32]{1,0:T(8,128)S(1)}, f32[32,32]{1,0:T(8,128)}, u32[]{:S(2)}) copy-start(f32[32,32]{1,0:T(8,128)} %constant.57.clone) | copy-start | bytes 12292

commit v15 on v14

--- a/solution.py
+++ b/solution.py
@@ -166,7 +166,7 @@
     span = cols // tiles
     width = span + 2 * margin
     tile = lax.axis_index("tm")
-    highest = lax.Precision.HIGHEST
+    highest = lax.Precision.HIGH
     forward, inverse = transform_matrices(total)
 
     wide_side, kappa_rows, inside_rows = with_halo(right_side, kappa, margin)

time: 59 us -> 58.7 us (level)
  no operation moved by 1% of the time
where the time goes in v15:
time: 58.7 us; the launch traced here: 58 us
  local copies, waits for them, and re-layouts  15.6 us (27%)
  starting transfers between devices  14.8 us (25%)
  blocking collectives  12.4 us (21%)
  waiting for transfers between devices  6.03 us (10%)
  Pallas kernels  6.01 us (10%)
  other arithmetic  1.92 us (3%)
  matrix products  0.85 us (1%)
    all_to_all x1, blocking collectives, body(): returned = lax.all_to_all(signal, 'tm', 0, 0, tiled=True)  12.4 us
    all_to_all x1, starting transfers between devices, body(): lax.all_to_all(sent, 'tm', 0, 0, tiled=True)  8.13 us
    all_to_all x1, waiting for transfers between devices, body(): lax.all_to_all(sent, 'tm', 0, 0, tiled=True)  6.03 us
    pallas_call x1, Pallas kernels, solve_slots(): pl.pallas_call(solve_kernel, out_shape=jax.ShapeDtypeStruct(spectrum.shap...  6.01 us
    ppermute x1, starting transfers between devices, with_halo(): low = lax.ppermute(bottom, 'row', forward)  4.76 us
    unnamed x21, local copies, waits for them, and re-layouts  2.21 us
    another operation x8, local copies, waits for them, and re-layouts, body(): jnp.tile(f, (1, half))  1.98 us
    ppermute x1, starting transfers between devices, with_halo(): high = lax.ppermute(top, 'row', backward)  1.92 us
  transfers between devices with their start and end apart: 3, of which 1 were waited for; matrix products, arithmetic and copies ran while one was open for 13% of the time, Pallas kernels for 0%

profile of v15, /device:TPU:97, one launch (start us, length us, event | category | flops | bytes accessed | tf_op | source)
XLA Modules:
  0.0 58.0 jit_solution(15052928806906107233)
XLA Ops:
  0.0 0.0 copy-start
  0.0 0.8 %slice_bitcast_fusion.1 = (f32[1,8,1024]{2,1,0:T(8,128)S(1)}, f32[1,8,1024]{2,1,0:T(8,128)S(1)}) fusion(f32[64,1024]{1,0:T(8,128)} %param.11), kind=kLoop, calls=%fused_computation.26 | loop fusion | bytes 131072 | tf_op jit(solution)/shard_map/stack | solution.py:36
  0.8 0.8 %fusion.21 = (f32[1,8,1024]{2,1,0:T(8,128)S(1)}, f32[1,8,1024]{2,1,0:T(8,128)S(1)}) fusion(f32[1,64,1024]{2,1,0:T(8,128)} %param.10), kind=kLoop, calls=%fused_computation.57 | loop fusion | bytes 131072 | tf_op jit(solution)/shard_map/slice | solution.py:36
  1.6 1.9 %collective-permute-start.1 = (f32[2,8,1024]{2,1,0:T(8,128)S(1)}, f32[2,8,1024]{2,1,0:T(8,128)S(1)}, u32[]{:S(2)}, u32[]{:S(2)}) collective-permute-start(f32[2,8,1024]{2,1,0:T(8,128)S(1)} %get-tuple-element.8), channel_id=1, source_target_pairs={{1,0},{2,1},{3,2},{4,3},{5,4},{6,5},{7,6},{9,8},{10,9},{11,10},{12... | collective-permute-start | bytes 196616 | tf_op jit(solution)/shard_map/ppermute | solution.py:39
  3.6 4.8 %collective-permute-start = (f32[2,8,1024]{2,1,0:T(8,128)S(1)}, f32[2,8,1024]{2,1,0:T(8,128)S(1)}, u32[]{:S(2)}, u32[]{:S(2)}) collective-permute-start(f32[2,8,1024]{2,1,0:T(8,128)S(1)} %get-tuple-element.7), channel_id=1, source_target_pairs={{0,1},{1,2},{2,3},{3,4},{4,5},{5,6},{6,7},{8,9},{9,10},{10,11},{11... | collective-permute-start | bytes 196616 | tf_op jit(solution)/shard_map/ppermute | solution.py:38
  8.3 0.1 iota_compare_fusion.2
  8.4 0.1 broadcast_and_fusion
  8.5 1.1 %copy.66 = f32[1,64,1024]{1,2,0:T(8,128)S(1)} copy(f32[1,64,1024]{2,1,0:T(8,128)} %param.10) | data formatting | bytes 524288 | tf_op args[0]
  9.7 0.0 copy-done
  9.7 0.2 copy.72
  9.9 0.2 copy.75
  10.1 0.0 collective-permute-done.1
  10.1 0.2 copy.88
  10.3 0.0 collective-permute-done
  10.4 0.2 copy.87
  10.6 0.3 select_maximum_fusion
  10.9 0.1 fusion.20
  11.0 0.1 maximum_bitcast_fusion
  11.1 0.4 copy.68
  11.5 1.3 %reshape.102 = f32[32,30,128]{2,1,0:T(8,128)} reshape(f32[32,80,48]{2,1,0:T(8,128)S(1)} %copy.68) | data formatting | bytes 983040 | tf_op jit(solution)/shard_map/reshape | solution.py:175
  12.8 8.1 %all-to-all-start = ((f32[32,30,128]{2,1,0:T(8,128)}), f32[32,30,128]{2,1,0:T(8,128)S(1)}, u32[]{:S(2)}, u32[]{:S(2)}) async-start(f32[32,30,128]{2,1,0:T(8,128)} %reshape.102), calls=%async_computation | async-start | bytes 1048576 | tf_op jit(solution)/shard_map/all_to_all | solution.py:176
  20.9 0.2 copy.90
  21.1 0.2 copy.89
  21.3 0.1 select_maximum_fusion.2
  21.4 0.1 broadcast_add_fusion.2
  21.6 0.8 %copy.79.north_ref = f32[80,768]{1,0:T(8,128)} copy(f32[80,768]{0,1:T(8,128)S(1)} %bitcast.50) | data formatting | bytes 491520 | tf_op jit(solution)/shard_map/tile | solution.py:185
  22.4 0.9 %copy.80.south_ref = f32[80,768]{1,0:T(8,128)} copy(f32[80,768]{0,1:T(8,128)S(1)} %bitcast.51) | data formatting | bytes 491520 | tf_op jit(solution)/shard_map/add | solution.py:152
  23.3 0.0 copy-start.3
  23.3 0.0 copy-start.4
  23.4 0.0 copy-start.5
  23.4 0.0 copy-start.6
  23.4 0.8 %copy.81.east_ref = f32[80,768]{1,0:T(8,128)} copy(f32[80,768]{0,1:T(8,128)S(1)} %bitcast.52) | data formatting | bytes 491520 | tf_op jit(solution)/shard_map/tile | solution.py:185
  24.3 0.9 %copy.82.west_ref = f32[80,768]{1,0:T(8,128)} copy(f32[80,768]{0,1:T(8,128)S(1)} %bitcast.53) | data formatting | bytes 491520 | tf_op jit(solution)/shard_map/add | solution.py:152
  25.1 0.0 copy-start.1
  25.2 0.1 copy.73
  25.3 0.0 copy-done.3
  25.3 0.0 copy-done.4
  25.3 0.0 copy-done.5
  25.3 0.0 copy-done.6
  25.3 1.1 %divide_select_fusion = (f32[80,768]{1,0:T(8,128)}, f32[80,768]{1,0:T(8,128)}, f32[80,768]{1,0:T(8,128)}, f32[80,768]{1,0:T(8,128)}, f32[80,768]{1,0:T(8,128)}) fusion(pred[80,768]{1,0:T(8,128)(4,1)S(1)} %copy.75, f32[768]{0:T(1024)S(1)} %copy-done.3, f32[768]{0:T(1024)S(1)} %copy-done.4, f32[80,768]{1,0:T(8,128)S(1)} %copy.73, f32[768]{0:T(1024)S(1)} %copy-done.5, ...), kind=kLoop, calls=%fused_computation.16 | loop fusion | flops 737280 | bytes 1548288 | tf_op jit(solution)/shard_map/jit(_where)/select_n | solution.py:151
  26.5 6.0 %all-to-all-done = f32[32,30,128]{2,1,0:T(8,128)S(1)} async-done(((f32[32,30,128]{2,1,0:T(8,128)}), f32[32,30,128]{2,1,0:T(8,128)S(1)}, u32[]{:S(2)}, u32[]{:S(2)}) %all-to-all-start) | async-done | bytes 491552 | tf_op jit(solution)/shard_map/all_to_all | solution.py:176
  32.5 0.0 copy-done.1
  32.5 0.6 %fusion.1 = f32[32,3840]{1,0:T(8,128)S(1)} fusion(f32[32,32]{1,0:T(8,128)S(1)} %copy-done.1, f32[4,8,30,128]{3,2,1,0:T(8,128)S(1)} %bitcast.49), kind=kOutput, calls=%fused_computation.13 | convolution fusion | flops 23592960 | bytes 987136 | tf_op jit(solution)/shard_map/dot_general | solution.py:177
  33.1 0.8 %reshape.104 = f32[2,16,80,48]{3,2,1,0:T(8,128)S(1)} reshape(f32[32,3840]{1,0:T(8,128)S(1)} %fusion.1) | data formatting | bytes 983040 | tf_op jit(solution)/shard_map/reshape | solution.py:178
  34.0 0.4 copy.69
  34.3 1.1 %copy.78.spec_ref = f32[2,80,768]{2,1,0:T(8,128)} copy(f32[2,80,768]{1,2,0:T(8,128)S(1)} %bitcast.40) | data formatting | bytes 983040 | tf_op jit(solution)/shard_map/reshape | solution.py:179
  35.4 6.0 %shard_map.100 = f32[2,80,768]{2,1,0:T(8,128)} custom-call(f32[2,80,768]{2,1,0:T(8,128)} %copy.78.spec_ref, f32[80,768]{1,0:T(8,128)} %copy.79.north_ref, f32[80,768]{1,0:T(8,128)} %copy.80.south_ref, f32[80,768]{1,0:T(8,128)} %copy.81.east_ref, f32[80,768]{1,0:T(8,128)} %copy.82.west_ref, f32[80,768]{1,0:T(8,128)} %get-tuple-element.22.diag_a_ref, ...), custom_call_target="tpu_custom_call" | custom-call | tf_op jit(solution)/shard_map/pallas_call | solution.py:154
  41.4 1.3 %copy.83 = f32[2,80,768]{1,2,0:T(8,128)S(1)} copy(f32[2,80,768]{2,1,0:T(8,128)} %shard_map.100) | data formatting | bytes 983040 | tf_op jit(solution)/shard_map/pallas_call | solution.py:154
  42.7 0.2 slice_bitcast_fusion
  42.9 0.0 copy-start.2
  42.9 0.4 copy.84
  43.3 0.5 reshape.107
  43.8 0.0 copy-done.2
  43.8 0.2 convolution_bitcast_fusion
  44.1 12.4 %all_to_all.10 = f32[32,16,128]{2,1,0:T(8,128)S(1)} all-to-all(f32[32,16,128]{2,1,0:T(8,128)S(1)} %bitcast.56), channel_id=1, replica_groups=mesh['tm'=32,'row'=8] {'tm'}, dimensions={0} | all-to-all | bytes 524288 | tf_op jit(solution)/shard_map/all_to_all | solution.py:193
  56.5 0.3 reshape.109
  56.8 0.3 copy.85
  57.1 0.9 %copy.86 = f32[1,64,1024]{2,1,0:T(8,128)} copy(f32[1,64,1024]{1,2,0:T(8,128)S(1)} %bitcast.42) | data formatting | bytes 524288 | tf_op jit(solution)/shard_map/reshape | solution.py:195
  (13 shorter events, 0.3 us)
Async XLA Ops:
  0.0 9.7 %copy-start = (f32[64,1024]{1,0:T(8,128)S(1)}, f32[64,1024]{1,0:T(8,128)}, u32[]{:S(2)}) copy-start(f32[64,1024]{1,0:T(8,128)} %param.11) | copy-start | bytes 786436
  1.6 8.5 %collective-permute-start.1 = (f32[2,8,1024]{2,1,0:T(8,128)S(1)}, f32[2,8,1024]{2,1,0:T(8,128)S(1)}, u32[]{:S(2)}, u32[]{:S(2)}) collective-permute-start(f32[2,8,1024]{2,1,0:T(8,128)S(1)} %get-tuple-element.8), channel_id=1, source_target_pairs={{1,0},{2,1},{3,2},{4,3},{5,4},{6,5},{7,6},{9,8},{10,9},{11,10},{12... | collective-permute-start | bytes 196616 | tf_op jit(solution)/shard_map/ppermute | solution.py:39
  3.6 6.8 %collective-permute-start = (f32[2,8,1024]{2,1,0:T(8,128)S(1)}, f32[2,8,1024]{2,1,0:T(8,128)S(1)}, u32[]{:S(2)}, u32[]{:S(2)}) collective-permute-start(f32[2,8,1024]{2,1,0:T(8,128)S(1)} %get-tuple-element.7), channel_id=1, source_target_pairs={{0,1},{1,2},{2,3},{3,4},{4,5},{5,6},{6,7},{8,9},{9,10},{10,11},{11... | collective-permute-start | bytes 196616 | tf_op jit(solution)/shard_map/ppermute | solution.py:38
  12.8 19.8 %all-to-all-start = ((f32[32,30,128]{2,1,0:T(8,128)}), f32[32,30,128]{2,1,0:T(8,128)S(1)}, u32[]{:S(2)}, u32[]{:S(2)}) async-start(f32[32,30,128]{2,1,0:T(8,128)} %reshape.102), calls=%async_computation | async-start | bytes 1048576 | tf_op jit(solution)/shard_map/all_to_all | solution.py:176
  23.3 2.0 %copy-start.3 = (f32[768]{0:T(1024)S(1)}, f32[768]{0:T(1024)}, u32[]{:S(2)}) copy-start(f32[768]{0:T(1024)} %constant.66) | copy-start | bytes 9220
  23.3 2.0 %copy-start.4 = (f32[768]{0:T(1024)S(1)}, f32[768]{0:T(1024)}, u32[]{:S(2)}) copy-start(f32[768]{0:T(1024)} %constant.65) | copy-start | bytes 9220
  23.4 2.0 %copy-start.5 = (f32[768]{0:T(1024)S(1)}, f32[768]{0:T(1024)}, u32[]{:S(2)}) copy-start(f32[768]{0:T(1024)} %constant.63) | copy-start | bytes 9220
  23.4 2.0 %copy-start.6 = (f32[768]{0:T(1024)S(1)}, f32[768]{0:T(1024)}, u32[]{:S(2)}) copy-start(f32[768]{0:T(1024)} %constant.64) | copy-start | bytes 9220
  25.1 7.4 %copy-start.1 = (f32[32,32]{1,0:T(8,128)S(1)}, f32[32,32]{1,0:T(8,128)}, u32[]{:S(2)}) copy-start(f32[32,32]{1,0:T(8,128)} %constant.51.clone) | copy-start | bytes 12292
  42.9 0.9 %copy-start.2 = (f32[32,32]{1,0:T(8,128)S(1)}, f32[32,32]{1,0:T(8,128)}, u32[]{:S(2)}) copy-start(f32[32,32]{1,0:T(8,128)} %constant.57.clone) | copy-start | bytes 12292

commit v16 on v14

--- a/solution.py
+++ b/solution.py
@@ -151,8 +151,17 @@
     inv_imag = jnp.where(inside, -imag / mag_a, 0.0)
     operands = (spectrum, north, south + courant_rows, east, west + courant_cols,
                 diag_a, diag_b, inv_a, inv_b, inv_imag, jnp.asarray(imag))
+    parts, extended, lanes = spectrum.shape
+    blocks = 2
+    block = lanes // blocks
+    field = pl.BlockSpec((extended, block), lambda i: (0, i))
+    pair = pl.BlockSpec((parts, extended, block), lambda i: (0, 0, i))
+    row = pl.BlockSpec((1, block), lambda i: (0, i))
     return pl.pallas_call(
         solve_kernel,
+        grid=(blocks,),
+        in_specs=[pair] + [field] * 9 + [row],
+        out_specs=pair,
         out_shape=jax.ShapeDtypeStruct(spectrum.shape, spectrum.dtype),
     )(*operands)
 

time: 59 us -> 59 us (level)
  no operation moved by 1% of the time
where the time goes in v16:
time: 59 us; the launch traced here: 58.2 us
  local copies, waits for them, and re-layouts  15.6 us (26%)
  starting transfers between devices  14.8 us (25%)
  blocking collectives  12.4 us (21%)
  waiting for transfers between devices  6.03 us (10%)
  Pallas kernels  5.94 us (10%)
  other arithmetic  1.92 us (3%)
  matrix products  1.16 us (2%)
    all_to_all x1, blocking collectives, body(): returned = lax.all_to_all(signal, 'tm', 0, 0, tiled=True)  12.4 us
    all_to_all x1, starting transfers between devices, body(): lax.all_to_all(sent, 'tm', 0, 0, tiled=True)  8.13 us
    all_to_all x1, waiting for transfers between devices, body(): lax.all_to_all(sent, 'tm', 0, 0, tiled=True)  6.03 us
    pallas_call x1, Pallas kernels, solve_slots(): pl.pallas_call(solve_kernel, grid=(blocks,), in_specs=[pair] + [field] *...  5.94 us
    ppermute x1, starting transfers between devices, with_halo(): low = lax.ppermute(bottom, 'row', forward)  4.76 us
    unnamed x21, local copies, waits for them, and re-layouts  2.21 us
    another operation x8, local copies, waits for them, and re-layouts, body(): jnp.tile(f, (1, half))  1.98 us
    ppermute x1, starting transfers between devices, with_halo(): high = lax.ppermute(top, 'row', backward)  1.92 us
  transfers between devices with their start and end apart: 3, of which 1 were waited for; matrix products, arithmetic and copies ran while one was open for 13% of the time, Pallas kernels for 0%

profile of v16, /device:TPU:97, one launch (start us, length us, event | category | flops | bytes accessed | tf_op | source)
XLA Modules:
  0.0 58.2 jit_solution(9983118722164380061)
XLA Ops:
  0.0 0.0 copy-start
  0.0 0.8 %slice_bitcast_fusion.1 = (f32[1,8,1024]{2,1,0:T(8,128)S(1)}, f32[1,8,1024]{2,1,0:T(8,128)S(1)}) fusion(f32[64,1024]{1,0:T(8,128)} %param.11), kind=kLoop, calls=%fused_computation.26 | loop fusion | bytes 131072 | tf_op jit(solution)/shard_map/stack | solution.py:36
  0.8 0.8 %fusion.21 = (f32[1,8,1024]{2,1,0:T(8,128)S(1)}, f32[1,8,1024]{2,1,0:T(8,128)S(1)}) fusion(f32[1,64,1024]{2,1,0:T(8,128)} %param.10), kind=kLoop, calls=%fused_computation.57 | loop fusion | bytes 131072 | tf_op jit(solution)/shard_map/slice | solution.py:36
  1.6 1.9 %collective-permute-start.1 = (f32[2,8,1024]{2,1,0:T(8,128)S(1)}, f32[2,8,1024]{2,1,0:T(8,128)S(1)}, u32[]{:S(2)}, u32[]{:S(2)}) collective-permute-start(f32[2,8,1024]{2,1,0:T(8,128)S(1)} %get-tuple-element.8), channel_id=1, source_target_pairs={{1,0},{2,1},{3,2},{4,3},{5,4},{6,5},{7,6},{9,8},{10,9},{11,10},{12... | collective-permute-start | bytes 196616 | tf_op jit(solution)/shard_map/ppermute | solution.py:39
  3.6 4.8 %collective-permute-start = (f32[2,8,1024]{2,1,0:T(8,128)S(1)}, f32[2,8,1024]{2,1,0:T(8,128)S(1)}, u32[]{:S(2)}, u32[]{:S(2)}) collective-permute-start(f32[2,8,1024]{2,1,0:T(8,128)S(1)} %get-tuple-element.7), channel_id=1, source_target_pairs={{0,1},{1,2},{2,3},{3,4},{4,5},{5,6},{6,7},{8,9},{9,10},{10,11},{11... | collective-permute-start | bytes 196616 | tf_op jit(solution)/shard_map/ppermute | solution.py:38
  8.3 0.1 iota_compare_fusion.2
  8.4 0.1 broadcast_and_fusion
  8.5 1.1 %copy.66 = f32[1,64,1024]{1,2,0:T(8,128)S(1)} copy(f32[1,64,1024]{2,1,0:T(8,128)} %param.10) | data formatting | bytes 524288 | tf_op args[0]
  9.7 0.0 copy-done
  9.7 0.2 copy.72
  9.9 0.2 copy.75
  10.1 0.0 collective-permute-done.1
  10.1 0.2 copy.88
  10.3 0.0 collective-permute-done
  10.4 0.2 copy.87
  10.6 0.3 select_maximum_fusion
  10.9 0.1 fusion.20
  11.0 0.1 maximum_bitcast_fusion
  11.1 0.4 copy.68
  11.5 1.3 %reshape.102 = f32[32,30,128]{2,1,0:T(8,128)} reshape(f32[32,80,48]{2,1,0:T(8,128)S(1)} %copy.68) | data formatting | bytes 983040 | tf_op jit(solution)/shard_map/reshape | solution.py:184
  12.8 8.1 %all-to-all-start = ((f32[32,30,128]{2,1,0:T(8,128)}), f32[32,30,128]{2,1,0:T(8,128)S(1)}, u32[]{:S(2)}, u32[]{:S(2)}) async-start(f32[32,30,128]{2,1,0:T(8,128)} %reshape.102), calls=%async_computation | async-start | bytes 1048576 | tf_op jit(solution)/shard_map/all_to_all | solution.py:185
  20.9 0.2 copy.90
  21.1 0.2 copy.89
  21.3 0.1 select_maximum_fusion.2
  21.4 0.1 broadcast_add_fusion.2
  21.6 0.8 %copy.79.north_ref = f32[80,768]{1,0:T(8,128)} copy(f32[80,768]{0,1:T(8,128)S(1)} %bitcast.50) | data formatting | bytes 491520 | tf_op jit(solution)/shard_map/tile | solution.py:194
  22.4 0.9 %copy.80.south_ref = f32[80,768]{1,0:T(8,128)} copy(f32[80,768]{0,1:T(8,128)S(1)} %bitcast.51) | data formatting | bytes 491520 | tf_op jit(solution)/shard_map/add | solution.py:152
  23.3 0.0 copy-start.3
  23.3 0.0 copy-start.4
  23.4 0.0 copy-start.5
  23.4 0.0 copy-start.6
  23.4 0.8 %copy.81.east_ref = f32[80,768]{1,0:T(8,128)} copy(f32[80,768]{0,1:T(8,128)S(1)} %bitcast.52) | data formatting | bytes 491520 | tf_op jit(solution)/shard_map/tile | solution.py:194
  24.3 0.9 %copy.82.west_ref = f32[80,768]{1,0:T(8,128)} copy(f32[80,768]{0,1:T(8,128)S(1)} %bitcast.53) | data formatting | bytes 491520 | tf_op jit(solution)/shard_map/add | solution.py:152
  25.1 0.0 copy-start.1
  25.2 0.1 copy.73
  25.3 0.0 copy-done.3
  25.3 0.0 copy-done.4
  25.3 0.0 copy-done.5
  25.3 0.0 copy-done.6
  25.3 1.1 %divide_select_fusion = (f32[80,768]{1,0:T(8,128)}, f32[80,768]{1,0:T(8,128)}, f32[80,768]{1,0:T(8,128)}, f32[80,768]{1,0:T(8,128)}, f32[80,768]{1,0:T(8,128)}) fusion(pred[80,768]{1,0:T(8,128)(4,1)S(1)} %copy.75, f32[768]{0:T(1024)S(1)} %copy-done.3, f32[768]{0:T(1024)S(1)} %copy-done.4, f32[80,768]{1,0:T(8,128)S(1)} %copy.73, f32[768]{0:T(1024)S(1)} %copy-done.5, ...), kind=kLoop, calls=%fused_computation.16 | loop fusion | flops 737280 | bytes 1548288 | tf_op jit(solution)/shard_map/jit(_where)/select_n | solution.py:151
  26.5 6.0 %all-to-all-done = f32[32,30,128]{2,1,0:T(8,128)S(1)} async-done(((f32[32,30,128]{2,1,0:T(8,128)}), f32[32,30,128]{2,1,0:T(8,128)S(1)}, u32[]{:S(2)}, u32[]{:S(2)}) %all-to-all-start) | async-done | bytes 491552 | tf_op jit(solution)/shard_map/all_to_all | solution.py:185
  32.5 0.0 copy-done.1
  32.5 0.8 %fusion.1 = f32[32,3840]{1,0:T(8,128)S(1)} fusion(f32[32,32]{1,0:T(8,128)S(1)} %copy-done.1, f32[4,8,30,128]{3,2,1,0:T(8,128)S(1)} %bitcast.49), kind=kOutput, calls=%fused_computation.13 | convolution fusion | flops 47185920 | bytes 987136 | tf_op jit(solution)/shard_map/dot_general | solution.py:186
  33.3 0.8 %reshape.104 = f32[2,16,80,48]{3,2,1,0:T(8,128)S(1)} reshape(f32[32,3840]{1,0:T(8,128)S(1)} %fusion.1) | data formatting | bytes 983040 | tf_op jit(solution)/shard_map/reshape | solution.py:187
  34.2 0.4 copy.69
  34.5 1.1 %copy.78.spec_ref = f32[2,80,768]{2,1,0:T(8,128)} copy(f32[2,80,768]{1,2,0:T(8,128)S(1)} %bitcast.40) | data formatting | bytes 983040 | tf_op jit(solution)/shard_map/reshape | solution.py:188
  35.6 5.9 %shard_map.100 = f32[2,80,768]{2,1,0:T(8,128)} custom-call(f32[2,80,768]{2,1,0:T(8,128)} %copy.78.spec_ref, f32[80,768]{1,0:T(8,128)} %copy.79.north_ref, f32[80,768]{1,0:T(8,128)} %copy.80.south_ref, f32[80,768]{1,0:T(8,128)} %copy.81.east_ref, f32[80,768]{1,0:T(8,128)} %copy.82.west_ref, f32[80,768]{1,0:T(8,128)} %get-tuple-element.22.diag_a_ref, ...), custom_call_target="tpu_custom_call" | custom-call | tf_op jit(solution)/shard_map/pallas_call | solution.py:160
  41.5 1.3 %copy.83 = f32[2,80,768]{1,2,0:T(8,128)S(1)} copy(f32[2,80,768]{2,1,0:T(8,128)} %shard_map.100) | data formatting | bytes 983040 | tf_op jit(solution)/shard_map/pallas_call | solution.py:160
  42.8 0.2 slice_bitcast_fusion
  43.0 0.0 copy-start.2
  43.0 0.4 copy.84
  43.4 0.5 reshape.107
  43.9 0.0 copy-done.2
  43.9 0.4 convolution_bitcast_fusion
  44.3 12.4 %all_to_all.10 = f32[32,16,128]{2,1,0:T(8,128)S(1)} all-to-all(f32[32,16,128]{2,1,0:T(8,128)S(1)} %bitcast.56), channel_id=1, replica_groups=mesh['tm'=32,'row'=8] {'tm'}, dimensions={0} | all-to-all | bytes 524288 | tf_op jit(solution)/shard_map/all_to_all | solution.py:202
  56.7 0.3 reshape.109
  57.0 0.3 copy.85
  57.3 0.9 %copy.86 = f32[1,64,1024]{2,1,0:T(8,128)} copy(f32[1,64,1024]{1,2,0:T(8,128)S(1)} %bitcast.42) | data formatting | bytes 524288 | tf_op jit(solution)/shard_map/reshape | solution.py:204
  (13 shorter events, 0.3 us)
Async XLA Ops:
  0.0 9.7 %copy-start = (f32[64,1024]{1,0:T(8,128)S(1)}, f32[64,1024]{1,0:T(8,128)}, u32[]{:S(2)}) copy-start(f32[64,1024]{1,0:T(8,128)} %param.11) | copy-start | bytes 786436
  1.6 8.5 %collective-permute-start.1 = (f32[2,8,1024]{2,1,0:T(8,128)S(1)}, f32[2,8,1024]{2,1,0:T(8,128)S(1)}, u32[]{:S(2)}, u32[]{:S(2)}) collective-permute-start(f32[2,8,1024]{2,1,0:T(8,128)S(1)} %get-tuple-element.8), channel_id=1, source_target_pairs={{1,0},{2,1},{3,2},{4,3},{5,4},{6,5},{7,6},{9,8},{10,9},{11,10},{12... | collective-permute-start | bytes 196616 | tf_op jit(solution)/shard_map/ppermute | solution.py:39
  3.6 6.8 %collective-permute-start = (f32[2,8,1024]{2,1,0:T(8,128)S(1)}, f32[2,8,1024]{2,1,0:T(8,128)S(1)}, u32[]{:S(2)}, u32[]{:S(2)}) collective-permute-start(f32[2,8,1024]{2,1,0:T(8,128)S(1)} %get-tuple-element.7), channel_id=1, source_target_pairs={{0,1},{1,2},{2,3},{3,4},{4,5},{5,6},{6,7},{8,9},{9,10},{10,11},{11... | collective-permute-start | bytes 196616 | tf_op jit(solution)/shard_map/ppermute | solution.py:38
  12.8 19.8 %all-to-all-start = ((f32[32,30,128]{2,1,0:T(8,128)}), f32[32,30,128]{2,1,0:T(8,128)S(1)}, u32[]{:S(2)}, u32[]{:S(2)}) async-start(f32[32,30,128]{2,1,0:T(8,128)} %reshape.102), calls=%async_computation | async-start | bytes 1048576 | tf_op jit(solution)/shard_map/all_to_all | solution.py:185
  23.3 2.0 %copy-start.3 = (f32[768]{0:T(1024)S(1)}, f32[768]{0:T(1024)}, u32[]{:S(2)}) copy-start(f32[768]{0:T(1024)} %constant.66) | copy-start | bytes 9220
  23.3 2.0 %copy-start.4 = (f32[768]{0:T(1024)S(1)}, f32[768]{0:T(1024)}, u32[]{:S(2)}) copy-start(f32[768]{0:T(1024)} %constant.65) | copy-start | bytes 9220
  23.4 2.0 %copy-start.5 = (f32[768]{0:T(1024)S(1)}, f32[768]{0:T(1024)}, u32[]{:S(2)}) copy-start(f32[768]{0:T(1024)} %constant.63) | copy-start | bytes 9220
  23.4 2.0 %copy-start.6 = (f32[768]{0:T(1024)S(1)}, f32[768]{0:T(1024)}, u32[]{:S(2)}) copy-start(f32[768]{0:T(1024)} %constant.64) | copy-start | bytes 9220
  25.1 7.4 %copy-start.1 = (f32[32,32]{1,0:T(8,128)S(1)}, f32[32,32]{1,0:T(8,128)}, u32[]{:S(2)}) copy-start(f32[32,32]{1,0:T(8,128)} %constant.51.clone) | copy-start | bytes 12292
  43.0 0.9 %copy-start.2 = (f32[32,32]{1,0:T(8,128)S(1)}, f32[32,32]{1,0:T(8,128)}, u32[]{:S(2)}) copy-start(f32[32,32]{1,0:T(8,128)} %constant.57.clone) | copy-start | bytes 12292

commit v17 on v14

--- a/solution.py
+++ b/solution.py
@@ -187,8 +187,7 @@
     solved = solve_slots(spectrum, faces, shifts, inside)
 
     solved = solved.reshape(2, extended, half, width)[:, margin : margin + rows, :, margin : margin + span]
-    solved = solved.transpose(0, 2, 1, 3).reshape(total, rows * span)
-    signal = jnp.dot(inverse, solved, precision=highest)
+    signal = jnp.einsum("tks,krsc->trc", inverse.reshape(total, 2, half), solved, precision=highest)
     signal = signal.reshape(total, -1, lane)
     returned = lax.all_to_all(signal, "tm", 0, 0, tiled=True)
     returned = returned.reshape(tiles, rows, span).transpose(1, 0, 2)

time: 59 us -> 59.3 us (level)
    unnamed x21 -> x20, local copies, waits for them, and re-layouts: 2.21 us -> 2.16 us
where the time goes in v17:
time: 59.3 us; the launch traced here: 58.6 us
  local copies, waits for them, and re-layouts  15.4 us (26%)
  starting transfers between devices  14.8 us (25%)
  blocking collectives  12.4 us (21%)
  waiting for transfers between devices  6.03 us (10%)
  Pallas kernels  6.01 us (10%)
  other arithmetic  1.92 us (3%)
  matrix products  1.68 us (3%)
    all_to_all x1, blocking collectives, body(): returned = lax.all_to_all(signal, 'tm', 0, 0, tiled=True)  12.4 us
    all_to_all x1, starting transfers between devices, body(): lax.all_to_all(sent, 'tm', 0, 0, tiled=True)  8.13 us
    all_to_all x1, waiting for transfers between devices, body(): lax.all_to_all(sent, 'tm', 0, 0, tiled=True)  6.03 us
    pallas_call x1, Pallas kernels, solve_slots(): pl.pallas_call(solve_kernel, out_shape=jax.ShapeDtypeStruct(spectrum.shap...  6.01 us
    ppermute x1, starting transfers between devices, with_halo(): low = lax.ppermute(bottom, 'row', forward)  4.76 us
    unnamed x20, local copies, waits for them, and re-layouts  2.16 us
    another operation x8, local copies, waits for them, and re-layouts, body(): jnp.tile(f, (1, half))  1.98 us
    ppermute x1, starting transfers between devices, with_halo(): high = lax.ppermute(top, 'row', backward)  1.92 us
  transfers between devices with their start and end apart: 3, of which 1 were waited for; matrix products, arithmetic and copies ran while one was open for 13% of the time, Pallas kernels for 0%

profile of v17, /device:TPU:97, one launch (start us, length us, event | category | flops | bytes accessed | tf_op | source)
XLA Modules:
  0.0 58.6 jit_solution(14194741540371259782)
XLA Ops:
  0.0 0.0 copy-start
  0.0 0.8 %slice_bitcast_fusion = (f32[1,8,1024]{2,1,0:T(8,128)S(1)}, f32[1,8,1024]{2,1,0:T(8,128)S(1)}) fusion(f32[64,1024]{1,0:T(8,128)} %param.11), kind=kLoop, calls=%fused_computation.26 | loop fusion | bytes 131072 | tf_op jit(solution)/shard_map/stack | solution.py:36
  0.8 0.8 %fusion.22 = (f32[1,8,1024]{2,1,0:T(8,128)S(1)}, f32[1,8,1024]{2,1,0:T(8,128)S(1)}) fusion(f32[1,64,1024]{2,1,0:T(8,128)} %param.10), kind=kLoop, calls=%fused_computation.57 | loop fusion | bytes 131072 | tf_op jit(solution)/shard_map/slice | solution.py:36
  1.6 1.9 %collective-permute-start.1 = (f32[2,8,1024]{2,1,0:T(8,128)S(1)}, f32[2,8,1024]{2,1,0:T(8,128)S(1)}, u32[]{:S(2)}, u32[]{:S(2)}) collective-permute-start(f32[2,8,1024]{2,1,0:T(8,128)S(1)} %get-tuple-element.8), channel_id=1, source_target_pairs={{1,0},{2,1},{3,2},{4,3},{5,4},{6,5},{7,6},{9,8},{10,9},{11,10},{12... | collective-permute-start | bytes 196616 | tf_op jit(solution)/shard_map/ppermute | solution.py:39
  3.6 4.8 %collective-permute-start = (f32[2,8,1024]{2,1,0:T(8,128)S(1)}, f32[2,8,1024]{2,1,0:T(8,128)S(1)}, u32[]{:S(2)}, u32[]{:S(2)}) collective-permute-start(f32[2,8,1024]{2,1,0:T(8,128)S(1)} %get-tuple-element.7), channel_id=1, source_target_pairs={{0,1},{1,2},{2,3},{3,4},{4,5},{5,6},{6,7},{8,9},{9,10},{10,11},{11... | collective-permute-start | bytes 196616 | tf_op jit(solution)/shard_map/ppermute | solution.py:38
  8.3 0.1 iota_compare_fusion.2
  8.4 0.1 broadcast_and_fusion
  8.5 1.1 %copy.68 = f32[1,64,1024]{1,2,0:T(8,128)S(1)} copy(f32[1,64,1024]{2,1,0:T(8,128)} %param.10) | data formatting | bytes 524288 | tf_op args[0]
  9.7 0.0 copy-done
  9.7 0.2 copy.74
  9.9 0.2 copy.77
  10.1 0.0 collective-permute-done.1
  10.1 0.2 copy.92
  10.3 0.0 collective-permute-done
  10.4 0.2 copy.91
  10.6 0.3 select_maximum_fusion
  10.9 0.1 fusion.21
  11.0 0.1 maximum_bitcast_fusion
  11.1 0.4 copy.70
  11.5 1.3 %reshape.99 = f32[32,30,128]{2,1,0:T(8,128)} reshape(f32[32,80,48]{2,1,0:T(8,128)S(1)} %copy.70) | data formatting | bytes 983040 | tf_op jit(solution)/shard_map/reshape | solution.py:175
  12.8 8.1 %all-to-all-start = ((f32[32,30,128]{2,1,0:T(8,128)}), f32[32,30,128]{2,1,0:T(8,128)S(1)}, u32[]{:S(2)}, u32[]{:S(2)}) async-start(f32[32,30,128]{2,1,0:T(8,128)} %reshape.99), calls=%async_computation | async-start | bytes 1048576 | tf_op jit(solution)/shard_map/all_to_all | solution.py:176
  20.9 0.2 copy.94
  21.1 0.2 copy.93
  21.3 0.1 select_maximum_fusion.2
  21.4 0.1 broadcast_add_fusion.2
  21.6 0.8 %copy.81.north_ref = f32[80,768]{1,0:T(8,128)} copy(f32[80,768]{0,1:T(8,128)S(1)} %bitcast.46) | data formatting | bytes 491520 | tf_op jit(solution)/shard_map/tile | solution.py:185
  22.4 0.9 %copy.82.south_ref = f32[80,768]{1,0:T(8,128)} copy(f32[80,768]{0,1:T(8,128)S(1)} %bitcast.47) | data formatting | bytes 491520 | tf_op jit(solution)/shard_map/add | solution.py:152
  23.3 0.0 copy-start.3
  23.3 0.0 copy-start.4
  23.4 0.0 copy-start.5
  23.4 0.0 copy-start.6
  23.4 0.8 %copy.83.east_ref = f32[80,768]{1,0:T(8,128)} copy(f32[80,768]{0,1:T(8,128)S(1)} %bitcast.48) | data formatting | bytes 491520 | tf_op jit(solution)/shard_map/tile | solution.py:185
  24.3 0.9 %copy.84.west_ref = f32[80,768]{1,0:T(8,128)} copy(f32[80,768]{0,1:T(8,128)S(1)} %bitcast.49) | data formatting | bytes 491520 | tf_op jit(solution)/shard_map/add | solution.py:152
  25.1 0.0 copy-start.2
  25.2 0.1 copy.75
  25.3 0.0 copy-done.3
  25.3 0.0 copy-done.4
  25.3 0.0 copy-done.5
  25.3 0.0 copy-done.6
  25.3 1.1 %divide_select_fusion = (f32[80,768]{1,0:T(8,128)}, f32[80,768]{1,0:T(8,128)}, f32[80,768]{1,0:T(8,128)}, f32[80,768]{1,0:T(8,128)}, f32[80,768]{1,0:T(8,128)}) fusion(pred[80,768]{1,0:T(8,128)(4,1)S(1)} %copy.77, f32[768]{0:T(1024)S(1)} %copy-done.3, f32[768]{0:T(1024)S(1)} %copy-done.4, f32[80,768]{1,0:T(8,128)S(1)} %copy.75, f32[768]{0:T(1024)S(1)} %copy-done.5, ...), kind=kLoop, calls=%fused_computation.16 | loop fusion | flops 737280 | bytes 1548288 | tf_op jit(solution)/shard_map/jit(_where)/select_n | solution.py:151
  26.5 6.0 %all-to-all-done = f32[32,30,128]{2,1,0:T(8,128)S(1)} async-done(((f32[32,30,128]{2,1,0:T(8,128)}), f32[32,30,128]{2,1,0:T(8,128)S(1)}, u32[]{:S(2)}, u32[]{:S(2)}) %all-to-all-start) | async-done | bytes 491552 | tf_op jit(solution)/shard_map/all_to_all | solution.py:176
  32.5 0.0 copy-done.2
  32.5 0.8 %fusion.2 = f32[32,3840]{1,0:T(8,128)S(1)} fusion(f32[32,32]{1,0:T(8,128)S(1)} %copy-done.2, f32[4,8,30,128]{3,2,1,0:T(8,128)S(1)} %bitcast.45), kind=kOutput, calls=%fused_computation.13 | convolution fusion | flops 47185920 | bytes 987136 | tf_op jit(solution)/shard_map/dot_general | solution.py:177
  33.3 0.8 %reshape.101 = f32[2,16,80,48]{3,2,1,0:T(8,128)S(1)} reshape(f32[32,3840]{1,0:T(8,128)S(1)} %fusion.2) | data formatting | bytes 983040 | tf_op jit(solution)/shard_map/reshape | solution.py:178
  34.2 0.4 copy.71
  34.5 1.1 %copy.80.spec_ref = f32[2,80,768]{2,1,0:T(8,128)} copy(f32[2,80,768]{1,2,0:T(8,128)S(1)} %bitcast.36) | data formatting | bytes 983040 | tf_op jit(solution)/shard_map/reshape | solution.py:179
  35.6 6.0 %shard_map.100 = f32[2,80,768]{2,1,0:T(8,128)} custom-call(f32[2,80,768]{2,1,0:T(8,128)} %copy.80.spec_ref, f32[80,768]{1,0:T(8,128)} %copy.81.north_ref, f32[80,768]{1,0:T(8,128)} %copy.82.south_ref, f32[80,768]{1,0:T(8,128)} %copy.83.east_ref, f32[80,768]{1,0:T(8,128)} %copy.84.west_ref, f32[80,768]{1,0:T(8,128)} %get-tuple-element.22.diag_a_ref, ...), custom_call_target="tpu_custom_call" | custom-call | tf_op jit(solution)/shard_map/pallas_call | solution.py:154
  41.6 0.0 copy-start.1
  41.6 1.3 %copy.85 = f32[2,80,768]{1,2,0:T(8,128)S(1)} copy(f32[2,80,768]{2,1,0:T(8,128)} %shard_map.100) | data formatting | bytes 983040 | tf_op jit(solution)/shard_map/pallas_call | solution.py:154
  42.9 0.2 slice.80
  43.1 0.0 copy-done.1
  43.1 0.9 %convolution_bitcast_fusion = f32[32,64,32]{1,0,2:T(8,128)S(1)} fusion(f32[32,2,16,1]{0,2,1,3:T(8,128)S(1)} %copy-done.1, f32[2,64,16,32]{1,3,2,0:T(8,128)S(1)} %slice.80), kind=kOutput, calls=%fused_computation | convolution fusion | flops 25165824 | bytes 528384 | tf_op jit(solution)/shard_map/tks,krsc->trc/dot_general | solution.py:190
  44.0 0.4 copy.87
  44.4 0.3 reshape.104
  44.7 12.4 %all_to_all.10 = f32[32,16,128]{2,1,0:T(8,128)S(1)} all-to-all(f32[32,16,128]{2,1,0:T(8,128)S(1)} %reshape.104), channel_id=1, replica_groups=mesh['tm'=32,'row'=8] {'tm'}, dimensions={0} | all-to-all | bytes 524288 | tf_op jit(solution)/shard_map/all_to_all | solution.py:192
  57.1 0.3 reshape.105
  57.4 0.3 copy.88
  57.7 0.9 %copy.89 = f32[1,64,1024]{2,1,0:T(8,128)} copy(f32[1,64,1024]{1,2,0:T(8,128)S(1)} %bitcast.38) | data formatting | bytes 524288 | tf_op jit(solution)/shard_map/reshape | solution.py:194
  (12 shorter events, 0.2 us)
Async XLA Ops:
  0.0 9.7 %copy-start = (f32[64,1024]{1,0:T(8,128)S(1)}, f32[64,1024]{1,0:T(8,128)}, u32[]{:S(2)}) copy-start(f32[64,1024]{1,0:T(8,128)} %param.11) | copy-start | bytes 786436
  1.6 8.5 %collective-permute-start.1 = (f32[2,8,1024]{2,1,0:T(8,128)S(1)}, f32[2,8,1024]{2,1,0:T(8,128)S(1)}, u32[]{:S(2)}, u32[]{:S(2)}) collective-permute-start(f32[2,8,1024]{2,1,0:T(8,128)S(1)} %get-tuple-element.8), channel_id=1, source_target_pairs={{1,0},{2,1},{3,2},{4,3},{5,4},{6,5},{7,6},{9,8},{10,9},{11,10},{12... | collective-permute-start | bytes 196616 | tf_op jit(solution)/shard_map/ppermute | solution.py:39
  3.6 6.8 %collective-permute-start = (f32[2,8,1024]{2,1,0:T(8,128)S(1)}, f32[2,8,1024]{2,1,0:T(8,128)S(1)}, u32[]{:S(2)}, u32[]{:S(2)}) collective-permute-start(f32[2,8,1024]{2,1,0:T(8,128)S(1)} %get-tuple-element.7), channel_id=1, source_target_pairs={{0,1},{1,2},{2,3},{3,4},{4,5},{5,6},{6,7},{8,9},{9,10},{10,11},{11... | collective-permute-start | bytes 196616 | tf_op jit(solution)/shard_map/ppermute | solution.py:38
  12.8 19.8 %all-to-all-start = ((f32[32,30,128]{2,1,0:T(8,128)}), f32[32,30,128]{2,1,0:T(8,128)S(1)}, u32[]{:S(2)}, u32[]{:S(2)}) async-start(f32[32,30,128]{2,1,0:T(8,128)} %reshape.99), calls=%async_computation | async-start | bytes 1048576 | tf_op jit(solution)/shard_map/all_to_all | solution.py:176
  23.3 2.0 %copy-start.3 = (f32[768]{0:T(1024)S(1)}, f32[768]{0:T(1024)}, u32[]{:S(2)}) copy-start(f32[768]{0:T(1024)} %constant.66) | copy-start | bytes 9220
  23.3 2.0 %copy-start.4 = (f32[768]{0:T(1024)S(1)}, f32[768]{0:T(1024)}, u32[]{:S(2)}) copy-start(f32[768]{0:T(1024)} %constant.65) | copy-start | bytes 9220
  23.4 2.0 %copy-start.5 = (f32[768]{0:T(1024)S(1)}, f32[768]{0:T(1024)}, u32[]{:S(2)}) copy-start(f32[768]{0:T(1024)} %constant.63) | copy-start | bytes 9220
  23.4 2.0 %copy-start.6 = (f32[768]{0:T(1024)S(1)}, f32[768]{0:T(1024)}, u32[]{:S(2)}) copy-start(f32[768]{0:T(1024)} %constant.64) | copy-start | bytes 9220
  25.1 7.4 %copy-start.2 = (f32[32,32]{1,0:T(8,128)S(1)}, f32[32,32]{1,0:T(8,128)}, u32[]{:S(2)}) copy-start(f32[32,32]{1,0:T(8,128)} %constant.51.clone) | copy-start | bytes 12292
  41.6 1.5 %copy-start.1 = (f32[32,2,16,1]{0,2,1,3:T(8,128)S(1)}, f32[32,2,16,1]{0,2,1,3:T(8,128)}, u32[]{:S(2)}) copy-start(f32[32,2,16,1]{0,2,1,3:T(8,128)} %constant.67) | copy-start | bytes 12292
